TPU v7x, 256 devices: a whole 4x4x8 slice. The times are simulated.
256 devices in a mesh: req: 32 (over z_hi, x, y), cand: 8 (over z_lo, core).
Axes of the slice: x: 4, y: 4, z: 8 (z_hi: 2, z_lo: 4; z = z_hi * 4 + z_lo), core: 2. Of those that a mesh axis runs over, the one named last changes fastest.
Arguments:
- item_table: bfloat16 [32, 8, 256, 1024], P('req', 'cand'), may hold values from -25 to 25
- picked_items: int32 [32, 8, 1024], P('req', 'cand'), may hold values from 0 to 255
- destination: int32 [32, 8, 1024], P('req', 'cand'), may hold values from 0 to 31, as said below
- slot_index: int32 [32, 8, 1024], P('req', 'cand'), may hold values from 0 to 1023, as said below
- history_cache: bfloat16 [32, 8, 128, 2048], P('req', 'cand'), may hold values from -6 to 6
- history_length: int32 [32, 8], P('req'), may hold values from 16 to 128
- input_weight: bfloat16 [1024, 4096], replicated, may hold values from -0.1875 to 0.1875
- output_weight: bfloat16 [1024, 1024], replicated, may hold values from -0.1875 to 0.1875
Outputs:
- cand_out: bfloat16 [32, 8, 1024, 1024], P('req', 'cand')
Inputs may be any that keep to these rules, and one draw needn't show every extreme that they name: Each device sends exactly 1024 rows, and within each index of cand every device receives exactly 1024; no device sends more than 64 rows to one destination, and within each index of cand some device sends exactly 64 to one destination. `slot_index`: the rows that reach one device fill each of its 1024 slots exactly once.
All inputs are finite; a program needn't handle non-finite values.
Results may differ from a plain program's by a relative error of at most 0.005.
Values may be sent and summed in bfloat16 or wider, within the bound.
No kernel may reach another device: no remote copies, remote signals or barrier semaphores. Data moves between devices by JAX's collectives and lax.ppermute only.
A program may use at most 128 MiB of HBM per device.

v0:
```python
import math

import jax
import jax.numpy as jnp
from jax import lax
from jax.sharding import PartitionSpec as P

HEADS = 8


epsilon = 1e-06


def layer_norm(values):
    average = jnp.mean(values, axis=-1, keepdims=True)
    centred = values - average
    variance = jnp.mean(centred * centred, axis=-1, keepdims=True)
    return centred * lax.rsqrt(variance + epsilon)


def attend(queries, cache_rows, lengths, head_count, score_scale):
    count_req, history_span, doubled = cache_rows.shape
    feature = doubled // 2
    head_width = feature // head_count
    keys = cache_rows[:, :, :feature].reshape(count_req, history_span, head_count, head_width)
    values = cache_rows[:, :, feature:].reshape(count_req, history_span, head_count, head_width)
    scores = (
        jnp.einsum("bihe,bjhe->bhij", queries, keys, preferred_element_type=jnp.float32)
        * score_scale
    )
    positions = jnp.arange(history_span, dtype=jnp.int32)
    valid = (positions[None, :] < lengths[:, None]).astype(jnp.float32)
    length_plus = lengths.astype(jnp.float32) + 1.0
    weights = (
        jax.nn.silu(scores) / length_plus[:, None, None, None] * valid[:, None, None, :]
    ).astype(jnp.bfloat16)
    return jnp.einsum("bhij,bjhe->bihe", weights, values, preferred_element_type=jnp.float32)


def shards(
    item_table,
    picked_items,
    destination,
    slot_index,
    history_cache,
    history_length,
    input_weight,
    output_weight,
):
    sources = lax.axis_size("req")
    item_rows = item_table[0, 0]
    pick_list = picked_items[0, 0]
    targets = destination[0, 0]
    places = slot_index[0, 0]
    slot_count = pick_list.shape[0]
    feature = item_rows.shape[1]
    capacity = 2 * slot_count // sources
    picked = jnp.take(item_rows, pick_list, axis=0)
    one_hot = (targets[:, None] == jnp.arange(sources, dtype=jnp.int32)[None, :]).astype(jnp.int32)
    earlier = jnp.cumsum(one_hot, axis=0) - one_hot
    within = jnp.sum(earlier * one_hot, axis=1)
    outgoing = jnp.zeros((sources, capacity, feature), jnp.bfloat16).at[targets, within].set(picked)
    slot_tags = jnp.full((sources, capacity), slot_count, jnp.int32).at[targets, within].set(places)
    arrived, arrived_tags = (
        lax.all_to_all(outgoing, "req", split_axis=0, concat_axis=0, tiled=True),
        lax.all_to_all(slot_tags, "req", split_axis=0, concat_axis=0, tiled=True),
    )
    arranged = (
        jnp.zeros((slot_count, feature), jnp.bfloat16)
        .at[arrived_tags.reshape(-1)]
        .set(arrived.reshape(-1, feature), mode="drop")
    )
    lengths = history_length[0]
    members = lengths.shape[0]
    per_request = slot_count // members
    head_count = HEADS
    head_width = feature // head_count
    score_scale = 1.0 / math.sqrt(head_width)
    as_float = arranged.astype(jnp.float32)
    normed_in = layer_norm(as_float).astype(jnp.bfloat16)
    projected = jax.nn.silu(
        jnp.dot(normed_in, input_weight, preferred_element_type=jnp.float32)
    ).astype(jnp.bfloat16)
    quarters = projected.reshape(members, per_request, 4, head_count, head_width)
    gate_u = projected[:, :feature]
    own_values = quarters[:, :, 1]
    queries = quarters[:, :, 2]
    own_keys = quarters[:, :, 3]
    length_plus = lengths.astype(jnp.float32) + 1.0
    own_scores = (
        jnp.einsum("bihe,bihe->bih", queries, own_keys, preferred_element_type=jnp.float32)
        * score_scale
    )
    own_weight = jax.nn.silu(own_scores) / length_plus[:, None, None]
    own_term = own_weight[..., None] * own_values.astype(jnp.float32)
    found = attend(
        queries,
        lax.all_gather(history_cache, "cand", axis=1, tiled=True)[0],
        lengths,
        head_count,
        score_scale,
    )
    attended = (found + own_term).reshape(slot_count, feature)
    normed_out = layer_norm(attended)
    gated = (normed_out * gate_u.astype(jnp.float32)).astype(jnp.bfloat16)
    mixed = as_float + jnp.dot(gated, output_weight, preferred_element_type=jnp.float32)
    return mixed.astype(jnp.bfloat16)[None, None]


def solution(mesh):
    in_specs = (
        P("req", "cand", None, None),
        P("req", "cand", None),
        P("req", "cand", None),
        P("req", "cand", None),
        P("req", "cand", None, None),
        P("req", None),
        P(),
        P(),
    )
    out_specs = P("req", "cand", None, None)
    return jax.shard_map(shards, mesh=mesh, in_specs=in_specs, out_specs=out_specs, check_vma=False)
```

profile of v0, /device:TPU:130, one launch (start us, length us, event | category | flops | bytes accessed | tf_op | source)
XLA Modules:
  0.0 297.7 jit_solution(13897950519749897282)
XLA Ops:
  6.5 0.8 fusion.34
  7.4 9.0 %reduce-window.6 = s32[32,8,128]{2,1,0:T(8,128)S(1)} reduce-window(s32[32,8,128]{2,1,0:T(8,128)S(1)} %fusion.34, s32[]{:T(128)} %constant.18.clone.1), window={size=1x1x128 pad=0_0x0_0x127_0}, to_apply=%region_0.1 | reduce-window | flops 4161536 | bytes 262148 | tf_op jit(solution)/shard_map/reduce-window
  18.3 0.8 and_reduce_fusion
  19.0 0.7 multiply_reduce_fusion.2
  19.8 4.5 %scatter_custom_fusion.1 = s32[2048]{0:T(1024)S(1)} fusion(s32[1024]{0:T(1024)S(1)} %broadcast_select_fusion, s32[1024]{0:T(1024)} %bitcast.101, s32[]{:T(128)} %constant.17.clone.1), kind=kCustom, calls=%fused_computation.57 | custom fusion | bytes 8704
  25.0 12.4 %all-to-all-start = ((s32[32,1,64]{2,1,0:T(1,128)}), s32[32,1,64]{2,1,0:T(1,128)S(1)}, u32[]{:S(2)}, u32[]{:S(2)}) async-start(s32[32,1,64]{2,1,0:T(1,128)} %all_to_all.9), calls=%async_computation | async-start | bytes 32768 | tf_op jit(solution)/shard_map/all_to_all | solution.py:66
  38.8 17.1 %scatter_custom_fusion.2 = bf16[2048,1024]{1,0:T(8,128)(2,1)} fusion(s32[1024]{0:T(1024)S(1)} %broadcast_select_fusion, bf16[]{:T(256)} %constant.16.clone.1, pred[1024]{0:T(1024)(128)(4,1)S(1)} %compare_and_fusion, bf16[]{:T(256)} %constant.31.clone.1, bf16[256,1024]{1,0:T(8,128)(2,1)} %bitcast.90, s32[1024]{0:T(1024)S(1)} %broadcast_clamp_fusion), kind=kCustom, calls=%fused_computation.28 | custom fusion | flops 1048576 | bytes 4723716
  55.9 12.4 %all-to-all-start.1 = ((bf16[32,64,1024]{2,1,0:T(8,128)(2,1)}), bf16[32,64,1024]{2,1,0:T(8,128)(2,1)}, u32[]{:S(2)}, u32[]{:S(2)}) async-start(bf16[32,64,1024]{2,1,0:T(8,128)(2,1)} %bitcast.84), calls=%async_computation.1 | async-start | bytes 8388608 | tf_op jit(solution)/shard_map/all_to_all | solution.py:65
  70.5 129.4 %all-gather.2.cloned.1.call-done = bf16[1,8,128,2048]{3,2,0,1:T(8,128)(2,1)} async-done(((bf16[1,1,128,2048]{3,2,0,1:T(8,128)(2,1)}), bf16[1,8,128,2048]{3,2,0,1:T(8,128)(2,1)}) %all-gather.2.cloned.1.call-update) | async-done | bytes 4194320 | tf_op jit(solution)/shard_map/all_gather | solution.py:98
  199.8 6.5 %copy.24 = bf16[1,8,128,2048]{2,3,1,0:T(8,128)(2,1)} copy(bf16[1,8,128,2048]{3,2,0,1:T(8,128)(2,1)} %all-gather.2.cloned.1.call-done) | data formatting | bytes 8388608 | tf_op jit(solution)/shard_map/all_gather | solution.py:98
  206.3 4.6 %fusion.43 = (bf16[8,128,1024]{1,2,0:T(8,128)(2,1)}, bf16[8,128,1024]{1,2,0:T(8,128)(2,1)}) fusion(bf16[8,128,2048]{1,2,0:T(8,128)(2,1)} %bitcast.85), kind=kLoop, calls=%fused_computation.74 | loop fusion | bytes 8388608 | tf_op jit(solution)/shard_map/slice | solution.py:25
  210.9 11.9 %scatter_custom_fusion = bf16[1024,1024]{1,0:T(8,128)(2,1)} fusion(s32[2048]{0:T(1024)S(1)} %bitcast.99, bf16[2048,1024]{1,0:T(8,128)(2,1)} %bitcast.13, bf16[]{:T(256)} %constant.16.clone.1), kind=kCustom, calls=%fused_computation.38 | custom fusion | bytes 2097664 | tf_op jit(solution)/shard_map/scatter | solution.py:71
  222.8 2.1 convert_reduce_fusion
  224.9 2.3 fusion.2
  227.2 15.6 %multiply_convert_fusion = bf16[1024,4096]{1,0:T(8,128)(2,1)} fusion(bf16[1024,4096]{1,0:T(8,128)(2,1)} %param.14, bf16[1024,1024]{1,0:T(8,128)(2,1)S(1)} %copy-done.1, f32[1024]{0:T(1024)S(1)} %add_rsqrt_fusion, f32[1024]{0:T(1024)S(1)} %broadcast_multiply_fusion.1), kind=kOutput, calls=%fused_computation.4 | convolution fusion | flops 8615100416 | bytes 18882560 | tf_op jit(solution)/shard_map/dot_general | solution.py:82
  242.8 9.4 %copy.37 = bf16[128,8,32,128]{3,2,1,0:T(8,128)(2,1)} copy(bf16[128,8,32,128]{3,1,2,0:T(8,128)(2,1)} %bitcast.86) | data formatting | bytes 16777216
  252.2 4.8 %fusion.42 = (bf16[8,128,1,8,128]{4,3,2,1,0:T(8,128)(2,1)}, bf16[8,128,1,8,128]{4,3,2,1,0:T(8,128)(2,1)}) fusion(bf16[8,128,4,8,128]{4,3,2,1,0:T(8,128)(2,1)} %bitcast.82), kind=kLoop, calls=%fused_computation.73 | loop fusion | bytes 8388608 | tf_op jit(solution)/shard_map/slice | solution.py:87
  257.0 4.1 %copy.35 = bf16[8,128,1,8,128]{1,4,3,0,2:T(8,128)(2,1)} copy(bf16[8,128,1,8,128]{4,3,2,1,0:T(8,128)(2,1)} %get-tuple-element.6) | data formatting | bytes 4194304
  261.1 2.1 fusion.25
  263.3 4.2 %multiply_reduce_fusion = f32[8,128,8]{2,1,0:T(8,128)S(1)} fusion(f32[8,128,8,128]{3,1,2,0:T(8,128)S(1)} %fusion.25, bf16[8,128,4,8,128]{4,3,2,1,0:T(8,128)(2,1)} %bitcast.83), kind=kLoop, calls=%fused_computation.19 | loop fusion | flops 3137536 | bytes 6324224
  267.7 8.2 %fusion.44 = (f32[8,128]{1,0:T(8,128)S(1)}, f32[8,128,8,128]{1,3,2,0:T(8,128)}) fusion(bf16[8,128,1,8,128]{1,4,3,0,2:T(8,128)(2,1)} %copy.35, f32[8,128,8]{1,2,0:T(8,128)S(1)} %multiply_divide_fusion, bf16[8,128,8,128]{1,3,2,0:T(8,128)(2,1)} %bitcast.89, bf16[8,128,8,128]{1,3,2,0:T(8,128)(2,1)} %bitcast.88, f32[8,128]{1,0:T(8,128)S(1)} %fusion.37, ...), kind=kOutput, calls=%fused_computation.75 | convolution fusion | flops 549452800 | bytes 12623904 | tf_op jit(solution)/shard_map/bhij,bjhe->bihe/dot_general | solution.py:37
  276.0 5.4 %copy.27 = f32[8,128,8,128]{3,2,1,0:T(8,128)} copy(f32[8,128,8,128]{1,3,2,0:T(8,128)} %get-tuple-element.12) | data formatting | bytes 8388608 | tf_op jit(solution)/shard_map/add | solution.py:103
  281.3 2.8 multiply_reduce_fusion.1
  284.2 6.7 %fusion.11 = bf16[1,1,1024,1024]{3,2,1,0:T(8,128)(2,1)} fusion(bf16[1024,1024]{1,0:T(8,128)(2,1)S(1)} %copy-done.2, bf16[1024,1024]{1,0:T(8,128)(2,1)S(1)} %copy-done, f32[128,8,8,128]{3,2,1,0:T(8,128)} %bitcast.87, bf16[1024,4096]{1,0:T(8,128)(2,1)} %multiply_convert_fusion, f32[1024]{0:T(1024)S(1)} %rsqrt_bitcast_fusion, f32[1024]{0:T(1024)S(1)} %get-tuple-element.9), kind=kOutput, calls=%fused_computation.23 | convolution fusion | flops 2155872256 | bytes 12591104 | tf_op jit(solution)/shard_map/dot_general | solution.py:106
  (37 shorter events, 6.3 us)
Async XLA Ops:
  6.5 277.6 %copy-start = (bf16[1024,1024]{1,0:T(8,128)(2,1)S(1)}, bf16[1024,1024]{1,0:T(8,128)(2,1)}, u32[]{:S(2)}) copy-start(bf16[1024,1024]{1,0:T(8,128)(2,1)} %param.15) | copy-start | bytes 6291460
  25.0 31.0 %all-to-all-start = ((s32[32,1,64]{2,1,0:T(1,128)}), s32[32,1,64]{2,1,0:T(1,128)S(1)}, u32[]{:S(2)}, u32[]{:S(2)}) async-start(s32[32,1,64]{2,1,0:T(1,128)} %all_to_all.9), calls=%async_computation | async-start | bytes 32768 | tf_op jit(solution)/shard_map/all_to_all | solution.py:66
  55.9 13.2 %copy-start.3 = (s32[1,8]{1,0:T(1,128)S(1)}, s32[1,8]{1,0:T(1,128)}, u32[]{:S(2)}) copy-start(s32[1,8]{1,0:T(1,128)} %param.13) | copy-start | bytes 100
  55.9 154.9 %all-to-all-start.1 = ((bf16[32,64,1024]{2,1,0:T(8,128)(2,1)}), bf16[32,64,1024]{2,1,0:T(8,128)(2,1)}, u32[]{:S(2)}, u32[]{:S(2)}) async-start(bf16[32,64,1024]{2,1,0:T(8,128)(2,1)} %bitcast.84), calls=%async_computation.1 | async-start | bytes 8388608 | tf_op jit(solution)/shard_map/all_to_all | solution.py:65
  68.3 131.5 %all-gather.2.cloned.1.call-start = ((), (), s32[]{:S(2)}) async-start(), calls=%async_computation.2 | async-start | bytes 4718592 | tf_op jit(solution)/shard_map/all_gather | solution.py:98
  222.8 4.4 %copy-start.1 = (bf16[1024,1024]{1,0:T(8,128)(2,1)S(1)}, bf16[1024,1024]{1,0:T(8,128)(2,1)}, u32[]{:S(2)}) copy-start(bf16[1024,1024]{1,0:T(8,128)(2,1)} %scatter_custom_fusion) | copy-start | bytes 6291460
  281.3 2.9 copy-start.2
Sparse Core Ops, SparseCore 0:
  70.9 128.8 all-gather.1
where the time goes:
time: 299 us; the launch traced here: 298 us
  waiting for transfers between devices  130 us (43%)
  local copies, waits for them, and re-layouts  52.9 us (18%)
  other arithmetic  45.8 us (15%)
  matrix products  30.5 us (10%)
  starting transfers between devices  25.1 us (8%)
  between operations  13.6 us (5%)
    all_gather x1, waiting for transfers between devices, shards(): lax.all_gather(history_cache, 'cand', axis=1, tiled=True)[0]  129 us
    unnamed x6, other arithmetic  24.9 us
    unnamed x11, local copies, waits for them, and re-layouts  18.1 us
    dot_general x1, matrix products, shards(): jnp.dot(normed_in, input_weight, preferred_element_type=jnp.float32)  15.6 us
    all_to_all x1, starting transfers between devices, shards(): lax.all_to_all(slot_tags, 'req', split_axis=0, concat_axis=0, tiled=True)  12.4 us
    all_to_all x1, starting transfers between devices, shards(): lax.all_to_all(outgoing, 'req', split_axis=0, concat_axis=0, tiled=True)  12.4 us
    scatter x1, local copies, waits for them, and re-layouts, shards(): arranged = jnp.zeros((slot_count, feature), jnp.bfloat16).at[arrived_tags...  11.9 us
    another operation x3, other arithmetic  9.15 us
  transfers between devices with their start and end apart: 3, of which 1 were waited for; matrix products, arithmetic and copies ran while one was open for 10% of the time, Pallas kernels for 0%

commit v1 on v0

--- a/solution.py
+++ b/solution.py
@@ -3,9 +3,11 @@
 import jax
 import jax.numpy as jnp
 from jax import lax
+from jax.sharding import Mesh
 from jax.sharding import PartitionSpec as P
 
 HEADS = 8
+HALVES = 2
 
 
 epsilon = 1e-06
@@ -37,6 +39,27 @@
     return jnp.einsum("bhij,bjhe->bihe", weights, values, preferred_element_type=jnp.float32)
 
 
+def ranks(targets, sources):
+    count = targets.shape[0]
+    one_hot = (targets[:, None] == jnp.arange(sources, dtype=jnp.int32)[None, :])
+    rows = jnp.arange(count, dtype=jnp.int32)
+    lower = (rows[None, :] < rows[:, None]).astype(jnp.bfloat16)
+    earlier = jnp.dot(lower, one_hot.astype(jnp.bfloat16), preferred_element_type=jnp.float32)
+    return jnp.sum(jnp.where(one_hot, earlier, 0.0), axis=1).astype(jnp.int32)
+
+
+def block_plan(ints, half, n_half, per_pair, sources):
+    picks, targets, places = ints[0], ints[1], ints[2]
+    within = ranks(targets, sources)
+    keep = (targets // n_half) == half
+    position = jnp.where(keep, (targets % n_half) * per_pair + within, -1)
+    spots = jnp.arange(n_half * per_pair, dtype=jnp.int32)
+    hit = position[None, :] == spots[:, None]
+    row = jnp.sum(jnp.where(hit, picks[None, :], 0), axis=1)
+    slot = jnp.sum(jnp.where(hit, places[None, :] + 1, 0), axis=1) - 1
+    return row.reshape(n_half, per_pair), slot.reshape(n_half, per_pair)
+
+
 def shards(
     item_table,
     picked_items,
@@ -47,29 +70,44 @@
     input_weight,
     output_weight,
 ):
-    sources = lax.axis_size("req")
+    n_half = lax.axis_size("xy")
+    sources = HALVES * n_half
+    half = lax.axis_index("zh")
     item_rows = item_table[0, 0]
-    pick_list = picked_items[0, 0]
-    targets = destination[0, 0]
-    places = slot_index[0, 0]
-    slot_count = pick_list.shape[0]
+    ints = jnp.stack([picked_items[0, 0], destination[0, 0], slot_index[0, 0]])
+    slot_count = ints.shape[1]
     feature = item_rows.shape[1]
-    capacity = 2 * slot_count // sources
-    picked = jnp.take(item_rows, pick_list, axis=0)
-    one_hot = (targets[:, None] == jnp.arange(sources, dtype=jnp.int32)[None, :]).astype(jnp.int32)
-    earlier = jnp.cumsum(one_hot, axis=0) - one_hot
-    within = jnp.sum(earlier * one_hot, axis=1)
-    outgoing = jnp.zeros((sources, capacity, feature), jnp.bfloat16).at[targets, within].set(picked)
-    slot_tags = jnp.full((sources, capacity), slot_count, jnp.int32).at[targets, within].set(places)
-    arrived, arrived_tags = (
-        lax.all_to_all(outgoing, "req", split_axis=0, concat_axis=0, tiled=True),
-        lax.all_to_all(slot_tags, "req", split_axis=0, concat_axis=0, tiled=True),
+    per_pair = 2 * slot_count // sources
+    swap = [(0, 1), (1, 0)]
+    other_rows = lax.ppermute(item_rows, "zh", swap)
+    other_ints = lax.ppermute(ints, "zh", swap)
+
+    own_row, own_slot = block_plan(ints, half, n_half, per_pair, sources)
+    far_row, far_slot = block_plan(other_ints, half, n_half, per_pair, sources)
+    own_data = jnp.take(item_rows, own_row.reshape(-1), axis=0).reshape(n_half, per_pair, feature)
+    far_data = jnp.take(other_rows, far_row.reshape(-1), axis=0).reshape(n_half, per_pair, feature)
+    slots = jnp.concatenate([own_slot, far_slot], axis=1)
+    capacity = 2 * per_pair
+    radix = 32
+    high = jnp.floor_divide(slots, radix)
+    low = slots - high * radix
+    tag_row = jnp.zeros((n_half, 8, feature), jnp.float32)
+    tag_row = tag_row.at[:, 0, :capacity].set(high.astype(jnp.float32))
+    tag_row = tag_row.at[:, 0, capacity : 2 * capacity].set(low.astype(jnp.float32))
+    outgoing = jnp.concatenate(
+        [own_data, far_data, tag_row.astype(jnp.bfloat16)], axis=1
     )
-    arranged = (
-        jnp.zeros((slot_count, feature), jnp.bfloat16)
-        .at[arrived_tags.reshape(-1)]
-        .set(arrived.reshape(-1, feature), mode="drop")
-    )
+    arrived = lax.all_to_all(outgoing, "xy", split_axis=0, concat_axis=0, tiled=True)
+    arrived_rows = arrived[:, :capacity].reshape(n_half * capacity, feature)
+    tags = (
+        arrived[:, capacity, :capacity].astype(jnp.int32) * radix
+        + arrived[:, capacity, capacity : 2 * capacity].astype(jnp.int32)
+    ).reshape(-1)
+    slot_ids = jnp.arange(slot_count, dtype=jnp.int32)
+    order = jnp.arange(n_half * capacity, dtype=jnp.int32)
+    fill = jnp.sum(jnp.where(tags[None, :] == slot_ids[:, None], order[None, :], 0), axis=1)
+    arranged = jnp.take(arrived_rows, fill, axis=0)
+
     lengths = history_length[0]
     members = lengths.shape[0]
     per_request = slot_count // members
@@ -108,15 +146,19 @@
 
 
 def solution(mesh):
+    n_req, n_cand = mesh.devices.shape
+    devices = mesh.devices.reshape(HALVES, n_req // HALVES, n_cand)
+    split = Mesh(devices, ("zh", "xy", "cand"))
+    req = ("zh", "xy")
     in_specs = (
-        P("req", "cand", None, None),
-        P("req", "cand", None),
-        P("req", "cand", None),
-        P("req", "cand", None),
-        P("req", "cand", None, None),
-        P("req", None),
+        P(req, "cand", None, None),
+        P(req, "cand", None),
+        P(req, "cand", None),
+        P(req, "cand", None),
+        P(req, "cand", None, None),
+        P(req, None),
         P(),
         P(),
     )
-    out_specs = P("req", "cand", None, None)
-    return jax.shard_map(shards, mesh=mesh, in_specs=in_specs, out_specs=out_specs, check_vma=False)
+    out_specs = P(req, "cand", None, None)
+    return jax.shard_map(shards, mesh=split, in_specs=in_specs, out_specs=out_specs, check_vma=False)

time: 299 us -> 225 us (0.75)
  the two profiles are of different devices: /device:TPU:130 before, /device:TPU:220 now
where the time goes in v1:
time: 225 us; the launch traced here: 224 us
  waiting for transfers between devices  71.3 us (32%)
  local copies, waits for them, and re-layouts  61.9 us (28%)
  matrix products  32.6 us (14%)
  other arithmetic  31.7 us (14%)
  between operations  13.6 us (6%)
  starting transfers between devices  13.3 us (6%)
    all_to_all x1, waiting for transfers between devices, shards(): lax.all_to_all(outgoing, 'xy', split_axis=0, concat_axis=0, tiled=True)  67.1 us
    dot_general x1, matrix products, shards(): jnp.dot(normed_in, input_weight, preferred_element_type=jnp.float32)  15.8 us
    unnamed x16, local copies, waits for them, and re-layouts  13.8 us
    gather x1, local copies, waits for them, and re-layouts, shards(): arranged = jnp.take(arrived_rows, fill, axis=0)  8.92 us
    dot_general x1, matrix products, attend(): jnp.einsum('bhij,bjhe->bihe', weights, values, preferred_element_type=jnp...  8.22 us
    all_to_all x1, starting transfers between devices, shards(): lax.all_to_all(outgoing, 'xy', split_axis=0, concat_axis=0, tiled=True)  7.24 us
    dot_general x1, matrix products, shards(): jnp.dot(gated, output_weight, preferred_element_type=jnp.float32)  6.8 us
    all_gather x1, local copies, waits for them, and re-layouts, shards(): lax.all_gather(history_cache, 'cand', axis=1, tiled=True)[0]  6.47 us
  transfers between devices with their start and end apart: 4, of which 2 were waited for; matrix products, arithmetic and copies ran while one was open for 36% of the time, Pallas kernels for 0%

profile of v1, /device:TPU:220, one launch (start us, length us, event | category | flops | bytes accessed | tf_op | source)
XLA Modules:
  0.0 224.5 jit_solution(4971782553543339096)
XLA Ops:
  8.1 5.4 %collective-permute-start = (bf16[256,1024]{1,0:T(8,128)(2,1)}, bf16[256,1024]{1,0:T(8,128)(2,1)S(1)}, u32[]{:S(2)}, u32[]{:S(2)}) collective-permute-start(bf16[256,1024]{1,0:T(8,128)(2,1)} %bitcast.70), channel_id=1, source_target_pairs={{0,128},{128,0},{1,129},{129,1},{2,130},{130,2},{3,131},{131,3},{4... | collective-permute-start | bytes 1572872 | tf_op jit(solution)/shard_map/ppermute | solution.py:82
  18.1 5.3 %gather_fusion.1 = bf16[1024,1024]{1,0:T(8,128)(2,1)} fusion(bf16[256,1024]{1,0:T(8,128)(2,1)S(1)} %bitcast.71, s32[1024]{0:T(1024)S(1)} %get-tuple-element.49), kind=kCustom, calls=%fused_computation.clone | custom fusion | bytes 4198400 | tf_op jit(solution)/shard_map/jit(_take)/gather | solution.py:87
  23.5 3.2 %broadcast_select_fusion.1 = bf16[1024,1024]{1,0:T(8,128)(2,1)} fusion(bf16[1024,1024]{1,0:T(8,128)(2,1)} %gather_fusion.1, pred[1024]{0:T(1024)(128)(4,1)S(1)} %compare_and_fusion.1), kind=kLoop, calls=%fused_computation.44 | loop fusion | flops 1048576 | bytes 4195328 | tf_op jit(solution)/shard_map/jit(_take)/select_n | solution.py:87
  33.8 3.6 %collective-permute-done = bf16[256,1024]{1,0:T(8,128)(2,1)S(1)} collective-permute-done((bf16[256,1024]{1,0:T(8,128)(2,1)}, bf16[256,1024]{1,0:T(8,128)(2,1)S(1)}, u32[]{:S(2)}, u32[]{:S(2)}) %collective-permute-start) | collective-permute-done | bytes 524320 | tf_op jit(solution)/shard_map/ppermute | solution.py:82
  37.3 5.3 %gather_fusion.2 = bf16[1024,1024]{1,0:T(8,128)(2,1)} fusion(bf16[256,1024]{1,0:T(8,128)(2,1)S(1)} %collective-permute-done, s32[1024]{0:T(1024)S(1)} %fusion.44), kind=kCustom, calls=%fused_computation.1.clone | custom fusion | bytes 4198400 | tf_op jit(solution)/shard_map/jit(_take)/gather | solution.py:88
  44.9 2.3 %pad_maximum_fusion = bf16[16,136,1024]{2,1,0:T(8,128)(2,1)} fusion(bf16[16,8,1024]{2,1,0:T(8,128)(2,1)S(1)} %scatter.9, bf16[16,64,1024]{2,1,0:T(8,128)(2,1)S(1)} %bitcast.77, bf16[16,64,1024]{2,1,0:T(8,128)(2,1)S(1)} %bitcast.76), kind=kLoop, calls=%fused_computation.11 | loop fusion | flops 13369344 | bytes 8912896 | tf_op jit(solution)/shard_map/concatenate | solution.py:97
  47.2 7.2 %all-to-all-start = ((bf16[16,136,1024]{2,1,0:T(8,128)(2,1)}), bf16[16,136,1024]{2,1,0:T(8,128)(2,1)}, u32[]{:S(2)}, u32[]{:S(2)}) async-start(bf16[16,136,1024]{2,1,0:T(8,128)(2,1)} %pad_maximum_fusion), calls=%async_computation | async-start | bytes 8912896 | tf_op jit(solution)/shard_map/all_to_all | solution.py:100
  55.3 67.1 %all-to-all-done = bf16[16,136,1024]{2,1,0:T(8,128)(2,1)} async-done(((bf16[16,136,1024]{2,1,0:T(8,128)(2,1)}), bf16[16,136,1024]{2,1,0:T(8,128)(2,1)}, u32[]{:S(2)}, u32[]{:S(2)}) %all-to-all-start) | async-done | bytes 4456480 | tf_op jit(solution)/shard_map/all_to_all | solution.py:100
  122.3 4.8 %slice.113 = bf16[16,128,1024]{2,1,0:T(8,128)(2,1)} slice(bf16[16,136,1024]{2,1,0:T(8,128)(2,1)} %all-to-all-done), slice={[0:16], [0:128], [0:1024]} | slice | bytes 8388608 | tf_op jit(solution)/shard_map/slice | solution.py:101
  128.8 8.9 %gather_fusion = bf16[1024,1024]{1,0:T(8,128)(2,1)} fusion(bf16[2048,1024]{1,0:T(8,128)(2,1)} %bitcast.72, s32[1024]{0:T(1024)S(1)} %broadcast_clamp_fusion), kind=kCustom, calls=%fused_computation.2 | custom fusion | bytes 4198400 | tf_op jit(solution)/shard_map/jit(_take)/gather | solution.py:109
  137.8 2.3 %convert_reduce_fusion = f32[1024]{0:T(1024)S(1)} fusion(bf16[1024,1024]{1,0:T(8,128)(2,1)} %gather_fusion, pred[1024]{0:T(1024)(128)(4,1)S(1)} %compare_and_fusion.2), kind=kLoop, calls=%fused_computation.8 | loop fusion | flops 3144704 | bytes 2102272 | tf_op jit(solution)/shard_map/reduce_sum | solution.py:17
  140.1 2.4 %fusion.2 = f32[1024]{0:T(1024)S(1)} fusion(f32[1024]{0:T(1024)S(1)} %broadcast_multiply_fusion.1, bf16[1024,1024]{1,0:T(8,128)(2,1)} %gather_fusion, pred[1024]{0:T(1024)(128)(4,1)S(1)} %compare_and_fusion.2), kind=kLoop, calls=%fused_computation.12 | loop fusion | flops 5241856 | bytes 2106368 | tf_op jit(solution)/shard_map/reduce_sum | solution.py:19
  142.6 15.8 %multiply_convert_fusion = bf16[1024,4096]{1,0:T(8,128)(2,1)} fusion(bf16[1024,4096]{1,0:T(8,128)(2,1)} %param.20, f32[1024]{0:T(1024)S(1)} %add_rsqrt_fusion, f32[1024]{0:T(1024)S(1)} %broadcast_multiply_fusion.1, bf16[1024,1024]{1,0:T(8,128)(2,1)S(1)} %copy-done.2, pred[1024]{0:T(1024)(128)(4,1)S(1)} %compare_and_fusion.2), kind=kOutput, calls=%fused_computation.3 | convolution fusion | flops 8616148992 | bytes 18883584 | tf_op jit(solution)/shard_map/dot_general | solution.py:120
  158.4 9.4 %copy.38 = bf16[128,8,32,128]{3,2,1,0:T(8,128)(2,1)} copy(bf16[128,8,32,128]{3,1,2,0:T(8,128)(2,1)} %bitcast.78) | data formatting | bytes 16777216
  167.8 4.8 %fusion.49 = (bf16[8,128,1,8,128]{4,3,2,1,0:T(8,128)(2,1)}, bf16[8,128,1,8,128]{4,3,2,1,0:T(8,128)(2,1)}) fusion(bf16[8,128,4,8,128]{4,3,2,1,0:T(8,128)(2,1)} %bitcast.73), kind=kLoop, calls=%fused_computation.115 | loop fusion | bytes 8388608 | tf_op jit(solution)/shard_map/slice | solution.py:125
  172.6 4.1 %copy.37 = bf16[8,128,1,8,128]{1,4,3,0,2:T(8,128)(2,1)} copy(bf16[8,128,1,8,128]{4,3,2,1,0:T(8,128)(2,1)} %get-tuple-element.37) | data formatting | bytes 4194304
  176.7 2.1 fusion.23
  178.9 4.2 %multiply_reduce_fusion = f32[8,128,8]{2,1,0:T(8,128)S(1)} fusion(f32[8,128,8,128]{3,1,2,0:T(8,128)S(1)} %fusion.23, bf16[8,128,4,8,128]{4,3,2,1,0:T(8,128)(2,1)} %bitcast.74), kind=kLoop, calls=%fused_computation.21 | loop fusion | flops 3137536 | bytes 6324224
  183.3 6.5 %copy.26 = bf16[1,8,128,2048]{2,3,1,0:T(8,128)(2,1)} copy(bf16[1,8,128,2048]{3,2,0,1:T(8,128)(2,1)} %all-gather.2.cloned.1.call-done) | data formatting | bytes 8388608 | tf_op jit(solution)/shard_map/all_gather | solution.py:136
  189.8 4.6 %fusion.50 = (bf16[8,128,1024]{1,2,0:T(8,128)(2,1)}, bf16[8,128,1024]{1,2,0:T(8,128)(2,1)}) fusion(bf16[8,128,2048]{1,2,0:T(8,128)(2,1)} %bitcast.75), kind=kLoop, calls=%fused_computation.116 | loop fusion | bytes 8388608 | tf_op jit(solution)/shard_map/slice | solution.py:27
  194.4 8.2 %fusion.52 = (f32[8,128]{1,0:T(8,128)S(1)}, f32[8,128,8,128]{1,3,2,0:T(8,128)}) fusion(bf16[8,128,1,8,128]{1,4,3,0,2:T(8,128)(2,1)} %copy.37, f32[8,128,8]{1,2,0:T(8,128)S(1)} %multiply_divide_fusion, bf16[8,128,8,128]{1,3,2,0:T(8,128)(2,1)} %bitcast.81, bf16[8,128,8,128]{1,3,2,0:T(8,128)(2,1)} %bitcast.80, f32[8,128]{1,0:T(8,128)S(1)} %fusion.41, ...), kind=kOutput, calls=%fused_computation.118 | convolution fusion | flops 549452800 | bytes 12623904 | tf_op jit(solution)/shard_map/bhij,bjhe->bihe/dot_general | solution.py:39
  202.6 5.4 %copy.29 = f32[8,128,8,128]{3,2,1,0:T(8,128)} copy(f32[8,128,8,128]{1,3,2,0:T(8,128)} %get-tuple-element.48) | data formatting | bytes 8388608 | tf_op jit(solution)/shard_map/add | solution.py:141
  208.0 2.8 %multiply_reduce_fusion.1 = f32[8,128]{1,0:T(8,128)S(1)} fusion(f32[8,128,8,128]{1,3,2,0:T(8,128)} %get-tuple-element.48, f32[8,128]{1,0:T(8,128)S(1)} %get-tuple-element.44), kind=kLoop, calls=%fused_computation.22 | loop fusion | flops 3144704 | bytes 4202496 | tf_op jit(solution)/shard_map/reduce_sum | solution.py:19
  210.8 6.8 %fusion.13 = bf16[1,1,1024,1024]{3,2,1,0:T(8,128)(2,1)} fusion(bf16[1024,1024]{1,0:T(8,128)(2,1)S(1)} %copy-done, f32[128,8,8,128]{3,2,1,0:T(8,128)} %bitcast.79, bf16[1024,4096]{1,0:T(8,128)(2,1)} %multiply_convert_fusion, f32[1024]{0:T(1024)S(1)} %rsqrt_bitcast_fusion, f32[1024]{0:T(1024)S(1)} %get-tuple-element.43, bf16[1024,1024]{1,0:T(8,128)(2,1)S(1)} %copy-done.3, ...), kind=kOutput, calls=%fused_computation.34 | convolution fusion | flops 2156920832 | bytes 12592128 | tf_op jit(solution)/shard_map/dot_general | solution.py:144
  (57 shorter events, 18.2 us)
Async XLA Ops:
  6.5 204.3 %copy-start = (bf16[1024,1024]{1,0:T(8,128)(2,1)S(1)}, bf16[1024,1024]{1,0:T(8,128)(2,1)}, u32[]{:S(2)}) copy-start(bf16[1024,1024]{1,0:T(8,128)(2,1)} %param.21) | copy-start | bytes 6291460
  6.5 11.6 %copy-start.1 = (bf16[1,1,256,1024]{3,2,1,0:T(8,128)(2,1)S(1)}, bf16[1,1,256,1024]{3,2,1,0:T(8,128)(2,1)}, u32[]{:S(2)}) copy-start(bf16[1,1,256,1024]{3,2,1,0:T(8,128)(2,1)} %param.14) | copy-start | bytes 1572868
  7.4 20.6 %collective-permute-start.1 = (s32[3,1024]{1,0:T(4,128)S(1)}, s32[3,1024]{1,0:T(4,128)S(1)}, u32[]{:S(2)}, u32[]{:S(2)}) collective-permute-start(s32[3,1024]{1,0:T(4,128)S(1)} %pad_add_fusion), channel_id=1, source_target_pairs={{0,128},{128,0},{1,129},{129,1},{2,130},{130,2},{3,131},{131,3},{4... | collective-permute-start | bytes 36872 | tf_op jit(solution)/shard_map/ppermute | solution.py:83
  8.1 29.3 %collective-permute-start = (bf16[256,1024]{1,0:T(8,128)(2,1)}, bf16[256,1024]{1,0:T(8,128)(2,1)S(1)}, u32[]{:S(2)}, u32[]{:S(2)}) collective-permute-start(bf16[256,1024]{1,0:T(8,128)(2,1)} %bitcast.70), channel_id=1, source_target_pairs={{0,128},{128,0},{1,129},{129,1},{2,130},{130,2},{3,131},{131,3},{4... | collective-permute-start | bytes 1572872 | tf_op jit(solution)/shard_map/ppermute | solution.py:82
  23.5 3.2 %copy-start.6 = (s32[3]{0:T(128)S(1)}, s32[3]{0:T(128)}, u32[]{:S(2)}) copy-start(s32[3]{0:T(128)} %constant.161.clone.1) | copy-start | bytes 40
  42.7 2.2 copy-start.4
  47.2 8.0 %copy-start.5 = (s32[1,8]{1,0:T(1,128)S(1)}, s32[1,8]{1,0:T(1,128)}, u32[]{:S(2)}) copy-start(s32[1,8]{1,0:T(1,128)} %param.19) | copy-start | bytes 100
  47.2 75.1 %all-to-all-start = ((bf16[16,136,1024]{2,1,0:T(8,128)(2,1)}), bf16[16,136,1024]{2,1,0:T(8,128)(2,1)}, u32[]{:S(2)}, u32[]{:S(2)}) async-start(bf16[16,136,1024]{2,1,0:T(8,128)(2,1)} %pad_maximum_fusion), calls=%async_computation | async-start | bytes 8912896 | tf_op jit(solution)/shard_map/all_to_all | solution.py:100
  54.5 128.9 %all-gather.2.cloned.1.call-start = ((), (), s32[]{:S(2)}) async-start(), calls=%async_computation.1 | async-start | bytes 4718592 | tf_op jit(solution)/shard_map/all_gather | solution.py:136
  137.8 4.8 %copy-start.2 = (bf16[1024,1024]{1,0:T(8,128)(2,1)S(1)}, bf16[1024,1024]{1,0:T(8,128)(2,1)}, u32[]{:S(2)}) copy-start(bf16[1024,1024]{1,0:T(8,128)(2,1)} %gather_fusion) | copy-start | bytes 6291460
  208.0 2.9 %copy-start.3 = (bf16[1024,1024]{1,0:T(8,128)(2,1)S(1)}, bf16[1024,1024]{1,0:T(8,128)(2,1)}, u32[]{:S(2)}) copy-start(bf16[1024,1024]{1,0:T(8,128)(2,1)} %gather_fusion) | copy-start | bytes 6291460
Sparse Core Ops, SparseCore 0:
  57.0 52.5 all-gather.1

commit v2 on v1

--- a/solution.py
+++ b/solution.py
@@ -20,25 +20,6 @@
     return centred * lax.rsqrt(variance + epsilon)
 
 
-def attend(queries, cache_rows, lengths, head_count, score_scale):
-    count_req, history_span, doubled = cache_rows.shape
-    feature = doubled // 2
-    head_width = feature // head_count
-    keys = cache_rows[:, :, :feature].reshape(count_req, history_span, head_count, head_width)
-    values = cache_rows[:, :, feature:].reshape(count_req, history_span, head_count, head_width)
-    scores = (
-        jnp.einsum("bihe,bjhe->bhij", queries, keys, preferred_element_type=jnp.float32)
-        * score_scale
-    )
-    positions = jnp.arange(history_span, dtype=jnp.int32)
-    valid = (positions[None, :] < lengths[:, None]).astype(jnp.float32)
-    length_plus = lengths.astype(jnp.float32) + 1.0
-    weights = (
-        jax.nn.silu(scores) / length_plus[:, None, None, None] * valid[:, None, None, :]
-    ).astype(jnp.bfloat16)
-    return jnp.einsum("bhij,bjhe->bihe", weights, values, preferred_element_type=jnp.float32)
-
-
 def ranks(targets, sources):
     count = targets.shape[0]
     one_hot = (targets[:, None] == jnp.arange(sources, dtype=jnp.int32)[None, :])
@@ -58,6 +39,15 @@
     row = jnp.sum(jnp.where(hit, picks[None, :], 0), axis=1)
     slot = jnp.sum(jnp.where(hit, places[None, :] + 1, 0), axis=1) - 1
     return row.reshape(n_half, per_pair), slot.reshape(n_half, per_pair)
+
+
+def select_rows(table, rows, slots):
+    flat_rows = rows.reshape(-1)
+    used = slots.reshape(-1) >= 0
+    entries = jnp.arange(table.shape[0], dtype=jnp.int32)
+    one_hot = ((flat_rows[:, None] == entries[None, :]) & used[:, None]).astype(table.dtype)
+    picked = jnp.dot(one_hot, table, preferred_element_type=jnp.float32).astype(table.dtype)
+    return picked.reshape(rows.shape + (table.shape[1],))
 
 
 def shards(
@@ -84,27 +74,30 @@
 
     own_row, own_slot = block_plan(ints, half, n_half, per_pair, sources)
     far_row, far_slot = block_plan(other_ints, half, n_half, per_pair, sources)
-    own_data = jnp.take(item_rows, own_row.reshape(-1), axis=0).reshape(n_half, per_pair, feature)
-    far_data = jnp.take(other_rows, far_row.reshape(-1), axis=0).reshape(n_half, per_pair, feature)
+    own_data = select_rows(item_rows, own_row, own_slot)
+    far_data = select_rows(other_rows, far_row, far_slot)
     slots = jnp.concatenate([own_slot, far_slot], axis=1)
     capacity = 2 * per_pair
+    tag_rows = 16
     radix = 32
     high = jnp.floor_divide(slots, radix)
     low = slots - high * radix
-    tag_row = jnp.zeros((n_half, 8, feature), jnp.float32)
-    tag_row = tag_row.at[:, 0, :capacity].set(high.astype(jnp.float32))
-    tag_row = tag_row.at[:, 0, capacity : 2 * capacity].set(low.astype(jnp.float32))
-    outgoing = jnp.concatenate(
-        [own_data, far_data, tag_row.astype(jnp.bfloat16)], axis=1
+    spare = jnp.zeros((n_half, feature - 2 * capacity), jnp.int32)
+    tag_line = jnp.concatenate([high, low, spare], axis=1).astype(jnp.bfloat16)
+    tag_block = jnp.concatenate(
+        [tag_line[:, None, :], jnp.zeros((n_half, tag_rows - 1, feature), jnp.bfloat16)], axis=1
     )
+    outgoing = jnp.concatenate([own_data, far_data, tag_block], axis=1)
     arrived = lax.all_to_all(outgoing, "xy", split_axis=0, concat_axis=0, tiled=True)
-    arrived_rows = arrived[:, :capacity].reshape(n_half * capacity, feature)
+    block = capacity + tag_rows
+    arrived_rows = arrived.reshape(n_half * block, feature)
     tags = (
         arrived[:, capacity, :capacity].astype(jnp.int32) * radix
         + arrived[:, capacity, capacity : 2 * capacity].astype(jnp.int32)
     ).reshape(-1)
     slot_ids = jnp.arange(slot_count, dtype=jnp.int32)
     order = jnp.arange(n_half * capacity, dtype=jnp.int32)
+    order = (order // capacity) * block + order % capacity
     fill = jnp.sum(jnp.where(tags[None, :] == slot_ids[:, None], order[None, :], 0), axis=1)
     arranged = jnp.take(arrived_rows, fill, axis=0)
 
@@ -119,26 +112,35 @@
     projected = jax.nn.silu(
         jnp.dot(normed_in, input_weight, preferred_element_type=jnp.float32)
     ).astype(jnp.bfloat16)
-    quarters = projected.reshape(members, per_request, 4, head_count, head_width)
     gate_u = projected[:, :feature]
-    own_values = quarters[:, :, 1]
-    queries = quarters[:, :, 2]
-    own_keys = quarters[:, :, 3]
     length_plus = lengths.astype(jnp.float32) + 1.0
-    own_scores = (
-        jnp.einsum("bihe,bihe->bih", queries, own_keys, preferred_element_type=jnp.float32)
-        * score_scale
-    )
-    own_weight = jax.nn.silu(own_scores) / length_plus[:, None, None]
-    own_term = own_weight[..., None] * own_values.astype(jnp.float32)
-    found = attend(
-        queries,
-        lax.all_gather(history_cache, "cand", axis=1, tiled=True)[0],
-        lengths,
-        head_count,
-        score_scale,
-    )
-    attended = (found + own_term).reshape(slot_count, feature)
+    cache = lax.all_gather(history_cache, "cand", axis=1, tiled=True)[0]
+    history_span = cache.shape[1]
+    positions = jnp.arange(history_span, dtype=jnp.int32)
+    valid = (positions[None, :] < lengths[:, None]).astype(jnp.float32)
+    outputs = []
+    for head in range(head_count):
+        def part(block, offset=head * head_width):
+            start = block * feature + offset
+            return projected[:, start : start + head_width].reshape(members, per_request, head_width)
+        own_values, queries, own_keys = part(1), part(2), part(3)
+        keys = cache[:, :, head * head_width : (head + 1) * head_width]
+        values = cache[:, :, feature + head * head_width : feature + (head + 1) * head_width]
+        scores = (
+            jnp.einsum("bie,bje->bij", queries, keys, preferred_element_type=jnp.float32)
+            * score_scale
+        )
+        weights = (
+            jax.nn.silu(scores) / length_plus[:, None, None] * valid[:, None, :]
+        ).astype(jnp.bfloat16)
+        found = jnp.einsum("bij,bje->bie", weights, values, preferred_element_type=jnp.float32)
+        own_scores = (
+            jnp.sum(queries.astype(jnp.float32) * own_keys.astype(jnp.float32), axis=-1)
+            * score_scale
+        )
+        own_weight = jax.nn.silu(own_scores) / length_plus[:, None]
+        outputs.append(found + own_weight[..., None] * own_values.astype(jnp.float32))
+    attended = jnp.concatenate(outputs, axis=-1).reshape(slot_count, feature)
     normed_out = layer_norm(attended)
     gated = (normed_out * gate_u.astype(jnp.float32)).astype(jnp.bfloat16)
     mixed = as_float + jnp.dot(gated, output_weight, preferred_element_type=jnp.float32)

time: 225 us -> 216 us (0.960)
  the two profiles are of different devices: /device:TPU:220 before, /device:TPU:92 now
where the time goes in v2:
time: 216 us; the launch traced here: 215 us
  waiting for transfers between devices  87.8 us (41%)
  matrix products  45.9 us (21%)
  local copies, waits for them, and re-layouts  28.4 us (13%)
  other arithmetic  25.9 us (12%)
  between operations  13.7 us (6%)
  starting transfers between devices  13.5 us (6%)
    all_to_all x1, waiting for transfers between devices, shards(): lax.all_to_all(outgoing, 'xy', split_axis=0, concat_axis=0, tiled=True)  69.3 us
    dot_general x8, matrix products, shards(): jnp.einsum('bij,bje->bie', weights, values, preferred_element_type=jnp.fl...  20.9 us
    ppermute x1, waiting for transfers between devices, shards(): other_rows = lax.ppermute(item_rows, 'zh', swap)  18 us
    dot_general x1, matrix products, shards(): jnp.dot(normed_in, input_weight, preferred_element_type=jnp.float32)  14.9 us
    gather x1, local copies, waits for them, and re-layouts, shards(): arranged = jnp.take(arrived_rows, fill, axis=0)  8.95 us
    convert_element_type x8, local copies, waits for them, and re-layouts, shards(): own_values.astype(jnp.float32)  8.94 us
    all_to_all x1, starting transfers between devices, shards(): lax.all_to_all(outgoing, 'xy', split_axis=0, concat_axis=0, tiled=True)  7.24 us
    ppermute x1, starting transfers between devices, shards(): other_ints = lax.ppermute(ints, 'zh', swap)  5.48 us
  transfers between devices with their start and end apart: 4, of which 2 were waited for; matrix products, arithmetic and copies ran while one was open for 26% of the time, Pallas kernels for 0%

profile of v2, /device:TPU:92, one launch (start us, length us, event | category | flops | bytes accessed | tf_op | source)
XLA Modules:
  0.0 215.1 jit_solution(7630457811827415851)
XLA Ops:
  7.4 5.5 %collective-permute-start = (s32[3,1024]{1,0:T(4,128)S(1)}, s32[3,1024]{1,0:T(4,128)S(1)}, u32[]{:S(2)}, u32[]{:S(2)}) collective-permute-start(s32[3,1024]{1,0:T(4,128)S(1)} %pad_add_fusion), channel_id=1, source_target_pairs={{0,128},{128,0},{1,129},{129,1},{2,130},{130,2},{3,131},{131,3},{4... | collective-permute-start | bytes 36872 | tf_op jit(solution)/shard_map/ppermute | solution.py:73
  18.1 3.3 %convolution_convert_fusion.1 = bf16[1024,1024]{1,0:T(8,128)(2,1)} fusion(s32[1024]{0:T(1024)S(1)} %get-tuple-element.13, pred[1024]{0:T(1024)(128)(4,1)S(1)} %broadcast_compare_fusion, bf16[1,1,256,1024]{3,2,1,0:T(8,128)(2,1)} %param.8), kind=kOutput, calls=%fused_computation.33 | convolution fusion | flops 538443776 | bytes 2626560 | tf_op jit(solution)/shard_map/dot_general | solution.py:49
  23.7 18.0 %collective-permute-done.1 = bf16[256,1024]{1,0:T(8,128)(2,1)S(1)} collective-permute-done((bf16[256,1024]{1,0:T(8,128)(2,1)}, bf16[256,1024]{1,0:T(8,128)(2,1)S(1)}, u32[]{:S(2)}, u32[]{:S(2)}) %collective-permute-start.1) | collective-permute-done | bytes 524320 | tf_op jit(solution)/shard_map/ppermute | solution.py:72
  42.9 4.5 %maximum_maximum_fusion = bf16[16,144,1024]{2,1,0:T(8,128)(2,1)} fusion(bf16[16,1,128]{2,1,0:T(2,128)(2,1)S(1)} %copy.67, bf16[16,1,128]{2,1,0:T(2,128)(2,1)S(1)} %copy.66, bf16[16,64,1024]{2,1,0:T(8,128)(2,1)S(1)} %bitcast.182, bf16[16,64,1024]{2,1,0:T(8,128)(2,1)} %bitcast.181, bf16[144]{0:T(256)(128)(2,1)S(1)} %pad.5.clone, bf16[144,1024]{1,0:T(8,128)(2,1)S(1)} %pad.4.clone), kind=kLoop, calls=%fused_computation.9 | loop fusion | flops 28311552 | bytes 9216288 | tf_op jit(solution)/shard_map/concatenate | solution.py:90
  47.4 7.2 %all-to-all-start = ((bf16[16,144,1024]{2,1,0:T(8,128)(2,1)}), bf16[16,144,1024]{2,1,0:T(8,128)(2,1)}, u32[]{:S(2)}, u32[]{:S(2)}) async-start(bf16[16,144,1024]{2,1,0:T(8,128)(2,1)} %maximum_maximum_fusion), calls=%async_computation | async-start | bytes 9437184 | tf_op jit(solution)/shard_map/all_to_all | solution.py:91
  55.5 69.3 %all-to-all-done = bf16[16,144,1024]{2,1,0:T(8,128)(2,1)} async-done(((bf16[16,144,1024]{2,1,0:T(8,128)(2,1)}), bf16[16,144,1024]{2,1,0:T(8,128)(2,1)}, u32[]{:S(2)}, u32[]{:S(2)}) %all-to-all-start) | async-done | bytes 4718624 | tf_op jit(solution)/shard_map/all_to_all | solution.py:91
  126.5 9.0 %gather_fusion = bf16[1024,1024]{1,0:T(8,128)(2,1)} fusion(bf16[2304,1024]{1,0:T(8,128)(2,1)} %bitcast.17, s32[1024]{0:T(1024)S(1)} %broadcast_clamp_fusion), kind=kCustom, calls=%fused_computation | custom fusion | bytes 4198400 | tf_op jit(solution)/shard_map/jit(_take)/gather | solution.py:102
  135.5 2.3 %convert_reduce_fusion = f32[1024]{0:T(1024)S(1)} fusion(bf16[1024,1024]{1,0:T(8,128)(2,1)} %gather_fusion, pred[1024]{0:T(1024)(128)(4,1)S(1)} %compare_and_fusion), kind=kLoop, calls=%fused_computation.6 | loop fusion | flops 3144704 | bytes 2102272 | tf_op jit(solution)/shard_map/reduce_sum | solution.py:17
  137.9 2.4 %fusion.2 = f32[1024]{0:T(1024)S(1)} fusion(f32[1024]{0:T(1024)S(1)} %broadcast_multiply_fusion, bf16[1024,1024]{1,0:T(8,128)(2,1)} %gather_fusion, pred[1024]{0:T(1024)(128)(4,1)S(1)} %compare_and_fusion), kind=kLoop, calls=%fused_computation.10 | loop fusion | flops 5241856 | bytes 2106368 | tf_op jit(solution)/shard_map/reduce_sum | solution.py:19
  140.3 14.9 %multiply_convert_fusion = bf16[1024,4096]{1,0:T(8,128)(2,1)S(1)} fusion(bf16[1024,4096]{1,0:T(8,128)(2,1)} %param.14, f32[1024]{0:T(1024)S(1)} %add_rsqrt_fusion, f32[1024]{0:T(1024)S(1)} %broadcast_multiply_fusion, bf16[1024,1024]{1,0:T(8,128)(2,1)S(1)} %copy-done.1, pred[1024]{0:T(1024)(128)(4,1)S(1)} %compare_and_fusion), kind=kOutput, calls=%fused_computation.1 | convolution fusion | flops 8616148992 | bytes 18883584 | tf_op jit(solution)/shard_map/dot_general | solution.py:113
  155.2 2.6 %fusion.161 = (bf16[1024,128]{1,0:T(8,128)(2,1)}, bf16[1024,128]{1,0:T(8,128)(2,1)S(1)}, bf16[1024,128]{1,0:T(8,128)(2,1)S(1)}, bf16[1024,128]{1,0:T(8,128)(2,1)...) fusion(bf16[1024,4096]{1,0:T(8,128)(2,1)S(1)} %multiply_convert, ...), kind=kLoop, calls=%fused_computation.270 | loop fusion | bytes 8388608 | tf_op jit(solution)/shard_map/slice | solution.py:125
  168.5 3.5 %multiply_reduce_fusion.1 = (f32[1024]{0:T(1024)S(1)}, f32[1024]{0:T(1024)S(1)}, f32[1024]{0:T(1024)S(1)}, f32[1024]{0:T(1024)S(1)}, f32[1024]{0:T(1024)S(1)}, /...) fusion(bf16[1024,4096]{1,0:T(8,128)(2,1)} %copy-done.4), kind=kLoop, calls=%fused_computation.58 | loop fusion | flops 4186112 | bytes 4227072 | tf_op jit(solution)/shard_map/reduce_sum | solution.py:138
  172.0 2.7 %fusion.163 = (f32[8,128]{1,0:T(8,128)S(1)}, f32[8,128,1024]{1,2,0:T(8,128)}) fusion(f32[8,128,128]{1,2,0:T(8,128)} %copy.70, f32[8,128]{1,0:T(8,128)S(1)} %get-tuple-element.61, bf16[8,128,2048]{2,1,0:T(8,128)(2,1)} %bitcast.218, bf16[8,128,128]{2,1,0:T(8,128)(2,1)} %bitcast.200, f32[8,128]{1,0:T(8,128)S(1)} %fusion.142, f32[8]{0:T(128)S(1)} %convert_add_fusion.1), kind=kOutput, calls=%fused_computation.272 | convolution fusion | flops 68549632 | bytes 1847328 | tf_op jit(solution)/shard_map/bij,bje->bie/dot_general | solution.py:136
  174.7 2.6 %fusion.162 = (f32[8,128]{1,0:T(8,128)S(1)}, f32[8,128,1024]{1,2,0:T(8,128)}) fusion(f32[8,128,1024]{1,2,0:T(8,128)} %get-tuple-element.36, f32[8,128,128]{1,2,0:T(8,128)} %copy.72, f32[8,128]{1,0:T(8,128)S(1)} %get-tuple-element.55, bf16[8,128,2048]{2,1,0:T(8,128)(2,1)} %bitcast.219, bf16[8,128,128]{2,1,0:T(8,128)(2,1)S(1)} %bitcast.199, ...), kind=kOutput, calls=%fused_computation.271 | convolution fusion | flops 68549632 | bytes 1847328 | tf_op jit(solution)/shard_map/bij,bje->bie/dot_general | solution.py:136
  177.2 2.7 %fusion.164 = (f32[8,128]{1,0:T(8,128)S(1)}, f32[8,128,1024]{1,2,0:T(8,128)}) fusion(f32[8,128,1024]{1,2,0:T(8,128)} %get-tuple-element.34, f32[8,128,128]{1,2,0:T(8,128)} %copy.74, f32[8,128]{1,0:T(8,128)S(1)} %get-tuple-element.56, bf16[8,128,2048]{2,1,0:T(8,128)(2,1)} %bitcast.220, bf16[8,128,128]{2,1,0:T(8,128)(2,1)} %bitcast.198, ...), kind=kOutput, calls=%fused_computation.273 | convolution fusion | flops 68549632 | bytes 1847328 | tf_op jit(solution)/shard_map/bij,bje->bie/dot_general | solution.py:136
  180.0 2.6 %fusion.165 = (f32[8,128]{1,0:T(8,128)S(1)}, f32[8,128,1024]{1,2,0:T(8,128)}) fusion(f32[8,128,1024]{1,2,0:T(8,128)} %get-tuple-element.38, f32[8,128,128]{1,2,0:T(8,128)} %copy.76, f32[8,128]{1,0:T(8,128)S(1)} %get-tuple-element.57, bf16[8,128,2048]{2,1,0:T(8,128)(2,1)} %bitcast.221, bf16[8,128,128]{2,1,0:T(8,128)(2,1)S(1)} %bitcast.197, ...), kind=kOutput, calls=%fused_computation.274 | convolution fusion | flops 68549632 | bytes 1847328 | tf_op jit(solution)/shard_map/bij,bje->bie/dot_general | solution.py:136
  182.6 2.7 %fusion.166 = (f32[8,128]{1,0:T(8,128)S(1)}, f32[8,128,1024]{1,2,0:T(8,128)}) fusion(f32[8,128,1024]{1,2,0:T(8,128)} %get-tuple-element.40, f32[8,128,128]{1,2,0:T(8,128)} %copy.78, f32[8,128]{1,0:T(8,128)S(1)} %get-tuple-element.58, bf16[8,128,2048]{2,1,0:T(8,128)(2,1)} %bitcast.222, bf16[8,128,128]{2,1,0:T(8,128)(2,1)} %bitcast.196, ...), kind=kOutput, calls=%fused_computation.275 | convolution fusion | flops 68549632 | bytes 1847328 | tf_op jit(solution)/shard_map/bij,bje->bie/dot_general | solution.py:136
  185.3 2.6 %fusion.167 = (f32[8,128]{1,0:T(8,128)S(1)}, f32[8,128,1024]{1,2,0:T(8,128)}) fusion(f32[8,128,1024]{1,2,0:T(8,128)} %get-tuple-element.42, f32[8,128,128]{1,2,0:T(8,128)} %copy.80, f32[8,128]{1,0:T(8,128)S(1)} %get-tuple-element.59, bf16[8,128,2048]{2,1,0:T(8,128)(2,1)} %bitcast.223, bf16[8,128,128]{2,1,0:T(8,128)(2,1)S(1)} %bitcast.195, ...), kind=kOutput, calls=%fused_computation.276 | convolution fusion | flops 68549632 | bytes 1847328 | tf_op jit(solution)/shard_map/bij,bje->bie/dot_general | solution.py:136
  187.9 2.5 %fusion.168 = (f32[8,128]{1,0:T(8,128)S(1)}, f32[8,128,1024]{1,2,0:T(8,128)}) fusion(f32[8,128,1024]{1,2,0:T(8,128)} %get-tuple-element.44, f32[8,128,128]{1,2,0:T(8,128)S(1)} %copy.82, f32[8,128]{1,0:T(8,128)S(1)} %get-tuple-element.60, bf16[8,128,2048]{2,1,0:T(8,128)(2,1)} %bitcast.224, bf16[8,128,128]{2,1,0:T(8,128)(2,1)} %bitcast.194, ...), kind=kOutput, calls=%fused_computation.277 | convolution fusion | flops 68549632 | bytes 1847328 | tf_op jit(solution)/shard_map/bij,bje->bie/dot_general | solution.py:136
  190.4 2.5 %fusion.169 = (f32[8,128]{1,0:T(8,128)S(1)}, f32[8,128,1024]{1,2,0:T(8,128)}) fusion(f32[8,128,1024]{1,2,0:T(8,128)} %get-tuple-element.46, f32[8,128,128]{1,2,0:T(8,128)S(1)} %copy.84, f32[8,128]{1,0:T(8,128)S(1)} %get-tuple-element.54, bf16[8,128,2048]{2,1,0:T(8,128)(2,1)} %bitcast.225, bf16[8,128,128]{2,1,0:T(8,128)(2,1)S(1)} %bitcast.193, ...), kind=kOutput, calls=%fused_computation.278 | convolution fusion | flops 68549632 | bytes 1847328 | tf_op jit(solution)/shard_map/bij,bje->bie/dot_general | solution.py:136
  192.9 5.3 %copy.85 = f32[8,128,1024]{2,1,0:T(8,128)} copy(f32[8,128,1024]{1,2,0:T(8,128)} %get-tuple-element.48) | data formatting | bytes 8388608 | tf_op jit(solution)/shard_map/concatenate | solution.py:143
  198.2 2.8 %multiply_reduce_fusion = f32[8,128]{1,0:T(8,128)S(1)} fusion(f32[8,128,1024]{1,2,0:T(8,128)} %get-tuple-element.48, f32[8,128]{1,0:T(8,128)S(1)} %add_multiply_fusion), kind=kLoop, calls=%fused_computation.17 | loop fusion | flops 3144704 | bytes 4202496 | tf_op jit(solution)/shard_map/reduce_sum | solution.py:19
  201.7 2.9 %fusion.7 = bf16[1024,1024]{1,0:T(8,128)(2,1)S(1)} fusion(f32[8,128,1024]{2,1,0:T(8,128)S(1)} %copy-done.3, bf16[1024,4096]{1,0:T(8,128)(2,1)} %copy-done.4, f32[1024]{0:T(1024)S(1)} %rsqrt_bitcast_fusion, f32[1024]{0:T(1024)S(1)} %bitcast.201), kind=kLoop, calls=%fused_computation.16 | loop fusion | flops 5242880 | bytes 8396800 | tf_op jit(solution)/shard_map/convert_element_type | solution.py:145
  204.6 3.7 %fusion.10 = bf16[1,1,1024,1024]{3,2,1,0:T(8,128)(2,1)} fusion(bf16[1024,1024]{1,0:T(8,128)(2,1)S(1)} %fusion.7, bf16[1024,1024]{1,0:T(8,128)(2,1)S(1)} %copy-done, bf16[1024,1024]{1,0:T(8,128)(2,1)S(1)} %copy-done.2, pred[1024]{0:T(1024)(128)(4,1)S(1)} %compare_and_fusion), kind=kOutput, calls=%fused_computation.27 | convolution fusion | flops 2151677952 | bytes 8389632 | tf_op jit(solution)/shard_map/dot_general | solution.py:146
  (70 shorter events, 23.4 us)
Async XLA Ops:
  6.5 198.1 %copy-start = (bf16[1024,1024]{1,0:T(8,128)(2,1)S(1)}, bf16[1024,1024]{1,0:T(8,128)(2,1)}, u32[]{:S(2)}) copy-start(bf16[1024,1024]{1,0:T(8,128)(2,1)} %param.15) | copy-start | bytes 6291460
  7.4 14.2 %collective-permute-start = (s32[3,1024]{1,0:T(4,128)S(1)}, s32[3,1024]{1,0:T(4,128)S(1)}, u32[]{:S(2)}, u32[]{:S(2)}) collective-permute-start(s32[3,1024]{1,0:T(4,128)S(1)} %pad_add_fusion), channel_id=1, source_target_pairs={{0,128},{128,0},{1,129},{129,1},{2,130},{130,2},{3,131},{131,3},{4... | collective-permute-start | bytes 36872 | tf_op jit(solution)/shard_map/ppermute | solution.py:73
  12.9 28.7 %collective-permute-start.1 = (bf16[256,1024]{1,0:T(8,128)(2,1)}, bf16[256,1024]{1,0:T(8,128)(2,1)S(1)}, u32[]{:S(2)}, u32[]{:S(2)}) collective-permute-start(bf16[256,1024]{1,0:T(8,128)(2,1)} %bitcast.191), channel_id=1, source_target_pairs={{0,128},{128,0},{1,129},{129,1},{2,130},{130,2},{3,131},{131,3},{4... | collective-permute-start | bytes 1572872 | tf_op jit(solution)/shard_map/ppermute | solution.py:72
  47.4 8.0 %copy-start.9 = (s32[1,8]{1,0:T(1,128)S(1)}, s32[1,8]{1,0:T(1,128)}, u32[]{:S(2)}) copy-start(s32[1,8]{1,0:T(1,128)} %param.13) | copy-start | bytes 100
  47.4 77.4 %all-to-all-start = ((bf16[16,144,1024]{2,1,0:T(8,128)(2,1)}), bf16[16,144,1024]{2,1,0:T(8,128)(2,1)}, u32[]{:S(2)}, u32[]{:S(2)}) async-start(bf16[16,144,1024]{2,1,0:T(8,128)(2,1)} %maximum_maximum_fusion), calls=%async_computation | async-start | bytes 9437184 | tf_op jit(solution)/shard_map/all_to_all | solution.py:91
  54.6 117.4 %all-gather.2.cloned.1.call-start = ((), (), s32[]{:S(2)}) async-start(), calls=%async_computation.1 | async-start | bytes 4718592 | tf_op jit(solution)/shard_map/all_gather | solution.py:117
  135.5 4.8 %copy-start.1 = (bf16[1024,1024]{1,0:T(8,128)(2,1)S(1)}, bf16[1024,1024]{1,0:T(8,128)(2,1)}, u32[]{:S(2)}) copy-start(bf16[1024,1024]{1,0:T(8,128)(2,1)} %gather_fusion) | copy-start | bytes 6291460
  155.2 4.3 %copy-start.4 = (bf16[1024,4096]{1,0:T(8,128)(2,1)}, bf16[1024,4096]{1,0:T(8,128)(2,1)S(1)}, u32[]{:S(2)}) copy-start(bf16[1024,4096]{1,0:T(8,128)(2,1)S(1)} %multiply_convert_fusion) | copy-start | bytes 25165828
  168.5 6.2 %copy-start.8 = (bf16[1024,128]{1,0:T(8,128)(2,1)S(1)}, bf16[1024,128]{1,0:T(8,128)(2,1)}, u32[]{:S(2)}) copy-start(bf16[1024,128]{1,0:T(8,128)(2,1)} %get-tuple-element.29) | copy-start | bytes 786436
  177.2 2.7 %copy-start.7 = (bf16[1024,128]{1,0:T(8,128)(2,1)S(1)}, bf16[1024,128]{1,0:T(8,128)(2,1)}, u32[]{:S(2)}) copy-start(bf16[1024,128]{1,0:T(8,128)(2,1)} %get-tuple-element.24) | copy-start | bytes 786436
  182.6 2.7 %copy-start.6 = (bf16[1024,128]{1,0:T(8,128)(2,1)S(1)}, bf16[1024,128]{1,0:T(8,128)(2,1)}, u32[]{:S(2)}) copy-start(bf16[1024,128]{1,0:T(8,128)(2,1)} %get-tuple-element.20) | copy-start | bytes 786436
  187.9 2.5 %copy-start.5 = (bf16[1024,128]{1,0:T(8,128)(2,1)S(1)}, bf16[1024,128]{1,0:T(8,128)(2,1)}, u32[]{:S(2)}) copy-start(bf16[1024,128]{1,0:T(8,128)(2,1)} %get-tuple-element.17) | copy-start | bytes 786436
  198.2 3.4 %copy-start.3 = (f32[8,128,1024]{2,1,0:T(8,128)S(1)}, f32[8,128,1024]{2,1,0:T(8,128)}, u32[]{:S(2)}) copy-start(f32[8,128,1024]{2,1,0:T(8,128)} %copy.85) | copy-start | bytes 12582916
  201.7 2.9 %copy-start.2 = (bf16[1024,1024]{1,0:T(8,128)(2,1)S(1)}, bf16[1024,1024]{1,0:T(8,128)(2,1)}, u32[]{:S(2)}) copy-start(bf16[1024,1024]{1,0:T(8,128)(2,1)} %gather_fusion) | copy-start | bytes 6291460
Sparse Core Ops, SparseCore 0:
  57.2 49.1 all-gather.1

commit v3 on v2

v3 whole, which is shorter than its diff:
```python
import math

import functools

import jax
import jax.numpy as jnp
from jax import lax
from jax.experimental import pallas as pl
from jax.experimental.pallas import tpu as pltpu
from jax.sharding import Mesh
from jax.sharding import PartitionSpec as P

HEADS = 8
HALVES = 2


epsilon = 1e-06


def layer_norm(values):
    average = jnp.mean(values, axis=-1, keepdims=True)
    centred = values - average
    variance = jnp.mean(centred * centred, axis=-1, keepdims=True)
    return centred * lax.rsqrt(variance + epsilon)


def silu(v):
    return v / (1.0 + jnp.exp(-v))

def tail_kernel(len_ref, proj_ref, cache_ref, rows_ref, wout_ref, out_ref, att_ref, *, heads, eps):
    b = pl.program_id(0)
    feature = rows_ref.shape[1]
    head_width = feature // heads
    hist = cache_ref.shape[1]
    scale = 1.0 / math.sqrt(head_width)
    length = len_ref[b]
    length_plus = length.astype(jnp.float32) + 1.0
    valid = lax.broadcasted_iota(jnp.int32, (1, hist), 1) < length
    for h in range(heads):
        lo = h * head_width
        q = proj_ref[:, 2 * feature + lo : 2 * feature + lo + head_width]
        k = cache_ref[0, :, lo : lo + head_width]
        v = cache_ref[0, :, feature + lo : feature + lo + head_width]
        s = lax.dot_general(q, k, (((1,), (1,)), ((), ())), preferred_element_type=jnp.float32) * scale
        w = jnp.where(valid, silu(s) / length_plus, 0.0).astype(jnp.bfloat16)
        found = jnp.dot(w, v, preferred_element_type=jnp.float32)
        own_k = proj_ref[:, 3 * feature + lo : 3 * feature + lo + head_width].astype(jnp.float32)
        own_v = proj_ref[:, feature + lo : feature + lo + head_width].astype(jnp.float32)
        own_s = jnp.sum(q.astype(jnp.float32) * own_k, axis=-1, keepdims=True) * scale
        att_ref[:, lo : lo + head_width] = found + (silu(own_s) / length_plus) * own_v
    att = att_ref[...]
    mean = jnp.mean(att, axis=-1, keepdims=True)
    centred = att - mean
    var = jnp.mean(centred * centred, axis=-1, keepdims=True)
    normed = centred * lax.rsqrt(var + eps)
    gated = (normed * proj_ref[:, 0:feature].astype(jnp.float32)).astype(jnp.bfloat16)
    update = jnp.dot(gated, wout_ref[...], preferred_element_type=jnp.float32)
    out_ref[...] = (rows_ref[...].astype(jnp.float32) + update).astype(out_ref.dtype)

def tail(lengths, projected, cache, rows, wout, heads=8, eps=1e-6):
    members, hist, doubled = cache.shape
    slots, feature = rows.shape
    per = slots // members
    width = projected.shape[1]
    kern = functools.partial(tail_kernel, heads=heads, eps=eps)
    spec = pltpu.PrefetchScalarGridSpec(
        num_scalar_prefetch=1, grid=(members,),
        in_specs=[pl.BlockSpec((per, width), lambda b, n: (b, 0)),
                  pl.BlockSpec((1, hist, doubled), lambda b, n: (b, 0, 0)),
                  pl.BlockSpec((per, feature), lambda b, n: (b, 0)),
                  pl.BlockSpec((feature, feature), lambda b, n: (0, 0))],
        out_specs=pl.BlockSpec((per, feature), lambda b, n: (b, 0)),
        scratch_shapes=[pltpu.VMEM((per, feature), jnp.float32)])
    return pl.pallas_call(kern, grid_spec=spec, out_shape=jax.ShapeDtypeStruct((slots, feature), jnp.bfloat16),
        cost_estimate=pl.CostEstimate(flops=2*slots*feature*feature + 4*slots*hist*feature, transcendentals=slots*(hist*heads+heads), bytes_accessed=slots*width*2 + members*hist*doubled*2 + 2*slots*feature*2 + feature*feature*2))(lengths, projected, cache, rows, wout)


def ranks(targets, sources):
    count = targets.shape[0]
    one_hot = (targets[:, None] == jnp.arange(sources, dtype=jnp.int32)[None, :])
    rows = jnp.arange(count, dtype=jnp.int32)
    lower = (rows[None, :] < rows[:, None]).astype(jnp.bfloat16)
    earlier = jnp.dot(lower, one_hot.astype(jnp.bfloat16), preferred_element_type=jnp.float32)
    return jnp.sum(jnp.where(one_hot, earlier, 0.0), axis=1).astype(jnp.int32)


def block_plan(ints, half, n_half, per_pair, sources):
    picks, targets, places = ints[0], ints[1], ints[2]
    within = ranks(targets, sources)
    keep = (targets // n_half) == half
    position = jnp.where(keep, (targets % n_half) * per_pair + within, -1)
    spots = jnp.arange(n_half * per_pair, dtype=jnp.int32)
    hit = position[None, :] == spots[:, None]
    row = jnp.sum(jnp.where(hit, picks[None, :], 0), axis=1)
    slot = jnp.sum(jnp.where(hit, places[None, :] + 1, 0), axis=1) - 1
    return row.reshape(n_half, per_pair), slot.reshape(n_half, per_pair)


def select_rows(table, rows, slots):
    flat_rows = rows.reshape(-1)
    used = slots.reshape(-1) >= 0
    entries = jnp.arange(table.shape[0], dtype=jnp.int32)
    one_hot = ((flat_rows[:, None] == entries[None, :]) & used[:, None]).astype(table.dtype)
    picked = jnp.dot(one_hot, table, preferred_element_type=jnp.float32).astype(table.dtype)
    return picked.reshape(rows.shape + (table.shape[1],))


def shards(
    item_table,
    picked_items,
    destination,
    slot_index,
    history_cache,
    history_length,
    input_weight,
    output_weight,
):
    n_half = lax.axis_size("xy")
    sources = HALVES * n_half
    half = lax.axis_index("zh")
    item_rows = item_table[0, 0]
    ints = jnp.stack([picked_items[0, 0], destination[0, 0], slot_index[0, 0]])
    slot_count = ints.shape[1]
    feature = item_rows.shape[1]
    per_pair = 2 * slot_count // sources
    swap = [(0, 1), (1, 0)]
    other_rows = lax.ppermute(item_rows, "zh", swap)
    other_ints = lax.ppermute(ints, "zh", swap)

    own_row, own_slot = block_plan(ints, half, n_half, per_pair, sources)
    far_row, far_slot = block_plan(other_ints, half, n_half, per_pair, sources)
    own_data = select_rows(item_rows, own_row, own_slot)
    far_data = select_rows(other_rows, far_row, far_slot)
    slots = jnp.concatenate([own_slot, far_slot], axis=1)
    capacity = 2 * per_pair
    every_slot = lax.all_gather(slots, "xy", axis=0, tiled=False)
    tags = lax.dynamic_index_in_dim(every_slot, lax.axis_index("xy"), axis=1, keepdims=False)
    tags = tags.reshape(-1)
    outgoing = jnp.concatenate([own_data, far_data], axis=1)
    arrived = lax.all_to_all(outgoing, "xy", split_axis=0, concat_axis=0, tiled=True)
    arrived_rows = arrived.reshape(n_half * capacity, feature)
    slot_ids = jnp.arange(slot_count, dtype=jnp.int32)
    order = jnp.arange(n_half * capacity, dtype=jnp.int32)
    fill = jnp.sum(jnp.where(tags[None, :] == slot_ids[:, None], order[None, :], 0), axis=1)
    arranged = jnp.take(arrived_rows, fill, axis=0)

    lengths = history_length[0]
    as_float = arranged.astype(jnp.float32)
    normed_in = layer_norm(as_float).astype(jnp.bfloat16)
    projected = jax.nn.silu(
        jnp.dot(normed_in, input_weight, preferred_element_type=jnp.float32)
    ).astype(jnp.bfloat16)
    cache = lax.all_gather(history_cache, "cand", axis=1, tiled=True)[0]
    mixed = tail(lengths, projected, cache, arranged, output_weight)
    return mixed[None, None]


def solution(mesh):
    n_req, n_cand = mesh.devices.shape
    devices = mesh.devices.reshape(HALVES, n_req // HALVES, n_cand)
    split = Mesh(devices, ("zh", "xy", "cand"))
    req = ("zh", "xy")
    in_specs = (
        P(req, "cand", None, None),
        P(req, "cand", None),
        P(req, "cand", None),
        P(req, "cand", None),
        P(req, "cand", None, None),
        P(req, None),
        P(),
        P(),
    )
    out_specs = P(req, "cand", None, None)
    return jax.shard_map(shards, mesh=split, in_specs=in_specs, out_specs=out_specs, check_vma=False)
```

time: 216 us -> 183 us (0.85)
  the two profiles are of different devices: /device:TPU:92 before, /device:TPU:64 now
where the time goes in v3:
time: 183 us; the launch traced here: 181 us
  blocking collectives  71.2 us (39%)
  matrix products  21.1 us (12%)
  Pallas kernels  20.9 us (11%)
  waiting for transfers between devices  20 us (11%)
  between operations  13.6 us (7%)
  starting transfers between devices  13.1 us (7%)
  other arithmetic  12 us (7%)
  local copies, waits for them, and re-layouts  8.9 us (5%)
    all_gather x1, blocking collectives, shards(): every_slot = lax.all_gather(slots, 'xy', axis=0, tiled=False)  71.2 us
    pallas_call x1, Pallas kernels, tail(): pl.pallas_call(kern, grid_spec=spec, out_shape=jax.ShapeDtypeStruct((slot...  20.9 us
    ppermute x1, waiting for transfers between devices, shards(): other_rows = lax.ppermute(item_rows, 'zh', swap)  19.3 us
    dot_general x1, matrix products, shards(): jnp.dot(normed_in, input_weight, preferred_element_type=jnp.float32)  15.6 us
    gather x1, local copies, waits for them, and re-layouts, shards(): arranged = jnp.take(arrived_rows, fill, axis=0)  8.74 us
    all_to_all x1, starting transfers between devices, shards(): lax.all_to_all(outgoing, 'xy', split_axis=0, concat_axis=0, tiled=True)  7.09 us
    ppermute x1, starting transfers between devices, shards(): other_ints = lax.ppermute(ints, 'zh', swap)  5.48 us
  transfers between devices with their start and end apart: 4, of which 1 were waited for; matrix products, arithmetic and copies ran while one was open for 21% of the time, Pallas kernels for 0%

profile of v3, /device:TPU:64, one launch (start us, length us, event | category | flops | bytes accessed | tf_op | source)
XLA Modules:
  0.0 180.8 jit_solution(7830269865696585949)
XLA Ops:
  6.5 0.7 pad_add_fusion
  7.3 5.5 %collective-permute-start = (s32[3,1024]{1,0:T(4,128)S(1)}, s32[3,1024]{1,0:T(4,128)S(1)}, u32[]{:S(2)}, u32[]{:S(2)}) collective-permute-start(s32[3,1024]{1,0:T(4,128)S(1)} %pad_add_fusion), channel_id=1, source_target_pairs={{0,128},{128,0},{1,129},{129,1},{2,130},{130,2},{3,131},{131,3},{4... | collective-permute-start | bytes 36872 | tf_op jit(solution)/shard_map/ppermute | solution.py:128
  12.8 0.5 collective-permute-start.1
  13.3 0.7 broadcast_add_fusion
  14.0 1.3 fusion.15
  15.3 0.7 fusion.29
  16.0 1.9 %select_reduce_fusion.4 = (s32[1024]{0:T(1024)S(1)}, s32[1024]{0:T(1024)S(1)}) fusion(s32[1024]{0:T(1024)S(1)} %bitcast.42, s32[1024]{0:T(1024)S(1)} %fusion.29, s32[1024]{0:T(1024)} %bitcast.37), kind=kLoop, calls=%fused_computation.15 | loop fusion | flops 5240832 | bytes 20480 | tf_op jit(solution)/shard_map/reduce_sum | solution.py:95
  17.9 2.3 %convolution_convert_fusion.1 = bf16[1024,1024]{1,0:T(8,128)(2,1)S(1)} fusion(s32[1024]{0:T(1024)S(1)} %get-tuple-element.6, pred[1024]{0:T(1024)(128)(4,1)S(1)} %broadcast_compare_fusion.1, bf16[1,1,256,1024]{3,2,1,0:T(8,128)(2,1)} %param.8), kind=kOutput, calls=%fused_computation.25 | convolution fusion | flops 538443776 | bytes 2626560 | tf_op jit(solution)/shard_map/dot_general | solution.py:104
  20.3 0.5 fusion.14
  20.9 1.2 select_reduce_fusion.3
  22.1 19.3 %collective-permute-done.1 = bf16[256,1024]{1,0:T(8,128)(2,1)S(1)} collective-permute-done((bf16[256,1024]{1,0:T(8,128)(2,1)}, bf16[256,1024]{1,0:T(8,128)(2,1)S(1)}, u32[]{:S(2)}, u32[]{:S(2)}) %collective-permute-start.1) | collective-permute-done | bytes 524320 | tf_op jit(solution)/shard_map/ppermute | solution.py:127
  41.5 1.3 convolution_convert_fusion
  42.8 2.6 %pad_maximum_fusion = bf16[16,128,1024]{2,1,0:T(8,128)(2,1)} fusion(bf16[16,64,1024]{2,1,0:T(8,128)(2,1)S(1)} %bitcast.28, bf16[16,64,1024]{2,1,0:T(8,128)(2,1)S(1)} %bitcast.27), kind=kLoop, calls=%fused_computation.10 | loop fusion | flops 8388608 | bytes 8388608 | tf_op jit(solution)/shard_map/concatenate | solution.py:139
  45.4 7.1 %all-to-all-start = ((bf16[16,128,1024]{2,1,0:T(8,128)(2,1)}), bf16[16,128,1024]{2,1,0:T(8,128)(2,1)}, u32[]{:S(2)}, u32[]{:S(2)}) async-start(bf16[16,128,1024]{2,1,0:T(8,128)(2,1)} %pad_maximum_fusion), calls=%async_computation | async-start | bytes 8388608 | tf_op jit(solution)/shard_map/all_to_all | solution.py:140
  52.5 0.7 all-gather.3.cloned.1.call-update
  53.3 0.1 sub.33
  53.4 0.1 pad_add_fusion.1
  53.5 71.2 %all-gather = s32[256,128]{1,0:T(8,128)S(1)} all-gather(s32[16,128]{1,0:T(8,128)S(1)} %pad_add_fusion.1), channel_id=2, replica_groups=mesh['zh'=2,'xy'=16,'cand'=8] {'xy'}, dimensions={0}, use_global_device_ids=true | all-gather | bytes 139264 | tf_op jit(solution)/shard_map/all_gather | solution.py:136
  124.7 0.9 select_reduce_fusion
  125.7 8.7 %gather_fusion = bf16[1024,1024]{1,0:T(8,128)(2,1)} fusion(bf16[2048,1024]{1,0:T(8,128)(2,1)} %bitcast.17, s32[1024]{0:T(1024)S(1)} %broadcast_clamp_fusion), kind=kCustom, calls=%fused_computation | custom fusion | bytes 4198400 | tf_op jit(solution)/shard_map/jit(_take)/gather | solution.py:145
  134.4 2.3 %convert_reduce_fusion = (f32[1024]{0:T(1024)S(1)}, bf16[1024,1024]{1,0:T(8,128)(2,1)S(1)}) fusion(bf16[1024,1024]{1,0:T(8,128)(2,1)} %gather_fusion, pred[1024]{0:T(1024)(128)(4,1)S(1)} %compare_and_fusion), kind=kLoop, calls=%fused_computation.5 | loop fusion | flops 3144704 | bytes 4199424 | tf_op jit(solution)/shard_map/reduce_sum | solution.py:21
  136.7 0.7 fusion.2
  137.4 15.6 %multiply_convert_fusion.proj_ref = bf16[1024,4096]{1,0:T(8,128)(2,1)} fusion(bf16[1024,4096]{1,0:T(8,128)(2,1)} %param.14, bf16[1024,1024]{1,0:T(8,128)(2,1)S(1)} %get-tuple-element.10.rows_ref, f32[1024]{0:T(1024)S(1)} %add_rsqrt_fusion, f32[1024]{0:T(1024)S(1)} %broadcast_multiply_fusion), kind=kOutput, calls=%fused_computation.1 | convolution fusion | flops 8615100416 | bytes 18882560 | tf_op jit(solution)/shard_map/dot_general | solution.py:151
  153.0 20.9 %shard_map.82 = bf16[1024,1024]{1,0:T(8,128)(2,1)} custom-call(s32[8]{0:T(128)} %bitcast.48, bf16[1024,4096]{1,0:T(8,128)(2,1)} %multiply_convert_fusion.proj_ref, bf16[8,128,2048]{2,1,0:T(8,128)(2,1)} %bitcast.29, bf16[1024,1024]{1,0:T(8,128)(2,1)} %copy-done, bf16[1024,1024]{1,0:T(8,128)(2,1)} %wout_ref.1), custom_call_target="tpu_custom_call" | custom-call | flops 2684354560 | bytes 18874368 | tf_op jit(solution)/shard_map/pallas_call | solution.py:74
  (20 shorter events, 0.2 us)
Async XLA Ops:
  7.3 13.0 %collective-permute-start = (s32[3,1024]{1,0:T(4,128)S(1)}, s32[3,1024]{1,0:T(4,128)S(1)}, u32[]{:S(2)}, u32[]{:S(2)}) collective-permute-start(s32[3,1024]{1,0:T(4,128)S(1)} %pad_add_fusion), channel_id=1, source_target_pairs={{0,128},{128,0},{1,129},{129,1},{2,130},{130,2},{3,131},{131,3},{4... | collective-permute-start | bytes 36872 | tf_op jit(solution)/shard_map/ppermute | solution.py:128
  12.8 28.7 %collective-permute-start.1 = (bf16[256,1024]{1,0:T(8,128)(2,1)}, bf16[256,1024]{1,0:T(8,128)(2,1)S(1)}, u32[]{:S(2)}, u32[]{:S(2)}) collective-permute-start(bf16[256,1024]{1,0:T(8,128)(2,1)} %bitcast.30), channel_id=1, source_target_pairs={{0,128},{128,0},{1,129},{129,1},{2,130},{130,2},{3,131},{131,3},{4... | collective-permute-start | bytes 1572872 | tf_op jit(solution)/shard_map/ppermute | solution.py:127
  45.4 80.3 %all-to-all-start = ((bf16[16,128,1024]{2,1,0:T(8,128)(2,1)}), bf16[16,128,1024]{2,1,0:T(8,128)(2,1)}, u32[]{:S(2)}, u32[]{:S(2)}) async-start(bf16[16,128,1024]{2,1,0:T(8,128)(2,1)} %pad_maximum_fusion), calls=%async_computation | async-start | bytes 8388608 | tf_op jit(solution)/shard_map/all_to_all | solution.py:140
  52.5 100.6 %all-gather.3.cloned.1.call-start = ((), (), s32[]{:S(2)}) async-start(), calls=%async_computation.1 | async-start | bytes 4718592 | tf_op jit(solution)/shard_map/all_gather | solution.py:153
  136.7 16.4 %copy-start = (bf16[1024,1024]{1,0:T(8,128)(2,1)}, bf16[1024,1024]{1,0:T(8,128)(2,1)S(1)}, u32[]{:S(2)}) copy-start(bf16[1024,1024]{1,0:T(8,128)(2,1)S(1)} %get-tuple-element.10.rows_ref) | copy-start | bytes 6291460
Sparse Core Ops, SparseCore 0:
  55.1 50.2 all-gather.2

commit v4 on v3

--- a/solution.py
+++ b/solution.py
@@ -105,6 +105,12 @@
     return picked.reshape(rows.shape + (table.shape[1],))
 
 
+def place_rows(arrived, tags, slot_ids):
+    rows = arrived.reshape(-1, arrived.shape[-1])
+    one_hot = (slot_ids[:, None] == tags.reshape(-1)[None, :]).astype(rows.dtype)
+    return jnp.dot(one_hot, rows, preferred_element_type=jnp.float32)
+
+
 def shards(
     item_table,
     picked_items,
@@ -136,16 +142,16 @@
     every_slot = lax.all_gather(slots, "xy", axis=0, tiled=False)
     tags = lax.dynamic_index_in_dim(every_slot, lax.axis_index("xy"), axis=1, keepdims=False)
     tags = tags.reshape(-1)
-    outgoing = jnp.concatenate([own_data, far_data], axis=1)
-    arrived = lax.all_to_all(outgoing, "xy", split_axis=0, concat_axis=0, tiled=True)
-    arrived_rows = arrived.reshape(n_half * capacity, feature)
+    own_arrived = lax.all_to_all(own_data, "xy", split_axis=0, concat_axis=0, tiled=True)
+    far_arrived = lax.all_to_all(far_data, "xy", split_axis=0, concat_axis=0, tiled=True)
     slot_ids = jnp.arange(slot_count, dtype=jnp.int32)
-    order = jnp.arange(n_half * capacity, dtype=jnp.int32)
-    fill = jnp.sum(jnp.where(tags[None, :] == slot_ids[:, None], order[None, :], 0), axis=1)
-    arranged = jnp.take(arrived_rows, fill, axis=0)
+    tags = tags.reshape(n_half, 2, per_pair)
+    as_float = place_rows(own_arrived, tags[:, 0], slot_ids) + place_rows(
+        far_arrived, tags[:, 1], slot_ids
+    )
+    arranged = as_float.astype(jnp.bfloat16)
 
     lengths = history_length[0]
-    as_float = arranged.astype(jnp.float32)
     normed_in = layer_norm(as_float).astype(jnp.bfloat16)
     projected = jax.nn.silu(
         jnp.dot(normed_in, input_weight, preferred_element_type=jnp.float32)

time: 183 us -> 168 us (0.918)
  blocking collectives: 71.2 us -> 41.4 us
  waiting for transfers between devices: 20 us -> 34.8 us
  local copies, waits for them, and re-layouts: 8.9 us -> 0.47 us
  matrix products: 21.1 us -> 29.5 us
  starting transfers between devices: 13.1 us -> 20.1 us
  other arithmetic: 12 us -> 6.91 us
    all_gather x1, blocking collectives: 71.2 us -> 41.4 us  [shards(): every_slot = lax.all_gather(slots, 'xy', axis=0, tiled=False)]
    ppermute x1, waiting for transfers between devices: 19.3 us -> 33 us  [shards(): other_rows = lax.ppermute(item_rows, 'zh', swap)]
    dot_general x0 -> x2, matrix products: none -> 9.64 us  [place_rows(): return jnp.dot(one_hot, rows, preferred_element_type=jnp.float32)]
    gather x1 -> x0, local copies, waits for them, and re-layouts: 8.74 us -> none  [shards(): arranged = jnp.take(arrived_rows, fill, axis=0)]
    all_to_all x1 -> x2, starting transfers between devices: 7.09 us -> 14 us  [the longest x1 7.03 us: shards(): lax.all_to_all(own_data, 'xy', split_axis=0, concat_axis=0, tiled=True)]
    dot_general x1, matrix products: 15.6 us -> 12.5 us  [shards(): jnp.dot(normed_in, input_weight, preferred_element_type=jnp.float32)]
    concatenate x1 -> x0, other arithmetic: 2.64 us -> none  [shards(): outgoing = jnp.concatenate([own_data, far_data], axis=1)]
    reduce_sum x3 -> x1, other arithmetic: 3.87 us -> 1.24 us  [block_plan(): row = jnp.sum(jnp.where(hit, picks[None, :], 0), axis=1)]
  transfers between devices with their start and end apart: 4 -> 5, of which waited for: 1 -> 2; matrix products, arithmetic and copies ran while one was open for 21% -> 17% of each run, Pallas kernels for 0% -> 0%
where the time goes in v4:
time: 168 us
  blocking collectives  41.4 us (25%)
  waiting for transfers between devices  34.8 us (21%)
  matrix products  29.5 us (18%)
  Pallas kernels  20.9 us (12%)
  starting transfers between devices  20.1 us (12%)
  between operations  13.5 us (8%)
  other arithmetic  6.91 us (4%)
    all_gather x1, blocking collectives, shards(): every_slot = lax.all_gather(slots, 'xy', axis=0, tiled=False)  41.4 us
    ppermute x1, waiting for transfers between devices, shards(): other_rows = lax.ppermute(item_rows, 'zh', swap)  33 us
    pallas_call x1, Pallas kernels, tail(): pl.pallas_call(kern, grid_spec=spec, out_shape=jax.ShapeDtypeStruct((slot...  20.9 us
    dot_general x1, matrix products, shards(): jnp.dot(normed_in, input_weight, preferred_element_type=jnp.float32)  12.5 us
    dot_general x2, matrix products, place_rows(): return jnp.dot(one_hot, rows, preferred_element_type=jnp.float32)  9.64 us
    all_to_all x1, starting transfers between devices, shards(): lax.all_to_all(own_data, 'xy', split_axis=0, concat_axis=0, tiled=True)  7.03 us
    all_to_all x1, starting transfers between devices, shards(): lax.all_to_all(far_data, 'xy', split_axis=0, concat_axis=0, tiled=True)  6.99 us
    dot_general x2, matrix products, select_rows(): jnp.dot(one_hot, table, preferred_element_type=jnp.float32)  5.54 us
  transfers between devices with their start and end apart: 5, of which 2 were waited for; matrix products, arithmetic and copies ran while one was open for 17% of the time, Pallas kernels for 0%

profile of v4, /device:TPU:64, one launch (start us, length us, event | category | flops | bytes accessed | tf_op | source)
XLA Modules:
  0.0 167.6 jit_solution(3728900333534310230)
XLA Ops:
  6.5 1.4 fusion.13
  7.9 0.7 broadcast_add_fusion
  8.6 0.7 fusion.27
  9.3 1.9 %select_reduce_fusion.3 = (s32[1024]{0:T(1024)S(1)}, s32[1024]{0:T(1024)S(1)}) fusion(s32[1024]{0:T(1024)S(1)} %bitcast.42, s32[1024]{0:T(1024)S(1)} %fusion.27, s32[1024]{0:T(1024)} %bitcast.35), kind=kLoop, calls=%fused_computation.8 | loop fusion | flops 5240832 | bytes 20480 | tf_op jit(solution)/shard_map/reduce_sum | solution.py:95
  11.2 3.3 %convolution_convert_fusion.1 = bf16[1024,1024]{1,0:T(8,128)(2,1)} fusion(s32[1024]{0:T(1024)S(1)} %get-tuple-element.10, pred[1024]{0:T(1024)(128)(4,1)S(1)} %broadcast_compare_fusion.1, bf16[1,1,256,1024]{3,2,1,0:T(8,128)(2,1)} %param.8), kind=kOutput, calls=%fused_computation.23 | convolution fusion | flops 538443776 | bytes 2626560 | tf_op jit(solution)/shard_map/dot_general | solution.py:104
  14.5 7.0 %all-to-all-start = ((bf16[16,64,1024]{2,1,0:T(8,128)(2,1)}), bf16[16,64,1024]{2,1,0:T(8,128)(2,1)S(1)}, u32[]{:S(2)}, u32[]{:S(2)}) async-start(bf16[16,64,1024]{2,1,0:T(8,128)(2,1)} %bitcast.13), calls=%async_computation | async-start | bytes 4194304 | tf_op jit(solution)/shard_map/all_to_all | solution.py:145
  21.7 5.5 %collective-permute-start = (s32[3,1024]{1,0:T(4,128)S(1)}, s32[3,1024]{1,0:T(4,128)S(1)}, u32[]{:S(2)}, u32[]{:S(2)}) collective-permute-start(s32[3,1024]{1,0:T(4,128)S(1)} %pad_add_fusion), channel_id=1, source_target_pairs={{0,128},{128,0},{1,129},{129,1},{2,130},{130,2},{3,131},{131,3},{4... | collective-permute-start | bytes 36872 | tf_op jit(solution)/shard_map/ppermute | solution.py:134
  27.2 0.5 collective-permute-start.1
  27.7 1.8 %collective-permute-done = s32[3,1024]{1,0:T(4,128)S(1)} collective-permute-done((s32[3,1024]{1,0:T(4,128)S(1)}, s32[3,1024]{1,0:T(4,128)S(1)}, u32[]{:S(2)}, u32[]{:S(2)}) %collective-permute-start) | collective-permute-done | bytes 12320 | tf_op jit(solution)/shard_map/ppermute | solution.py:134
  29.5 0.5 fusion.12
  30.1 1.2 select_reduce_fusion
  31.4 33.0 %collective-permute-done.1 = bf16[256,1024]{1,0:T(8,128)(2,1)S(1)} collective-permute-done((bf16[256,1024]{1,0:T(8,128)(2,1)S(1)}, bf16[256,1024]{1,0:T(8,128)(2,1)S(1)}, u32[]{:S(2)}, u32[]{:S(2)}) %collective-permute-start.1) | collective-permute-done | bytes 524320 | tf_op jit(solution)/shard_map/ppermute | solution.py:133
  64.3 2.2 %convolution_convert_fusion = bf16[1024,1024]{1,0:T(8,128)(2,1)} fusion(bf16[256,1024]{1,0:T(8,128)(2,1)S(1)} %collective-permute-done.1, s32[1024]{0:T(1024)S(1)} %get-tuple-element.7, pred[1024]{0:T(1024)(128)(4,1)S(1)} %broadcast_compare_fusion), kind=kOutput, calls=%fused_computation.22 | convolution fusion | flops 538443776 | bytes 2626560 | tf_op jit(solution)/shard_map/dot_general | solution.py:104
  66.6 7.0 %all-to-all-start.1 = ((bf16[16,64,1024]{2,1,0:T(8,128)(2,1)}), bf16[16,64,1024]{2,1,0:T(8,128)(2,1)}, u32[]{:S(2)}, u32[]{:S(2)}) async-start(bf16[16,64,1024]{2,1,0:T(8,128)(2,1)} %bitcast.16), calls=%async_computation.1 | async-start | bytes 4194304 | tf_op jit(solution)/shard_map/all_to_all | solution.py:146
  73.6 0.1 sub.30
  73.7 0.1 sub.33
  73.7 0.1 pad_add_fusion.1
  73.8 41.4 %all-gather = s32[256,128]{1,0:T(8,128)S(1)} all-gather(s32[16,128]{1,0:T(8,128)S(1)} %pad_add_fusion.1), channel_id=2, replica_groups=mesh['zh'=2,'xy'=16,'cand'=8] {'xy'}, dimensions={0}, use_global_device_ids=true | all-gather | bytes 139264 | tf_op jit(solution)/shard_map/all_gather | solution.py:142
  115.2 0.1 reshape_reshape.3
  115.5 4.3 %fusion.2 = f32[1024,1024]{1,0:T(8,128)} fusion(bf16[1024,1024]{1,0:T(8,128)(2,1)S(1)} %bitcast.28, s32[1024]{0:T(1024)S(1)} %eq.156), kind=kOutput, calls=%fused_computation.14 | convolution fusion | flops 2148532224 | bytes 6295552 | tf_op jit(solution)/shard_map/dot_general | solution.py:111
  119.8 5.4 %fusion.34 = (f32[1024]{0:T(1024)S(1)}, f32[1024,1024]{1,0:T(8,128)S(1)}) fusion(f32[1024,1024]{1,0:T(8,128)} %fusion.2, bf16[1024,1024]{1,0:T(8,128)(2,1)} %bitcast.17, s32[1024]{0:T(1024)S(1)} %eq.163), kind=kOutput, calls=%fused_computation.75 | convolution fusion | flops 2150628352 | bytes 10493952 | tf_op jit(solution)/shard_map/dot_general | solution.py:111
  125.2 2.2 %fusion.33 = (bf16[1024,1024]{1,0:T(8,128)(2,1)}, f32[1024]{0:T(1024)S(1)}) fusion(f32[1024,1024]{1,0:T(8,128)S(1)} %get-tuple-element.17, f32[1024]{0:T(1024)S(1)} %broadcast_multiply_fusion), kind=kLoop, calls=%fused_computation.74 | loop fusion | flops 4193280 | bytes 6299648 | tf_op jit(solution)/shard_map/convert_element_type | solution.py:152
  127.4 12.5 %multiply_convert_fusion.proj_ref = bf16[1024,4096]{1,0:T(8,128)(2,1)} fusion(bf16[1024,4096]{1,0:T(8,128)(2,1)S(1)} %bitcast.46, f32[1024,1024]{1,0:T(8,128)S(1)} %get-tuple-element.17, f32[1024]{0:T(1024)S(1)} %add_rsqrt_fusion, f32[1024]{0:T(1024)S(1)} %broadcast_multiply_fusion), kind=kOutput, calls=%fused_computation | convolution fusion | flops 8614051840 | bytes 20979712 | tf_op jit(solution)/shard_map/dot_general | solution.py:157
  139.8 20.9 %shard_map.82 = bf16[1024,1024]{1,0:T(8,128)(2,1)} custom-call(s32[8]{0:T(128)} %bitcast.44, bf16[1024,4096]{1,0:T(8,128)(2,1)} %multiply_convert_fusion.proj_ref, bf16[8,128,2048]{2,1,0:T(8,128)(2,1)} %bitcast.27, bf16[1024,1024]{1,0:T(8,128)(2,1)} %get-tuple-element.11.rows_ref, bf16[1024,1024]{1,0:T(8,128)(2,1)} %wout_ref.1), custom_call_target="tpu_custom_call" | custom-call | flops 2684354560 | bytes 18874368 | tf_op jit(solution)/shard_map/pallas_call | solution.py:74
  (32 shorter events, 0.4 us)
Async XLA Ops:
  6.5 15.1 %copy-start.1 = (s32[1,1,1024]{2,1,0:T(1,128)S(1)}, s32[1,1,1024]{2,1,0:T(1,128)}, u32[]{:S(2)}) copy-start(s32[1,1,1024]{2,1,0:T(1,128)} %param.10) | copy-start | bytes 12292
  6.5 15.1 %copy-start.3 = (s32[1,1,1024]{2,1,0:T(1,128)S(1)}, s32[1,1,1024]{2,1,0:T(1,128)}, u32[]{:S(2)}) copy-start(s32[1,1,1024]{2,1,0:T(1,128)} %param.11) | copy-start | bytes 12292
  6.5 15.1 %copy-start.2 = (s32[1,1,1024]{2,1,0:T(1,128)S(1)}, s32[1,1,1024]{2,1,0:T(1,128)}, u32[]{:S(2)}) copy-start(s32[1,1,1024]{2,1,0:T(1,128)} %param.9) | copy-start | bytes 12292
  6.5 20.6 %copy-start = (bf16[1,1,256,1024]{3,2,1,0:T(8,128)(2,1)S(1)}, bf16[1,1,256,1024]{3,2,1,0:T(8,128)(2,1)}, u32[]{:S(2)}) copy-start(bf16[1,1,256,1024]{3,2,1,0:T(8,128)(2,1)} %param.8) | copy-start | bytes 1572868
  14.5 52.0 %all-to-all-start = ((bf16[16,64,1024]{2,1,0:T(8,128)(2,1)}), bf16[16,64,1024]{2,1,0:T(8,128)(2,1)S(1)}, u32[]{:S(2)}, u32[]{:S(2)}) async-start(bf16[16,64,1024]{2,1,0:T(8,128)(2,1)} %bitcast.13), calls=%async_computation | async-start | bytes 4194304 | tf_op jit(solution)/shard_map/all_to_all | solution.py:145
  21.6 118.3 %all-gather.3.cloned.1.call-start = ((), (), s32[]{:S(2)}) async-start(), calls=%async_computation.2 | async-start | bytes 4718592 | tf_op jit(solution)/shard_map/all_gather | solution.py:159
  21.7 7.8 %collective-permute-start = (s32[3,1024]{1,0:T(4,128)S(1)}, s32[3,1024]{1,0:T(4,128)S(1)}, u32[]{:S(2)}, u32[]{:S(2)}) collective-permute-start(s32[3,1024]{1,0:T(4,128)S(1)} %pad_add_fusion), channel_id=1, source_target_pairs={{0,128},{128,0},{1,129},{129,1},{2,130},{130,2},{3,131},{131,3},{4... | collective-permute-start | bytes 36872 | tf_op jit(solution)/shard_map/ppermute | solution.py:134
  27.2 37.2 %collective-permute-start.1 = (bf16[256,1024]{1,0:T(8,128)(2,1)S(1)}, bf16[256,1024]{1,0:T(8,128)(2,1)S(1)}, u32[]{:S(2)}, u32[]{:S(2)}) collective-permute-start(bf16[256,1024]{1,0:T(8,128)(2,1)S(1)} %bitcast.29), channel_id=1, source_target_pairs={{0,128},{128,0},{1,129},{129,1},{2,130},{130,2},{3,131},{131,3},{4... | collective-permute-start | bytes 1572872 | tf_op jit(solution)/shard_map/ppermute | solution.py:133
  66.6 53.2 %all-to-all-start.1 = ((bf16[16,64,1024]{2,1,0:T(8,128)(2,1)}), bf16[16,64,1024]{2,1,0:T(8,128)(2,1)}, u32[]{:S(2)}, u32[]{:S(2)}) async-start(bf16[16,64,1024]{2,1,0:T(8,128)(2,1)} %bitcast.16), calls=%async_computation.1 | async-start | bytes 4194304 | tf_op jit(solution)/shard_map/all_to_all | solution.py:146
  119.8 7.6 %slice-start = ((s8[8388608]{0:T(1024)(128)(4,1)}), s8[4194304]{0:T(1024)(128)(4,1)S(1)}, s32[]{:S(2)}) async-start(s8[8388608]{0:T(1024)(128)(4,1)} %bitcast.45), calls=%async_computation.3 | async-start | bytes 8388608
  119.8 7.6 %slice-start.1 = ((s8[8388608]{0:T(1024)(128)(4,1)}), s8[4194304]{0:T(1024)(128)(4,1)S(1)}, s32[]{:S(2)}) async-start(s8[8388608]{0:T(1024)(128)(4,1)} %bitcast.45), calls=%async_computation.4 | async-start | bytes 8388608
Sparse Core Ops, SparseCore 0:
  27.9 63.8 all-gather.2

commit v5 on v4

--- a/solution.py
+++ b/solution.py
@@ -28,26 +28,29 @@
     return v / (1.0 + jnp.exp(-v))
 
 def tail_kernel(len_ref, proj_ref, cache_ref, rows_ref, wout_ref, out_ref, att_ref, *, heads, eps):
-    b = pl.program_id(0)
+    step = pl.program_id(0)
+    group, hist, doubled = cache_ref.shape
+    per = rows_ref.shape[0] // group
     feature = rows_ref.shape[1]
     head_width = feature // heads
-    hist = cache_ref.shape[1]
     scale = 1.0 / math.sqrt(head_width)
-    length = len_ref[b]
-    length_plus = length.astype(jnp.float32) + 1.0
-    valid = lax.broadcasted_iota(jnp.int32, (1, hist), 1) < length
-    for h in range(heads):
-        lo = h * head_width
-        q = proj_ref[:, 2 * feature + lo : 2 * feature + lo + head_width]
-        k = cache_ref[0, :, lo : lo + head_width]
-        v = cache_ref[0, :, feature + lo : feature + lo + head_width]
-        s = lax.dot_general(q, k, (((1,), (1,)), ((), ())), preferred_element_type=jnp.float32) * scale
-        w = jnp.where(valid, silu(s) / length_plus, 0.0).astype(jnp.bfloat16)
-        found = jnp.dot(w, v, preferred_element_type=jnp.float32)
-        own_k = proj_ref[:, 3 * feature + lo : 3 * feature + lo + head_width].astype(jnp.float32)
-        own_v = proj_ref[:, feature + lo : feature + lo + head_width].astype(jnp.float32)
-        own_s = jnp.sum(q.astype(jnp.float32) * own_k, axis=-1, keepdims=True) * scale
-        att_ref[:, lo : lo + head_width] = found + (silu(own_s) / length_plus) * own_v
+    for member in range(group):
+        length = len_ref[step * group + member]
+        inverse = 1.0 / (length.astype(jnp.float32) + 1.0)
+        valid = lax.broadcasted_iota(jnp.int32, (1, hist), 1) < length
+        rows = pl.ds(member * per, per)
+        for h in range(heads):
+            lo = h * head_width
+            q = proj_ref[rows, 2 * feature + lo : 2 * feature + lo + head_width]
+            k = cache_ref[member, :, lo : lo + head_width]
+            v = cache_ref[member, :, feature + lo : feature + lo + head_width]
+            s = lax.dot_general(q, k, (((1,), (1,)), ((), ())), preferred_element_type=jnp.float32) * scale
+            w = jnp.where(valid, silu(s) * inverse, 0.0).astype(jnp.bfloat16)
+            found = jnp.dot(w, v, preferred_element_type=jnp.float32)
+            own_k = proj_ref[rows, 3 * feature + lo : 3 * feature + lo + head_width].astype(jnp.float32)
+            own_v = proj_ref[rows, feature + lo : feature + lo + head_width].astype(jnp.float32)
+            own_s = jnp.sum(q.astype(jnp.float32) * own_k, axis=-1, keepdims=True) * scale
+            att_ref[rows, lo : lo + head_width] = found + (silu(own_s) * inverse) * own_v
     att = att_ref[...]
     mean = jnp.mean(att, axis=-1, keepdims=True)
     centred = att - mean
@@ -57,16 +60,16 @@
     update = jnp.dot(gated, wout_ref[...], preferred_element_type=jnp.float32)
     out_ref[...] = (rows_ref[...].astype(jnp.float32) + update).astype(out_ref.dtype)
 
-def tail(lengths, projected, cache, rows, wout, heads=8, eps=1e-6):
+def tail(lengths, projected, cache, rows, wout, heads=8, eps=1e-6, group=2):
     members, hist, doubled = cache.shape
     slots, feature = rows.shape
-    per = slots // members
+    per = slots // members * group
     width = projected.shape[1]
     kern = functools.partial(tail_kernel, heads=heads, eps=eps)
     spec = pltpu.PrefetchScalarGridSpec(
-        num_scalar_prefetch=1, grid=(members,),
+        num_scalar_prefetch=1, grid=(members // group,),
         in_specs=[pl.BlockSpec((per, width), lambda b, n: (b, 0)),
-                  pl.BlockSpec((1, hist, doubled), lambda b, n: (b, 0, 0)),
+                  pl.BlockSpec((group, hist, doubled), lambda b, n: (b, 0, 0)),
                   pl.BlockSpec((per, feature), lambda b, n: (b, 0)),
                   pl.BlockSpec((feature, feature), lambda b, n: (0, 0))],
         out_specs=pl.BlockSpec((per, feature), lambda b, n: (b, 0)),
@@ -143,6 +146,7 @@
     tags = lax.dynamic_index_in_dim(every_slot, lax.axis_index("xy"), axis=1, keepdims=False)
     tags = tags.reshape(-1)
     own_arrived = lax.all_to_all(own_data, "xy", split_axis=0, concat_axis=0, tiled=True)
+    tags, far_data = lax.optimization_barrier((tags, far_data))
     far_arrived = lax.all_to_all(far_data, "xy", split_axis=0, concat_axis=0, tiled=True)
     slot_ids = jnp.arange(slot_count, dtype=jnp.int32)
     tags = tags.reshape(n_half, 2, per_pair)

time: 168 us -> 149 us (0.89)
  waiting for transfers between devices: 34.8 us -> 24.9 us
  blocking collectives: 41.4 us -> 34.2 us
    ppermute x1, waiting for transfers between devices: 33 us -> 0.01 us  [shards(): other_rows = lax.ppermute(item_rows, 'zh', swap)]
    all_to_all x1, waiting for transfers between devices: 0.01 us -> 23.2 us  [shards(): lax.all_to_all(far_data, 'xy', split_axis=0, concat_axis=0, tiled=True)]
    all_gather x1, blocking collectives: 41.4 us -> 34.2 us  [shards(): every_slot = lax.all_gather(slots, 'xy', axis=0, tiled=False)]
  transfers between devices with their start and end apart: 5 -> 5, of which waited for: 2 -> 2; matrix products, arithmetic and copies ran while one was open for 17% -> 20% of each run, Pallas kernels for 0% -> 0%
where the time goes in v5:
time: 149 us; the launch traced here: 148 us
  blocking collectives  34.2 us (23%)
  matrix products  29.6 us (20%)
  waiting for transfers between devices  24.9 us (17%)
  Pallas kernels  20 us (13%)
  starting transfers between devices  18.7 us (13%)
  between operations  13.5 us (9%)
  other arithmetic  6.91 us (5%)
    all_gather x1, blocking collectives, shards(): every_slot = lax.all_gather(slots, 'xy', axis=0, tiled=False)  34.2 us
    all_to_all x1, waiting for transfers between devices, shards(): lax.all_to_all(far_data, 'xy', split_axis=0, concat_axis=0, tiled=True)  23.2 us
    pallas_call x1, Pallas kernels, tail(): pl.pallas_call(kern, grid_spec=spec, out_shape=jax.ShapeDtypeStruct((slot...  20 us
    dot_general x1, matrix products, shards(): jnp.dot(normed_in, input_weight, preferred_element_type=jnp.float32)  12.5 us
    dot_general x2, matrix products, place_rows(): return jnp.dot(one_hot, rows, preferred_element_type=jnp.float32)  9.64 us
    all_to_all x1, starting transfers between devices, shards(): lax.all_to_all(own_data, 'xy', split_axis=0, concat_axis=0, tiled=True)  7.03 us
    all_to_all x1, starting transfers between devices, shards(): lax.all_to_all(far_data, 'xy', split_axis=0, concat_axis=0, tiled=True)  5.56 us
    dot_general x2, matrix products, select_rows(): jnp.dot(one_hot, table, preferred_element_type=jnp.float32)  5.55 us
  transfers between devices with their start and end apart: 5, of which 2 were waited for; matrix products, arithmetic and copies ran while one was open for 20% of the time, Pallas kernels for 0%

profile of v5, /device:TPU:64, one launch (start us, length us, event | category | flops | bytes accessed | tf_op | source)
XLA Modules:
  0.0 148.3 jit_solution(233466179023781530)
XLA Ops:
  6.5 1.4 fusion.13
  7.9 0.7 broadcast_add_fusion
  8.6 0.7 fusion.27
  9.3 1.9 %select_reduce_fusion.3 = (s32[1024]{0:T(1024)S(1)}, s32[1024]{0:T(1024)S(1)}) fusion(s32[1024]{0:T(1024)S(1)} %bitcast.44, s32[1024]{0:T(1024)S(1)} %fusion.27, s32[1024]{0:T(1024)} %bitcast.37), kind=kLoop, calls=%fused_computation.8 | loop fusion | flops 5240832 | bytes 20480 | tf_op jit(solution)/shard_map/reduce_sum | solution.py:98
  11.2 3.3 %convolution_convert_fusion = bf16[1024,1024]{1,0:T(8,128)(2,1)} fusion(s32[1024]{0:T(1024)S(1)} %get-tuple-element.14, pred[1024]{0:T(1024)(128)(4,1)S(1)} %broadcast_compare_fusion, bf16[1,1,256,1024]{3,2,1,0:T(8,128)(2,1)} %param.8), kind=kOutput, calls=%fused_computation.22 | convolution fusion | flops 538443776 | bytes 2626560 | tf_op jit(solution)/shard_map/dot_general | solution.py:107
  14.5 7.0 %all-to-all-start = ((bf16[16,64,1024]{2,1,0:T(8,128)(2,1)}), bf16[16,64,1024]{2,1,0:T(8,128)(2,1)S(1)}, u32[]{:S(2)}, u32[]{:S(2)}) async-start(bf16[16,64,1024]{2,1,0:T(8,128)(2,1)} %bitcast.16), calls=%async_computation | async-start | bytes 4194304 | tf_op jit(solution)/shard_map/all_to_all | solution.py:148
  21.7 5.5 %collective-permute-start = (s32[3,1024]{1,0:T(4,128)S(1)}, s32[3,1024]{1,0:T(4,128)S(1)}, u32[]{:S(2)}, u32[]{:S(2)}) collective-permute-start(s32[3,1024]{1,0:T(4,128)S(1)} %pad_add_fusion), channel_id=1, source_target_pairs={{0,128},{128,0},{1,129},{129,1},{2,130},{130,2},{3,131},{131,3},{4... | collective-permute-start | bytes 36872 | tf_op jit(solution)/shard_map/ppermute | solution.py:137
  27.2 0.5 collective-permute-start.1
  27.7 0.1 sub.30
  27.8 1.7 %collective-permute-done = s32[3,1024]{1,0:T(4,128)S(1)} collective-permute-done((s32[3,1024]{1,0:T(4,128)S(1)}, s32[3,1024]{1,0:T(4,128)S(1)}, u32[]{:S(2)}, u32[]{:S(2)}) %collective-permute-start) | collective-permute-done | bytes 12320 | tf_op jit(solution)/shard_map/ppermute | solution.py:137
  29.5 0.5 fusion.12
  30.1 1.2 select_reduce_fusion.1
  31.4 0.1 sub.33
  31.4 0.1 pad_add_fusion.1
  31.5 34.2 %all-gather = s32[256,128]{1,0:T(8,128)S(1)} all-gather(s32[16,128]{1,0:T(8,128)S(1)} %pad_add_fusion.1), channel_id=2, replica_groups=mesh['zh'=2,'xy'=16,'cand'=8] {'xy'}, dimensions={0}, use_global_device_ids=true | all-gather | bytes 139264 | tf_op jit(solution)/shard_map/all_gather | solution.py:145
  65.8 2.3 %convolution_convert_fusion.1 = bf16[1024,1024]{1,0:T(8,128)(2,1)} fusion(bf16[256,1024]{1,0:T(8,128)(2,1)S(1)} %collective-permute-done.1, s32[1024]{0:T(1024)S(1)} %get-tuple-element.11, pred[1024]{0:T(1024)(128)(4,1)S(1)} %broadcast_compare_fusion.1), kind=kOutput, calls=%fused_computation.23 | convolution fusion | flops 538443776 | bytes 2626560 | tf_op jit(solution)/shard_map/dot_general | solution.py:107
  68.0 5.6 %all-to-all-start.1 = ((bf16[16,64,1024]{2,1,0:T(8,128)(2,1)}), bf16[16,64,1024]{2,1,0:T(8,128)(2,1)}, u32[]{:S(2)}, u32[]{:S(2)}) async-start(bf16[16,64,1024]{2,1,0:T(8,128)(2,1)} %bitcast.14), calls=%async_computation.1 | async-start | bytes 4194304 | tf_op jit(solution)/shard_map/all_to_all | solution.py:150
  73.6 0.1 reshape.128
  73.9 4.3 %fusion.2 = f32[1024,1024]{1,0:T(8,128)} fusion(bf16[1024,1024]{1,0:T(8,128)(2,1)S(1)} %bitcast.29, s32[1024]{0:T(1024)S(1)} %eq.159), kind=kOutput, calls=%fused_computation.14 | convolution fusion | flops 2148532224 | bytes 6295552 | tf_op jit(solution)/shard_map/dot_general | solution.py:114
  78.1 23.2 %all-to-all-done.1 = bf16[16,64,1024]{2,1,0:T(8,128)(2,1)} async-done(((bf16[16,64,1024]{2,1,0:T(8,128)(2,1)}), bf16[16,64,1024]{2,1,0:T(8,128)(2,1)}, u32[]{:S(2)}, u32[]{:S(2)}) %all-to-all-start.1) | async-done | bytes 2097184 | tf_op jit(solution)/shard_map/all_to_all | solution.py:150
  101.3 5.4 %fusion.34 = (f32[1024]{0:T(1024)S(1)}, f32[1024,1024]{1,0:T(8,128)S(1)}) fusion(f32[1024,1024]{1,0:T(8,128)} %fusion.2, bf16[1024,1024]{1,0:T(8,128)(2,1)} %bitcast.18, s32[1024]{0:T(1024)S(1)} %eq.166), kind=kOutput, calls=%fused_computation.75 | convolution fusion | flops 2150628352 | bytes 10493952 | tf_op jit(solution)/shard_map/dot_general | solution.py:114
  106.7 2.2 %fusion.33 = (bf16[1024,1024]{1,0:T(8,128)(2,1)}, f32[1024]{0:T(1024)S(1)}) fusion(f32[1024,1024]{1,0:T(8,128)S(1)} %get-tuple-element.21, f32[1024]{0:T(1024)S(1)} %broadcast_multiply_fusion), kind=kLoop, calls=%fused_computation.74 | loop fusion | flops 4193280 | bytes 6299648 | tf_op jit(solution)/shard_map/convert_element_type | solution.py:156
  108.9 12.5 %multiply_convert_fusion.proj_ref = bf16[1024,4096]{1,0:T(8,128)(2,1)} fusion(bf16[1024,4096]{1,0:T(8,128)(2,1)S(1)} %bitcast.48, f32[1024,1024]{1,0:T(8,128)S(1)} %get-tuple-element.21, f32[1024]{0:T(1024)S(1)} %add_rsqrt_fusion, f32[1024]{0:T(1024)S(1)} %broadcast_multiply_fusion), kind=kOutput, calls=%fused_computation | convolution fusion | flops 8614051840 | bytes 20979712 | tf_op jit(solution)/shard_map/dot_general | solution.py:161
  121.4 20.0 %shard_map.82 = bf16[1024,1024]{1,0:T(8,128)(2,1)} custom-call(s32[8]{0:T(128)} %bitcast.46, bf16[1024,4096]{1,0:T(8,128)(2,1)} %multiply_convert_fusion.proj_ref, bf16[8,128,2048]{2,1,0:T(8,128)(2,1)} %bitcast.28, bf16[1024,1024]{1,0:T(8,128)(2,1)} %get-tuple-element.15.rows_ref, bf16[1024,1024]{1,0:T(8,128)(2,1)} %wout_ref.1), custom_call_target="tpu_custom_call" | custom-call | flops 2684354560 | bytes 18874368 | tf_op jit(solution)/shard_map/pallas_call | solution.py:77
  (32 shorter events, 0.4 us)
Async XLA Ops:
  6.5 15.1 %copy-start.1 = (s32[1,1,1024]{2,1,0:T(1,128)S(1)}, s32[1,1,1024]{2,1,0:T(1,128)}, u32[]{:S(2)}) copy-start(s32[1,1,1024]{2,1,0:T(1,128)} %param.10) | copy-start | bytes 12292
  6.5 15.1 %copy-start.3 = (s32[1,1,1024]{2,1,0:T(1,128)S(1)}, s32[1,1,1024]{2,1,0:T(1,128)}, u32[]{:S(2)}) copy-start(s32[1,1,1024]{2,1,0:T(1,128)} %param.11) | copy-start | bytes 12292
  6.5 15.1 %copy-start.2 = (s32[1,1,1024]{2,1,0:T(1,128)S(1)}, s32[1,1,1024]{2,1,0:T(1,128)}, u32[]{:S(2)}) copy-start(s32[1,1,1024]{2,1,0:T(1,128)} %param.9) | copy-start | bytes 12292
  6.5 20.6 %copy-start = (bf16[1,1,256,1024]{3,2,1,0:T(8,128)(2,1)S(1)}, bf16[1,1,256,1024]{3,2,1,0:T(8,128)(2,1)}, u32[]{:S(2)}) copy-start(bf16[1,1,256,1024]{3,2,1,0:T(8,128)(2,1)} %param.8) | copy-start | bytes 1572868
  14.5 53.5 %all-to-all-start = ((bf16[16,64,1024]{2,1,0:T(8,128)(2,1)}), bf16[16,64,1024]{2,1,0:T(8,128)(2,1)S(1)}, u32[]{:S(2)}, u32[]{:S(2)}) async-start(bf16[16,64,1024]{2,1,0:T(8,128)(2,1)} %bitcast.16), calls=%async_computation | async-start | bytes 4194304 | tf_op jit(solution)/shard_map/all_to_all | solution.py:148
  21.6 99.8 %all-gather.3.cloned.1.call-start = ((), (), s32[]{:S(2)}) async-start(), calls=%async_computation.2 | async-start | bytes 4718592 | tf_op jit(solution)/shard_map/all_gather | solution.py:163
  21.7 7.8 %collective-permute-start = (s32[3,1024]{1,0:T(4,128)S(1)}, s32[3,1024]{1,0:T(4,128)S(1)}, u32[]{:S(2)}, u32[]{:S(2)}) collective-permute-start(s32[3,1024]{1,0:T(4,128)S(1)} %pad_add_fusion), channel_id=1, source_target_pairs={{0,128},{128,0},{1,129},{129,1},{2,130},{130,2},{3,131},{131,3},{4... | collective-permute-start | bytes 36872 | tf_op jit(solution)/shard_map/ppermute | solution.py:137
  27.2 38.6 %collective-permute-start.1 = (bf16[256,1024]{1,0:T(8,128)(2,1)S(1)}, bf16[256,1024]{1,0:T(8,128)(2,1)S(1)}, u32[]{:S(2)}, u32[]{:S(2)}) collective-permute-start(bf16[256,1024]{1,0:T(8,128)(2,1)S(1)} %bitcast.30), channel_id=1, source_target_pairs={{0,128},{128,0},{1,129},{129,1},{2,130},{130,2},{3,131},{131,3},{4... | collective-permute-start | bytes 1572872 | tf_op jit(solution)/shard_map/ppermute | solution.py:136
  68.0 33.3 %all-to-all-start.1 = ((bf16[16,64,1024]{2,1,0:T(8,128)(2,1)}), bf16[16,64,1024]{2,1,0:T(8,128)(2,1)}, u32[]{:S(2)}, u32[]{:S(2)}) async-start(bf16[16,64,1024]{2,1,0:T(8,128)(2,1)} %bitcast.14), calls=%async_computation.1 | async-start | bytes 4194304 | tf_op jit(solution)/shard_map/all_to_all | solution.py:150
  101.3 7.6 %slice-start = ((s8[8388608]{0:T(1024)(128)(4,1)}), s8[4194304]{0:T(1024)(128)(4,1)S(1)}, s32[]{:S(2)}) async-start(s8[8388608]{0:T(1024)(128)(4,1)} %bitcast.47), calls=%async_computation.3 | async-start | bytes 8388608
  101.3 7.6 %slice-start.1 = ((s8[8388608]{0:T(1024)(128)(4,1)}), s8[4194304]{0:T(1024)(128)(4,1)S(1)}, s32[]{:S(2)}) async-start(s8[8388608]{0:T(1024)(128)(4,1)} %bitcast.47), calls=%async_computation.4 | async-start | bytes 8388608
Sparse Core Ops, SparseCore 0:
  27.8 63.8 all-gather.2

commit v6 on v5

--- a/solution.py
+++ b/solution.py
@@ -25,7 +25,7 @@
 
 
 def silu(v):
-    return v / (1.0 + jnp.exp(-v))
+    return v * (0.5 + 0.5 * jnp.tanh(0.5 * v))
 
 def tail_kernel(len_ref, proj_ref, cache_ref, rows_ref, wout_ref, out_ref, att_ref, *, heads, eps):
     step = pl.program_id(0)
@@ -108,10 +108,23 @@
     return picked.reshape(rows.shape + (table.shape[1],))
 
 
-def place_rows(arrived, tags, slot_ids):
+RADIX = 32
+TAG_LANES = 128
+
+
+def with_tags(data, slots):
+    high = jnp.floor_divide(slots, RADIX)
+    low = slots - high * RADIX
+    lane = lax.broadcasted_iota(jnp.int32, slots.shape + (TAG_LANES,), 2)
+    tags = jnp.where(lane == 0, high[..., None], jnp.where(lane == 1, low[..., None], 0))
+    return jnp.concatenate([data, tags.astype(data.dtype)], axis=-1)
+
+
+def place_rows(arrived, slot_ids, feature):
     rows = arrived.reshape(-1, arrived.shape[-1])
-    one_hot = (slot_ids[:, None] == tags.reshape(-1)[None, :]).astype(rows.dtype)
-    return jnp.dot(one_hot, rows, preferred_element_type=jnp.float32)
+    tags = rows[:, feature].astype(jnp.int32) * RADIX + rows[:, feature + 1].astype(jnp.int32)
+    one_hot = (slot_ids[:, None] == tags[None, :]).astype(rows.dtype)
+    return jnp.dot(one_hot, rows[:, :feature], preferred_element_type=jnp.float32)
 
 
 def shards(
@@ -140,18 +153,15 @@
     far_row, far_slot = block_plan(other_ints, half, n_half, per_pair, sources)
     own_data = select_rows(item_rows, own_row, own_slot)
     far_data = select_rows(other_rows, far_row, far_slot)
-    slots = jnp.concatenate([own_slot, far_slot], axis=1)
-    capacity = 2 * per_pair
-    every_slot = lax.all_gather(slots, "xy", axis=0, tiled=False)
-    tags = lax.dynamic_index_in_dim(every_slot, lax.axis_index("xy"), axis=1, keepdims=False)
-    tags = tags.reshape(-1)
-    own_arrived = lax.all_to_all(own_data, "xy", split_axis=0, concat_axis=0, tiled=True)
-    tags, far_data = lax.optimization_barrier((tags, far_data))
-    far_arrived = lax.all_to_all(far_data, "xy", split_axis=0, concat_axis=0, tiled=True)
+    own_arrived = lax.all_to_all(
+        with_tags(own_data, own_slot), "xy", split_axis=0, concat_axis=0, tiled=True
+    )
+    far_arrived = lax.all_to_all(
+        with_tags(far_data, far_slot), "xy", split_axis=0, concat_axis=0, tiled=True
+    )
     slot_ids = jnp.arange(slot_count, dtype=jnp.int32)
-    tags = tags.reshape(n_half, 2, per_pair)
-    as_float = place_rows(own_arrived, tags[:, 0], slot_ids) + place_rows(
-        far_arrived, tags[:, 1], slot_ids
+    as_float = place_rows(own_arrived, slot_ids, feature) + place_rows(
+        far_arrived, slot_ids, feature
     )
     arranged = as_float.astype(jnp.bfloat16)
 

time: 149 us -> 159 us (1.067)
  waiting for transfers between devices: 24.9 us -> 62.5 us
  blocking collectives: 34.2 us -> 0 us
  other arithmetic: 6.91 us -> 13.5 us
    ppermute x1, waiting for transfers between devices: 0.01 us -> 36.6 us  [shards(): other_rows = lax.ppermute(item_rows, 'zh', swap)]
    all_gather x1 -> x0, blocking collectives: 34.2 us -> none  [shards(): every_slot = lax.all_gather(slots, 'xy', axis=0, tiled=False)]
    concatenate x1 -> x2, other arithmetic: 0.07 us -> 3.42 us  [with_tags(): return jnp.concatenate([data, tags.astype(data.dtype)], axis=-1)]
    all_to_all x2, waiting for transfers between devices: 23.2 us -> 25.9 us  [the longest x1 25.9 us: shards(): lax.all_to_all(with_tags(far_data, far_slot), 'xy', split_axis=0, concat_...]
    reduce_sum x1 -> x0, other arithmetic: 1.92 us -> none  [block_plan(): slot = jnp.sum(jnp.where(hit, places[None, :] + 1, 0), axis=1) - 1]
    reduce_sum x1 -> x2, other arithmetic: 1.24 us -> 3.16 us  [block_plan(): row = jnp.sum(jnp.where(hit, picks[None, :], 0), axis=1)]
    add x0 -> x2, other arithmetic: none -> 1.79 us  [place_rows(): rows[:, feature].astype(jnp.int32) * RADIX]
    ppermute x1, waiting for transfers between devices: 1.7 us -> 0.01 us  [shards(): other_ints = lax.ppermute(ints, 'zh', swap)]
  transfers between devices with their start and end apart: 5 -> 5, of which waited for: 2 -> 2; matrix products, arithmetic and copies ran while one was open for 20% -> 24% of each run, Pallas kernels for 0% -> 0%
where the time goes in v6:
time: 159 us; the launch traced here: 158 us
  waiting for transfers between devices  62.5 us (39%)
  matrix products  28.6 us (18%)
  starting transfers between devices  20.2 us (13%)
  Pallas kernels  19.6 us (12%)
  between operations  13.6 us (9%)
  other arithmetic  13.5 us (8%)
    ppermute x1, waiting for transfers between devices, shards(): other_rows = lax.ppermute(item_rows, 'zh', swap)  36.6 us
    all_to_all x1, waiting for transfers between devices, shards(): lax.all_to_all(with_tags(far_data, far_slot), 'xy', split_axis=0, concat_...  25.9 us
    pallas_call x1, Pallas kernels, tail(): pl.pallas_call(kern, grid_spec=spec, out_shape=jax.ShapeDtypeStruct((slot...  19.6 us
    dot_general x1, matrix products, shards(): jnp.dot(normed_in, input_weight, preferred_element_type=jnp.float32)  12.5 us
    dot_general x2, matrix products, place_rows(): jnp.dot(one_hot, rows[:, :feature], preferred_element_type=jnp.float32)  9.72 us
    all_to_all x1, starting transfers between devices, shards(): lax.all_to_all(with_tags(own_data, own_slot), 'xy', split_axis=0, concat_...  7.04 us
    all_to_all x1, starting transfers between devices, shards(): lax.all_to_all(with_tags(far_data, far_slot), 'xy', split_axis=0, concat_...  6.98 us
    ppermute x1, starting transfers between devices, shards(): other_ints = lax.ppermute(ints, 'zh', swap)  5.48 us
  transfers between devices with their start and end apart: 5, of which 2 were waited for; matrix products, arithmetic and copies ran while one was open for 24% of the time, Pallas kernels for 0%

profile of v6, /device:TPU:64, one launch (start us, length us, event | category | flops | bytes accessed | tf_op | source)
XLA Modules:
  0.0 158.2 jit_solution(11643680059118171166)
XLA Ops:
  6.5 0.7 pad_add_fusion
  7.3 5.5 %collective-permute-start = (s32[3,1024]{1,0:T(4,128)S(1)}, s32[3,1024]{1,0:T(4,128)S(1)}, u32[]{:S(2)}, u32[]{:S(2)}) collective-permute-start(s32[3,1024]{1,0:T(4,128)S(1)} %pad_add_fusion), channel_id=1, source_target_pairs={{0,128},{128,0},{1,129},{129,1},{2,130},{130,2},{3,131},{131,3},{4... | collective-permute-start | bytes 36872 | tf_op jit(solution)/shard_map/ppermute | solution.py:150
  12.8 0.7 broadcast_add_fusion
  13.4 1.3 fusion.17
  14.7 0.7 fusion.35
  15.4 1.9 %select_reduce_fusion.3 = (s32[1024]{0:T(1024)S(1)}, s32[1024]{0:T(1024)S(1)}) fusion(s32[1024]{0:T(1024)} %bitcast.35, s32[1024]{0:T(1024)S(1)} %fusion.35, s32[1024]{0:T(1024)S(1)} %bitcast.40), kind=kLoop, calls=%fused_computation.8 | loop fusion | flops 5240832 | bytes 20480 | tf_op jit(solution)/shard_map/reduce_sum | solution.py:97
  17.4 2.3 %convolution_convert_fusion.1 = bf16[1024,1024]{1,0:T(8,128)(2,1)S(1)} fusion(s32[1024]{0:T(1024)S(1)} %get-tuple-element.7, pred[1024]{0:T(1024)(128)(4,1)S(1)} %broadcast_compare_fusion.1, bf16[1,1,256,1024]{3,2,1,0:T(8,128)(2,1)} %param.8), kind=kOutput, calls=%fused_computation.27 | convolution fusion | flops 538443776 | bytes 2626560 | tf_op jit(solution)/shard_map/dot_general | solution.py:107
  19.8 0.5 fusion.16
  20.4 1.2 select_reduce_fusion.1
  21.8 0.7 select_convert_fusion
  22.5 1.7 %pad_maximum_fusion = bf16[16,64,1152]{2,1,0:T(8,128)(2,1)} fusion(bf16[16,64,128]{2,1,0:T(8,128)(2,1)S(1)} %get-tuple-element.19, bf16[16,64,1024]{2,1,0:T(8,128)(2,1)S(1)} %bitcast.24), kind=kLoop, calls=%fused_computation.16 | loop fusion | flops 4718592 | bytes 4718592 | tf_op jit(solution)/shard_map/concatenate | solution.py:120
  24.2 7.0 %all-to-all-start = ((bf16[16,64,1152]{2,1,0:T(8,128)(2,1)}), bf16[16,64,1152]{2,1,0:T(8,128)(2,1)S(1)}, u32[]{:S(2)}, u32[]{:S(2)}) async-start(bf16[16,64,1152]{2,1,0:T(8,128)(2,1)} %pad_maximum_fusion), calls=%async_computation | async-start | bytes 4718592 | tf_op jit(solution)/shard_map/all_to_all | solution.py:156
  31.3 0.7 collective-permute-start.1
  32.0 36.6 %collective-permute-done.1 = bf16[256,1024]{1,0:T(8,128)(2,1)} collective-permute-done((bf16[256,1024]{1,0:T(8,128)(2,1)S(1)}, bf16[256,1024]{1,0:T(8,128)(2,1)}, u32[]{:S(2)}, u32[]{:S(2)}) %collective-permute-start.1) | collective-permute-done | bytes 524320 | tf_op jit(solution)/shard_map/ppermute | solution.py:149
  68.6 2.3 %convolution_convert_fusion = bf16[1024,1024]{1,0:T(8,128)(2,1)S(1)} fusion(bf16[256,1024]{1,0:T(8,128)(2,1)} %collective-permute-done.1, s32[1024]{0:T(1024)S(1)} %get-tuple-element.5, pred[1024]{0:T(1024)(128)(4,1)S(1)} %broadcast_compare_fusion), kind=kOutput, calls=%fused_computation.26 | convolution fusion | flops 538443776 | bytes 2626560 | tf_op jit(solution)/shard_map/dot_general | solution.py:107
  70.9 1.7 %pad_maximum_fusion.1 = bf16[16,64,1152]{2,1,0:T(8,128)(2,1)} fusion(bf16[16,64,128]{2,1,0:T(8,128)(2,1)S(1)} %get-tuple-element.18, bf16[16,64,1024]{2,1,0:T(8,128)(2,1)S(1)} %bitcast.25), kind=kLoop, calls=%fused_computation.17 | loop fusion | flops 4718592 | bytes 4718592 | tf_op jit(solution)/shard_map/concatenate | solution.py:120
  72.7 7.0 %all-to-all-start.1 = ((bf16[16,64,1152]{2,1,0:T(8,128)(2,1)}), bf16[16,64,1152]{2,1,0:T(8,128)(2,1)}, u32[]{:S(2)}, u32[]{:S(2)}) async-start(bf16[16,64,1152]{2,1,0:T(8,128)(2,1)} %pad_maximum_fusion.1), calls=%async_computation.1 | async-start | bytes 4718592 | tf_op jit(solution)/shard_map/all_to_all | solution.py:159
  80.0 4.3 %fusion.2 = f32[1024,1024]{1,0:T(8,128)} fusion(bf16[1024,1152]{1,0:T(8,128)(2,1)S(1)} %bitcast.28, s32[1024]{0:T(1024)S(1)} %add_reduce_fusion.1), kind=kOutput, calls=%fused_computation.14 | convolution fusion | flops 2148532224 | bytes 6295552 | tf_op jit(solution)/shard_map/dot_general | solution.py:127
  84.3 25.9 %all-to-all-done.1 = bf16[16,64,1152]{2,1,0:T(8,128)(2,1)} async-done(((bf16[16,64,1152]{2,1,0:T(8,128)(2,1)}), bf16[16,64,1152]{2,1,0:T(8,128)(2,1)}, u32[]{:S(2)}, u32[]{:S(2)}) %all-to-all-start.1) | async-done | bytes 2359328 | tf_op jit(solution)/shard_map/all_to_all | solution.py:159
  110.2 1.5 add_reduce_fusion
  111.7 5.4 %fusion.42 = (f32[1024]{0:T(1024)S(1)}, f32[1024,1024]{1,0:T(8,128)S(1)}) fusion(f32[1024,1024]{1,0:T(8,128)} %fusion.2, bf16[1024,1152]{1,0:T(8,128)(2,1)} %bitcast.16, s32[1024]{0:T(1024)S(1)} %add_reduce_fusion), kind=kOutput, calls=%fused_computation.97 | convolution fusion | flops 2150628352 | bytes 10493952 | tf_op jit(solution)/shard_map/dot_general | solution.py:127
  117.1 2.2 %fusion.41 = (bf16[1024,1024]{1,0:T(8,128)(2,1)}, f32[1024]{0:T(1024)S(1)}) fusion(f32[1024,1024]{1,0:T(8,128)S(1)} %get-tuple-element.21, f32[1024]{0:T(1024)S(1)} %broadcast_multiply_fusion), kind=kLoop, calls=%fused_computation.96 | loop fusion | flops 4193280 | bytes 6299648 | tf_op jit(solution)/shard_map/convert_element_type | solution.py:166
  119.3 12.5 %multiply_convert_fusion.proj_ref = bf16[1024,4096]{1,0:T(8,128)(2,1)} fusion(bf16[1024,4096]{1,0:T(8,128)(2,1)S(1)} %bitcast.45, f32[1024,1024]{1,0:T(8,128)S(1)} %get-tuple-element.21, f32[1024]{0:T(1024)S(1)} %add_rsqrt_fusion, f32[1024]{0:T(1024)S(1)} %broadcast_multiply_fusion), kind=kOutput, calls=%fused_computation | convolution fusion | flops 8614051840 | bytes 20979712 | tf_op jit(solution)/shard_map/dot_general | solution.py:171
  131.8 19.6 %shard_map.82 = bf16[1024,1024]{1,0:T(8,128)(2,1)} custom-call(s32[8]{0:T(128)} %bitcast.43, bf16[1024,4096]{1,0:T(8,128)(2,1)} %multiply_convert_fusion.proj_ref, bf16[8,128,2048]{2,1,0:T(8,128)(2,1)} %bitcast.26, bf16[1024,1024]{1,0:T(8,128)(2,1)} %get-tuple-element.9.rows_ref, bf16[1024,1024]{1,0:T(8,128)(2,1)} %wout_ref.1), custom_call_target="tpu_custom_call" | custom-call | flops 2684354560 | bytes 18874368 | tf_op jit(solution)/shard_map/pallas_call | solution.py:77
  (26 shorter events, 0.6 us)
Async XLA Ops:
  7.3 12.5 %collective-permute-start = (s32[3,1024]{1,0:T(4,128)S(1)}, s32[3,1024]{1,0:T(4,128)S(1)}, u32[]{:S(2)}, u32[]{:S(2)}) collective-permute-start(s32[3,1024]{1,0:T(4,128)S(1)} %pad_add_fusion), channel_id=1, source_target_pairs={{0,128},{128,0},{1,129},{129,1},{2,130},{130,2},{3,131},{131,3},{4... | collective-permute-start | bytes 36872 | tf_op jit(solution)/shard_map/ppermute | solution.py:150
  22.5 8.8 %copy-start = (bf16[1,1,256,1024]{3,2,1,0:T(8,128)(2,1)S(1)}, bf16[1,1,256,1024]{3,2,1,0:T(8,128)(2,1)}, u32[]{:S(2)}) copy-start(bf16[1,1,256,1024]{3,2,1,0:T(8,128)(2,1)} %param.8) | copy-start | bytes 1572868
  24.2 48.5 %all-to-all-start = ((bf16[16,64,1152]{2,1,0:T(8,128)(2,1)}), bf16[16,64,1152]{2,1,0:T(8,128)(2,1)S(1)}, u32[]{:S(2)}, u32[]{:S(2)}) async-start(bf16[16,64,1152]{2,1,0:T(8,128)(2,1)} %pad_maximum_fusion), calls=%async_computation | async-start | bytes 4718592 | tf_op jit(solution)/shard_map/all_to_all | solution.py:156
  31.2 100.5 %all-gather.2.cloned.1.call-start = ((), (), s32[]{:S(2)}) async-start(), calls=%async_computation.2 | async-start | bytes 4718592 | tf_op jit(solution)/shard_map/all_gather | solution.py:173
  31.3 37.3 %collective-permute-start.1 = (bf16[256,1024]{1,0:T(8,128)(2,1)S(1)}, bf16[256,1024]{1,0:T(8,128)(2,1)}, u32[]{:S(2)}, u32[]{:S(2)}) collective-permute-start(bf16[256,1024]{1,0:T(8,128)(2,1)S(1)} %bitcast.29), channel_id=1, source_target_pairs={{0,128},{128,0},{1,129},{129,1},{2,130},{130,2},{3,131},{131,3},{4... | collective-permute-start | bytes 1572872 | tf_op jit(solution)/shard_map/ppermute | solution.py:149
  72.7 37.5 %all-to-all-start.1 = ((bf16[16,64,1152]{2,1,0:T(8,128)(2,1)}), bf16[16,64,1152]{2,1,0:T(8,128)(2,1)}, u32[]{:S(2)}, u32[]{:S(2)}) async-start(bf16[16,64,1152]{2,1,0:T(8,128)(2,1)} %pad_maximum_fusion.1), calls=%async_computation.1 | async-start | bytes 4718592 | tf_op jit(solution)/shard_map/all_to_all | solution.py:159
  110.2 9.1 %slice-start = ((s8[8388608]{0:T(1024)(128)(4,1)}), s8[4194304]{0:T(1024)(128)(4,1)S(1)}, s32[]{:S(2)}) async-start(s8[8388608]{0:T(1024)(128)(4,1)} %bitcast.44), calls=%async_computation.3 | async-start | bytes 8388608
  111.7 7.6 %slice-start.1 = ((s8[8388608]{0:T(1024)(128)(4,1)}), s8[4194304]{0:T(1024)(128)(4,1)S(1)}, s32[]{:S(2)}) async-start(s8[8388608]{0:T(1024)(128)(4,1)} %bitcast.44), calls=%async_computation.4 | async-start | bytes 8388608
Sparse Core Ops, SparseCore 0:
  33.8 61.6 all-gather.1

commit v7 on v5

--- a/solution.py
+++ b/solution.py
@@ -140,16 +140,18 @@
     far_row, far_slot = block_plan(other_ints, half, n_half, per_pair, sources)
     own_data = select_rows(item_rows, own_row, own_slot)
     far_data = select_rows(other_rows, far_row, far_slot)
-    slots = jnp.concatenate([own_slot, far_slot], axis=1)
-    capacity = 2 * per_pair
-    every_slot = lax.all_gather(slots, "xy", axis=0, tiled=False)
-    tags = lax.dynamic_index_in_dim(every_slot, lax.axis_index("xy"), axis=1, keepdims=False)
-    tags = tags.reshape(-1)
+    sent_slot = block_plan(ints, 1 - half, n_half, per_pair, sources)[1]
+    plans = jnp.stack([own_slot, sent_slot])
+    every_plan = lax.all_gather(plans, ("zh", "xy"), axis=0, tiled=False)
+    every_plan = every_plan.reshape((HALVES, n_half) + plans.shape)
+    here = lax.axis_index("xy")
+    own_tags = lax.dynamic_index_in_dim(every_plan[half, :, 0], here, axis=1, keepdims=False)
+    far_tags = lax.dynamic_index_in_dim(every_plan[1 - half, :, 1], here, axis=1, keepdims=False)
+    tags = jnp.stack([own_tags, far_tags], axis=1)
+    tags, own_data = lax.optimization_barrier((tags, own_data))
     own_arrived = lax.all_to_all(own_data, "xy", split_axis=0, concat_axis=0, tiled=True)
-    tags, far_data = lax.optimization_barrier((tags, far_data))
     far_arrived = lax.all_to_all(far_data, "xy", split_axis=0, concat_axis=0, tiled=True)
     slot_ids = jnp.arange(slot_count, dtype=jnp.int32)
-    tags = tags.reshape(n_half, 2, per_pair)
     as_float = place_rows(own_arrived, tags[:, 0], slot_ids) + place_rows(
         far_arrived, tags[:, 1], slot_ids
     )

time: 149 us -> 238 us (1.60)
  blocking collectives: 34.2 us -> 119 us
  waiting for transfers between devices: 24.9 us -> 28.8 us
    all_gather x1, blocking collectives: 34.2 us -> 119 us  [shards(): every_plan = lax.all_gather(plans, ('zh', 'xy'), axis=0, tiled=False)]
    ppermute x1, waiting for transfers between devices: 0.01 us -> 12.1 us  [shards(): other_rows = lax.ppermute(item_rows, 'zh', swap)]
    all_to_all x1, waiting for transfers between devices: 23.2 us -> 15.1 us  [shards(): lax.all_to_all(far_data, 'xy', split_axis=0, concat_axis=0, tiled=True)]
    ppermute x1, starting transfers between devices: 5.48 us -> 0.58 us  [shards(): other_ints = lax.ppermute(ints, 'zh', swap)]
    ppermute x1, starting transfers between devices: 0.54 us -> 5.44 us  [shards(): other_rows = lax.ppermute(item_rows, 'zh', swap)]
    all_to_all x1, starting transfers between devices: 7.03 us -> 3.72 us  [shards(): lax.all_to_all(own_data, 'xy', split_axis=0, concat_axis=0, tiled=True)]
  transfers between devices with their start and end apart: 5 -> 5, of which waited for: 2 -> 3; matrix products, arithmetic and copies ran while one was open for 20% -> 12% of each run, Pallas kernels for 0% -> 0%
where the time goes in v7:
time: 238 us; the launch traced here: 236 us
  blocking collectives  119 us (50%)
  matrix products  29.6 us (12%)
  waiting for transfers between devices  28.8 us (12%)
  Pallas kernels  20 us (8%)
  starting transfers between devices  17.1 us (7%)
  between operations  13.5 us (6%)
  other arithmetic  7.5 us (3%)
    all_gather x1, blocking collectives, shards(): every_plan = lax.all_gather(plans, ('zh', 'xy'), axis=0, tiled=False)  119 us
    pallas_call x1, Pallas kernels, tail(): pl.pallas_call(kern, grid_spec=spec, out_shape=jax.ShapeDtypeStruct((slot...  20 us
    all_to_all x1, waiting for transfers between devices, shards(): lax.all_to_all(far_data, 'xy', split_axis=0, concat_axis=0, tiled=True)  15.1 us
    dot_general x1, matrix products, shards(): jnp.dot(normed_in, input_weight, preferred_element_type=jnp.float32)  12.5 us
    ppermute x1, waiting for transfers between devices, shards(): other_rows = lax.ppermute(item_rows, 'zh', swap)  12.1 us
    dot_general x2, matrix products, place_rows(): return jnp.dot(one_hot, rows, preferred_element_type=jnp.float32)  9.72 us
    all_to_all x1, starting transfers between devices, shards(): lax.all_to_all(far_data, 'xy', split_axis=0, concat_axis=0, tiled=True)  7.33 us
    dot_general x2, matrix products, select_rows(): jnp.dot(one_hot, table, preferred_element_type=jnp.float32)  5.53 us
  transfers between devices with their start and end apart: 5, of which 3 were waited for; matrix products, arithmetic and copies ran while one was open for 12% of the time, Pallas kernels for 0%

profile of v7, /device:TPU:64, one launch (start us, length us, event | category | flops | bytes accessed | tf_op | source)
XLA Modules:
  0.0 236.4 jit_solution(12410831582874352368)
XLA Ops:
  6.5 1.4 fusion.13
  7.9 0.7 compare_select_fusion.4
  8.6 0.7 broadcast_add_fusion
  9.3 2.6 %select_reduce_fusion.2 = (s32[1024]{0:T(1024)S(1)}, s32[1024]{0:T(1024)S(1)}, s32[1024]{0:T(1024)S(1)}) fusion(s32[1024]{0:T(1024)} %bitcast.48, s32[1024]{0:T(1024)S(1)} %get-tuple-element.24, s32[1024]{0:T(1024)S(1)} %bitcast.50, s32[1024]{0:T(1024)S(1)} %get-tuple-element.23), kind=kLoop, calls=%fused_computation.7 | loop fusion | flops 8385536 | bytes 28672 | tf_op jit(solution)/shard_map/reduce_sum | solution.py:97
  11.9 0.1 sub.39
  12.0 0.1 sub.42
  12.1 119.4 %all-gather = s32[64,16,64]{2,1,0:T(8,128)S(1)} all-gather(s32[2,16,64]{2,1,0:T(8,128)S(1)} %pad_add_fusion), channel_id=2, replica_groups=mesh['zh'=2,'xy'=16,'cand'=8] {'zh','xy'}, dimensions={0}, use_global_device_ids=true | all-gather | bytes 270336 | tf_op jit(solution)/shard_map/all_gather | solution.py:145
  131.5 3.3 %convolution_convert_fusion.1 = bf16[1024,1024]{1,0:T(8,128)(2,1)} fusion(s32[1024]{0:T(1024)S(1)} %get-tuple-element.11, pred[1024]{0:T(1024)(128)(4,1)S(1)} %broadcast_compare_fusion, bf16[1,1,256,1024]{3,2,1,0:T(8,128)(2,1)} %param.8), kind=kOutput, calls=%fused_computation.25 | convolution fusion | flops 538443776 | bytes 2626560 | tf_op jit(solution)/shard_map/dot_general | solution.py:107
  134.8 3.7 %all-to-all-start = ((bf16[16,64,1024]{2,1,0:T(8,128)(2,1)}), bf16[16,64,1024]{2,1,0:T(8,128)(2,1)S(1)}, u32[]{:S(2)}, u32[]{:S(2)}) async-start(bf16[16,64,1024]{2,1,0:T(8,128)(2,1)} %bitcast.8), calls=%async_computation | async-start | bytes 4194304 | tf_op jit(solution)/shard_map/all_to_all | solution.py:152
  138.7 0.6 collective-permute-start
  139.2 5.4 %collective-permute-start.1 = (bf16[256,1024]{1,0:T(8,128)(2,1)S(1)}, bf16[256,1024]{1,0:T(8,128)(2,1)S(1)}, u32[]{:S(2)}, u32[]{:S(2)}) collective-permute-start(bf16[256,1024]{1,0:T(8,128)(2,1)S(1)} %bitcast.36), channel_id=1, source_target_pairs={{0,128},{128,0},{1,129},{129,1},{2,130},{130,2},{3,131},{131,3},{4... | collective-permute-start | bytes 1572872 | tf_op jit(solution)/shard_map/ppermute | solution.py:136
  144.7 1.7 collective-permute-done
  146.4 0.5 fusion.12
  147.0 1.2 select_reduce_fusion
  148.3 12.1 %collective-permute-done.1 = bf16[256,1024]{1,0:T(8,128)(2,1)S(1)} collective-permute-done((bf16[256,1024]{1,0:T(8,128)(2,1)S(1)}, bf16[256,1024]{1,0:T(8,128)(2,1)S(1)}, u32[]{:S(2)}, u32[]{:S(2)}) %collective-permute-start.1) | collective-permute-done | bytes 524320 | tf_op jit(solution)/shard_map/ppermute | solution.py:136
  160.3 2.2 convolution_convert_fusion
  162.6 7.3 %all-to-all-start.1 = ((bf16[16,64,1024]{2,1,0:T(8,128)(2,1)}), bf16[16,64,1024]{2,1,0:T(8,128)(2,1)}, u32[]{:S(2)}, u32[]{:S(2)}) async-start(bf16[16,64,1024]{2,1,0:T(8,128)(2,1)} %bitcast.18), calls=%async_computation.1 | async-start | bytes 4194304 | tf_op jit(solution)/shard_map/all_to_all | solution.py:153
  169.9 0.1 eq.185
  170.1 4.3 %fusion.2 = f32[1024,1024]{1,0:T(8,128)} fusion(bf16[1024,1024]{1,0:T(8,128)(2,1)S(1)} %bitcast.34, s32[1024]{0:T(1024)S(1)} %eq.185), kind=kOutput, calls=%fused_computation.16 | convolution fusion | flops 2148532224 | bytes 6295552 | tf_op jit(solution)/shard_map/dot_general | solution.py:114
  174.3 15.1 %all-to-all-done.1 = bf16[16,64,1024]{2,1,0:T(8,128)(2,1)} async-done(((bf16[16,64,1024]{2,1,0:T(8,128)(2,1)}), bf16[16,64,1024]{2,1,0:T(8,128)(2,1)}, u32[]{:S(2)}, u32[]{:S(2)}) %all-to-all-start.1) | async-done | bytes 2097184 | tf_op jit(solution)/shard_map/all_to_all | solution.py:153
  189.4 5.4 %fusion.34 = (f32[1024]{0:T(1024)S(1)}, f32[1024,1024]{1,0:T(8,128)S(1)}) fusion(f32[1024,1024]{1,0:T(8,128)} %fusion.2, bf16[1024,1024]{1,0:T(8,128)(2,1)} %bitcast.19, s32[1024]{0:T(1024)S(1)} %eq.189), kind=kOutput, calls=%fused_computation.79 | convolution fusion | flops 2150628352 | bytes 10493952 | tf_op jit(solution)/shard_map/dot_general | solution.py:114
  194.9 2.2 fusion.31
  197.1 12.5 %multiply_convert_fusion.proj_ref = bf16[1024,4096]{1,0:T(8,128)(2,1)} fusion(bf16[1024,4096]{1,0:T(8,128)(2,1)S(1)} %bitcast.54, f32[1024,1024]{1,0:T(8,128)S(1)} %get-tuple-element.26, f32[1024]{0:T(1024)S(1)} %add_rsqrt_fusion, f32[1024]{0:T(1024)S(1)} %broadcast_multiply_fusion), kind=kOutput, calls=%fused_computation | convolution fusion | flops 8614051840 | bytes 20979712 | tf_op jit(solution)/shard_map/dot_general | solution.py:163
  209.6 20.0 %shard_map.82 = bf16[1024,1024]{1,0:T(8,128)(2,1)} custom-call(s32[8]{0:T(128)} %bitcast.52, bf16[1024,4096]{1,0:T(8,128)(2,1)} %multiply_convert_fusion.proj_ref, bf16[8,128,2048]{2,1,0:T(8,128)(2,1)} %bitcast.33, bf16[1024,1024]{1,0:T(8,128)(2,1)} %get-tuple-element.14.rows_ref, bf16[1024,1024]{1,0:T(8,128)(2,1)} %wout_ref.1), custom_call_target="tpu_custom_call" | custom-call | flops 2684354560 | bytes 18874368 | tf_op jit(solution)/shard_map/pallas_call | solution.py:77
  (31 shorter events, 0.3 us)
Async XLA Ops:
  6.5 132.1 %copy-start.1 = (s32[1,1,1024]{2,1,0:T(1,128)S(1)}, s32[1,1,1024]{2,1,0:T(1,128)}, u32[]{:S(2)}) copy-start(s32[1,1,1024]{2,1,0:T(1,128)} %param.10) | copy-start | bytes 12292
  6.5 132.1 %copy-start.2 = (s32[1,1,1024]{2,1,0:T(1,128)S(1)}, s32[1,1,1024]{2,1,0:T(1,128)}, u32[]{:S(2)}) copy-start(s32[1,1,1024]{2,1,0:T(1,128)} %param.11) | copy-start | bytes 12292
  6.5 132.1 %copy-start.3 = (s32[1,1,1024]{2,1,0:T(1,128)S(1)}, s32[1,1,1024]{2,1,0:T(1,128)}, u32[]{:S(2)}) copy-start(s32[1,1,1024]{2,1,0:T(1,128)} %param.9) | copy-start | bytes 12292
  6.5 132.7 %copy-start = (bf16[1,1,256,1024]{3,2,1,0:T(8,128)(2,1)S(1)}, bf16[1,1,256,1024]{3,2,1,0:T(8,128)(2,1)}, u32[]{:S(2)}) copy-start(bf16[1,1,256,1024]{3,2,1,0:T(8,128)(2,1)} %param.8) | copy-start | bytes 1572868
  134.8 27.7 %all-to-all-start = ((bf16[16,64,1024]{2,1,0:T(8,128)(2,1)}), bf16[16,64,1024]{2,1,0:T(8,128)(2,1)S(1)}, u32[]{:S(2)}, u32[]{:S(2)}) async-start(bf16[16,64,1024]{2,1,0:T(8,128)(2,1)} %bitcast.8), calls=%async_computation | async-start | bytes 4194304 | tf_op jit(solution)/shard_map/all_to_all | solution.py:152
  138.6 71.0 %all-gather.3.cloned.1.call-start = ((), (), s32[]{:S(2)}) async-start(), calls=%async_computation.2 | async-start | bytes 4718592 | tf_op jit(solution)/shard_map/all_gather | solution.py:165
  138.7 7.7 %collective-permute-start = (s32[3,1024]{1,0:T(4,128)S(1)}, s32[3,1024]{1,0:T(4,128)S(1)}, u32[]{:S(2)}, u32[]{:S(2)}) collective-permute-start(s32[3,1024]{1,0:T(4,128)S(1)} %pad_add_fusion.2), channel_id=1, source_target_pairs={{0,128},{128,0},{1,129},{129,1},{2,130},{130,2},{3,131},{131,3},{4... | collective-permute-start | bytes 36872 | tf_op jit(solution)/shard_map/ppermute | solution.py:137
  139.2 21.1 %collective-permute-start.1 = (bf16[256,1024]{1,0:T(8,128)(2,1)S(1)}, bf16[256,1024]{1,0:T(8,128)(2,1)S(1)}, u32[]{:S(2)}, u32[]{:S(2)}) collective-permute-start(bf16[256,1024]{1,0:T(8,128)(2,1)S(1)} %bitcast.36), channel_id=1, source_target_pairs={{0,128},{128,0},{1,129},{129,1},{2,130},{130,2},{3,131},{131,3},{4... | collective-permute-start | bytes 1572872 | tf_op jit(solution)/shard_map/ppermute | solution.py:136
  162.6 26.8 %all-to-all-start.1 = ((bf16[16,64,1024]{2,1,0:T(8,128)(2,1)}), bf16[16,64,1024]{2,1,0:T(8,128)(2,1)}, u32[]{:S(2)}, u32[]{:S(2)}) async-start(bf16[16,64,1024]{2,1,0:T(8,128)(2,1)} %bitcast.18), calls=%async_computation.1 | async-start | bytes 4194304 | tf_op jit(solution)/shard_map/all_to_all | solution.py:153
  189.4 7.6 %slice-start = ((s8[8388608]{0:T(1024)(128)(4,1)}), s8[4194304]{0:T(1024)(128)(4,1)S(1)}, s32[]{:S(2)}) async-start(s8[8388608]{0:T(1024)(128)(4,1)} %bitcast.53), calls=%async_computation.3 | async-start | bytes 8388608
  189.4 7.7 %slice-start.1 = ((s8[8388608]{0:T(1024)(128)(4,1)}), s8[4194304]{0:T(1024)(128)(4,1)S(1)}, s32[]{:S(2)}) async-start(s8[8388608]{0:T(1024)(128)(4,1)} %bitcast.53), calls=%async_computation.4 | async-start | bytes 8388608
Sparse Core Ops, SparseCore 0:
  144.8 53.2 all-gather.2

commit v8 on v5

--- a/solution.py
+++ b/solution.py
@@ -142,8 +142,7 @@
     far_data = select_rows(other_rows, far_row, far_slot)
     slots = jnp.concatenate([own_slot, far_slot], axis=1)
     capacity = 2 * per_pair
-    every_slot = lax.all_gather(slots, "xy", axis=0, tiled=False)
-    tags = lax.dynamic_index_in_dim(every_slot, lax.axis_index("xy"), axis=1, keepdims=False)
+    tags = lax.all_to_all(slots, "xy", split_axis=0, concat_axis=0, tiled=True)
     tags = tags.reshape(-1)
     own_arrived = lax.all_to_all(own_data, "xy", split_axis=0, concat_axis=0, tiled=True)
     tags, far_data = lax.optimization_barrier((tags, far_data))

time: 149 us -> 152 us (1.020)
  blocking collectives: 34.2 us -> 0 us
  waiting for transfers between devices: 24.9 us -> 53.1 us
  starting transfers between devices: 18.7 us -> 26.3 us
    all_gather x1 -> x0, blocking collectives: 34.2 us -> none  [shards(): every_slot = lax.all_gather(slots, 'xy', axis=0, tiled=False)]
    ppermute x1, waiting for transfers between devices: 0.01 us -> 30.8 us  [shards(): other_rows = lax.ppermute(item_rows, 'zh', swap)]
    all_to_all x0 -> x1, starting transfers between devices: none -> 7.04 us  [shards(): tags = lax.all_to_all(slots, 'xy', split_axis=0, concat_axis=0, tiled=True)]
    all_to_all x1, waiting for transfers between devices: 23.2 us -> 18 us  [shards(): lax.all_to_all(far_data, 'xy', split_axis=0, concat_axis=0, tiled=True)]
    all_to_all x0 -> x1, waiting for transfers between devices: none -> 4.29 us  [shards(): tags = lax.all_to_all(slots, 'xy', split_axis=0, concat_axis=0, tiled=True)]
    all_to_all x1, starting transfers between devices: 7.03 us -> 3.72 us  [shards(): lax.all_to_all(own_data, 'xy', split_axis=0, concat_axis=0, tiled=True)]
    ppermute x1, starting transfers between devices: 0.54 us -> 2.94 us  [shards(): other_rows = lax.ppermute(item_rows, 'zh', swap)]
    ppermute x1, waiting for transfers between devices: 1.7 us -> 0.01 us  [shards(): other_ints = lax.ppermute(ints, 'zh', swap)]
  transfers between devices with their start and end apart: 5 -> 6, of which waited for: 2 -> 3; matrix products, arithmetic and copies ran while one was open for 20% -> 23% of each run, Pallas kernels for 0% -> 0%
where the time goes in v8:
time: 152 us; the launch traced here: 151 us
  waiting for transfers between devices  53.1 us (35%)
  matrix products  29.5 us (19%)
  starting transfers between devices  26.3 us (17%)
  Pallas kernels  20 us (13%)
  between operations  13.5 us (9%)
  other arithmetic  8.29 us (5%)
    ppermute x1, waiting for transfers between devices, shards(): other_rows = lax.ppermute(item_rows, 'zh', swap)  30.8 us
    pallas_call x1, Pallas kernels, tail(): pl.pallas_call(kern, grid_spec=spec, out_shape=jax.ShapeDtypeStruct((slot...  20 us
    all_to_all x1, waiting for transfers between devices, shards(): lax.all_to_all(far_data, 'xy', split_axis=0, concat_axis=0, tiled=True)  18 us
    dot_general x1, matrix products, shards(): jnp.dot(normed_in, input_weight, preferred_element_type=jnp.float32)  12.5 us
    dot_general x2, matrix products, place_rows(): return jnp.dot(one_hot, rows, preferred_element_type=jnp.float32)  9.67 us
    all_to_all x1, starting transfers between devices, shards(): tags = lax.all_to_all(slots, 'xy', split_axis=0, concat_axis=0, tiled=True)  7.04 us
    all_to_all x1, starting transfers between devices, shards(): lax.all_to_all(far_data, 'xy', split_axis=0, concat_axis=0, tiled=True)  7.04 us
    dot_general x2, matrix products, select_rows(): jnp.dot(one_hot, table, preferred_element_type=jnp.float32)  5.54 us
  transfers between devices with their start and end apart: 6, of which 3 were waited for; matrix products, arithmetic and copies ran while one was open for 23% of the time, Pallas kernels for 0%

profile of v8, /device:TPU:64, one launch (start us, length us, event | category | flops | bytes accessed | tf_op | source)
XLA Modules:
  0.0 151.2 jit_solution(9435045767647781428)
XLA Ops:
  6.5 0.7 pad_add_fusion
  7.3 5.5 %collective-permute-start = (s32[3,1024]{1,0:T(4,128)S(1)}, s32[3,1024]{1,0:T(4,128)S(1)}, u32[]{:S(2)}, u32[]{:S(2)}) collective-permute-start(s32[3,1024]{1,0:T(4,128)S(1)} %pad_add_fusion), channel_id=1, source_target_pairs={{0,128},{128,0},{1,129},{129,1},{2,130},{130,2},{3,131},{131,3},{4... | collective-permute-start | bytes 36872 | tf_op jit(solution)/shard_map/ppermute | solution.py:137
  12.8 0.7 broadcast_add_fusion
  13.4 1.3 fusion.13
  14.7 0.7 fusion.27
  15.5 2.0 %select_reduce_fusion.3 = (s32[1024]{0:T(1024)S(1)}, s32[1024]{0:T(1024)S(1)}) fusion(s32[1024]{0:T(1024)S(1)} %bitcast.42, s32[1024]{0:T(1024)S(1)} %fusion.27, s32[1024]{0:T(1024)} %bitcast.37), kind=kLoop, calls=%fused_computation.8 | loop fusion | flops 5240832 | bytes 20480 | tf_op jit(solution)/shard_map/reduce_sum | solution.py:98
  17.5 0.5 fusion.12
  18.1 1.2 select_reduce_fusion.1
  19.5 0.7 pad_add_fusion.1
  20.1 7.0 %all-to-all-start = ((s32[16,1,128]{2,1,0:T(1,128)}), s32[16,1,128]{2,1,0:T(1,128)S(1)}, u32[]{:S(2)}, u32[]{:S(2)}) async-start(s32[16,1,128]{2,1,0:T(1,128)} %bitcast.10), calls=%async_computation | async-start | bytes 16384 | tf_op jit(solution)/shard_map/all_to_all | solution.py:145
  27.2 3.3 %convolution_convert_fusion = bf16[1024,1024]{1,0:T(8,128)(2,1)} fusion(s32[1024]{0:T(1024)S(1)} %get-tuple-element.14, pred[1024]{0:T(1024)(128)(4,1)S(1)} %broadcast_compare_fusion, bf16[1,1,256,1024]{3,2,1,0:T(8,128)(2,1)} %param.8), kind=kOutput, calls=%fused_computation.22 | convolution fusion | flops 538443776 | bytes 2626560 | tf_op jit(solution)/shard_map/dot_general | solution.py:107
  30.5 4.3 %all-to-all-done = s32[16,1,128]{2,1,0:T(1,128)S(1)} async-done(((s32[16,1,128]{2,1,0:T(1,128)}), s32[16,1,128]{2,1,0:T(1,128)S(1)}, u32[]{:S(2)}, u32[]{:S(2)}) %all-to-all-start) | async-done | bytes 8224 | tf_op jit(solution)/shard_map/all_to_all | solution.py:145
  34.8 3.7 %all-to-all-start.1 = ((bf16[16,64,1024]{2,1,0:T(8,128)(2,1)}), bf16[16,64,1024]{2,1,0:T(8,128)(2,1)S(1)}, u32[]{:S(2)}, u32[]{:S(2)}) async-start(bf16[16,64,1024]{2,1,0:T(8,128)(2,1)} %bitcast.16), calls=%async_computation.1 | async-start | bytes 4194304 | tf_op jit(solution)/shard_map/all_to_all | solution.py:147
  38.6 2.9 %collective-permute-start.1 = (bf16[256,1024]{1,0:T(8,128)(2,1)S(1)}, bf16[256,1024]{1,0:T(8,128)(2,1)S(1)}, u32[]{:S(2)}, u32[]{:S(2)}) collective-permute-start(bf16[256,1024]{1,0:T(8,128)(2,1)S(1)} %bitcast.30), channel_id=1, source_target_pairs={{0,128},{128,0},{1,129},{129,1},{2,130},{130,2},{3,131},{131,3},{4... | collective-permute-start | bytes 1572872 | tf_op jit(solution)/shard_map/ppermute | solution.py:136
  41.6 30.8 %collective-permute-done.1 = bf16[256,1024]{1,0:T(8,128)(2,1)S(1)} collective-permute-done((bf16[256,1024]{1,0:T(8,128)(2,1)S(1)}, bf16[256,1024]{1,0:T(8,128)(2,1)S(1)}, u32[]{:S(2)}, u32[]{:S(2)}) %collective-permute-start.1) | collective-permute-done | bytes 524320 | tf_op jit(solution)/shard_map/ppermute | solution.py:136
  72.4 2.2 %convolution_convert_fusion.1 = bf16[1024,1024]{1,0:T(8,128)(2,1)} fusion(bf16[256,1024]{1,0:T(8,128)(2,1)S(1)} %collective-permute-done.1, s32[1024]{0:T(1024)S(1)} %get-tuple-element.11, pred[1024]{0:T(1024)(128)(4,1)S(1)} %broadcast_compare_fusion.1), kind=kOutput, calls=%fused_computation.23 | convolution fusion | flops 538443776 | bytes 2626560 | tf_op jit(solution)/shard_map/dot_general | solution.py:107
  74.6 7.0 %all-to-all-start.2 = ((bf16[16,64,1024]{2,1,0:T(8,128)(2,1)}), bf16[16,64,1024]{2,1,0:T(8,128)(2,1)}, u32[]{:S(2)}, u32[]{:S(2)}) async-start(bf16[16,64,1024]{2,1,0:T(8,128)(2,1)} %bitcast.14), calls=%async_computation.2 | async-start | bytes 4194304 | tf_op jit(solution)/shard_map/all_to_all | solution.py:149
  81.7 0.1 reshape.130
  81.9 4.3 %fusion.2 = f32[1024,1024]{1,0:T(8,128)} fusion(bf16[1024,1024]{1,0:T(8,128)(2,1)S(1)} %bitcast.29, s32[1024]{0:T(1024)S(1)} %eq.159), kind=kOutput, calls=%fused_computation.14 | convolution fusion | flops 2148532224 | bytes 6295552 | tf_op jit(solution)/shard_map/dot_general | solution.py:114
  86.2 18.0 %all-to-all-done.2 = bf16[16,64,1024]{2,1,0:T(8,128)(2,1)} async-done(((bf16[16,64,1024]{2,1,0:T(8,128)(2,1)}), bf16[16,64,1024]{2,1,0:T(8,128)(2,1)}, u32[]{:S(2)}, u32[]{:S(2)}) %all-to-all-start.2) | async-done | bytes 2097184 | tf_op jit(solution)/shard_map/all_to_all | solution.py:149
  104.2 5.4 %fusion.34 = (f32[1024]{0:T(1024)S(1)}, f32[1024,1024]{1,0:T(8,128)S(1)}) fusion(f32[1024,1024]{1,0:T(8,128)} %fusion.2, bf16[1024,1024]{1,0:T(8,128)(2,1)} %bitcast.18, s32[1024]{0:T(1024)S(1)} %eq.166), kind=kOutput, calls=%fused_computation.74 | convolution fusion | flops 2150628352 | bytes 10493952 | tf_op jit(solution)/shard_map/dot_general | solution.py:114
  109.6 2.2 %fusion.33 = (bf16[1024,1024]{1,0:T(8,128)(2,1)}, f32[1024]{0:T(1024)S(1)}) fusion(f32[1024,1024]{1,0:T(8,128)S(1)} %get-tuple-element.21, f32[1024]{0:T(1024)S(1)} %broadcast_multiply_fusion), kind=kLoop, calls=%fused_computation.73 | loop fusion | flops 4193280 | bytes 6299648 | tf_op jit(solution)/shard_map/convert_element_type | solution.py:155
  111.8 12.5 %multiply_convert_fusion.proj_ref = bf16[1024,4096]{1,0:T(8,128)(2,1)} fusion(bf16[1024,4096]{1,0:T(8,128)(2,1)S(1)} %bitcast.47, f32[1024,1024]{1,0:T(8,128)S(1)} %get-tuple-element.21, f32[1024]{0:T(1024)S(1)} %add_rsqrt_fusion, f32[1024]{0:T(1024)S(1)} %broadcast_multiply_fusion), kind=kOutput, calls=%fused_computation | convolution fusion | flops 8614051840 | bytes 20979712 | tf_op jit(solution)/shard_map/dot_general | solution.py:160
  124.3 20.0 %shard_map.82 = bf16[1024,1024]{1,0:T(8,128)(2,1)} custom-call(s32[8]{0:T(128)} %bitcast.45, bf16[1024,4096]{1,0:T(8,128)(2,1)} %multiply_convert_fusion.proj_ref, bf16[8,128,2048]{2,1,0:T(8,128)(2,1)} %bitcast.28, bf16[1024,1024]{1,0:T(8,128)(2,1)} %get-tuple-element.15.rows_ref, bf16[1024,1024]{1,0:T(8,128)(2,1)} %wout_ref.1), custom_call_target="tpu_custom_call" | custom-call | flops 2684354560 | bytes 18874368 | tf_op jit(solution)/shard_map/pallas_call | solution.py:77
  (26 shorter events, 0.5 us)
Async XLA Ops:
  7.3 10.3 %collective-permute-start = (s32[3,1024]{1,0:T(4,128)S(1)}, s32[3,1024]{1,0:T(4,128)S(1)}, u32[]{:S(2)}, u32[]{:S(2)}) collective-permute-start(s32[3,1024]{1,0:T(4,128)S(1)} %pad_add_fusion), channel_id=1, source_target_pairs={{0,128},{128,0},{1,129},{129,1},{2,130},{130,2},{3,131},{131,3},{4... | collective-permute-start | bytes 36872 | tf_op jit(solution)/shard_map/ppermute | solution.py:137
  15.4 23.1 %copy-start = (bf16[1,1,256,1024]{3,2,1,0:T(8,128)(2,1)S(1)}, bf16[1,1,256,1024]{3,2,1,0:T(8,128)(2,1)}, u32[]{:S(2)}) copy-start(bf16[1,1,256,1024]{3,2,1,0:T(8,128)(2,1)} %param.8) | copy-start | bytes 1572868
  20.1 14.6 %all-to-all-start = ((s32[16,1,128]{2,1,0:T(1,128)}), s32[16,1,128]{2,1,0:T(1,128)S(1)}, u32[]{:S(2)}, u32[]{:S(2)}) async-start(s32[16,1,128]{2,1,0:T(1,128)} %bitcast.10), calls=%async_computation | async-start | bytes 16384 | tf_op jit(solution)/shard_map/all_to_all | solution.py:145
  34.8 39.8 %all-to-all-start.1 = ((bf16[16,64,1024]{2,1,0:T(8,128)(2,1)}), bf16[16,64,1024]{2,1,0:T(8,128)(2,1)S(1)}, u32[]{:S(2)}, u32[]{:S(2)}) async-start(bf16[16,64,1024]{2,1,0:T(8,128)(2,1)} %bitcast.16), calls=%async_computation.1 | async-start | bytes 4194304 | tf_op jit(solution)/shard_map/all_to_all | solution.py:147
  38.5 85.8 %all-gather.2.cloned.1.call-start = ((), (), s32[]{:S(2)}) async-start(), calls=%async_computation.3 | async-start | bytes 4718592 | tf_op jit(solution)/shard_map/all_gather | solution.py:162
  38.6 33.8 %collective-permute-start.1 = (bf16[256,1024]{1,0:T(8,128)(2,1)S(1)}, bf16[256,1024]{1,0:T(8,128)(2,1)S(1)}, u32[]{:S(2)}, u32[]{:S(2)}) collective-permute-start(bf16[256,1024]{1,0:T(8,128)(2,1)S(1)} %bitcast.30), channel_id=1, source_target_pairs={{0,128},{128,0},{1,129},{129,1},{2,130},{130,2},{3,131},{131,3},{4... | collective-permute-start | bytes 1572872 | tf_op jit(solution)/shard_map/ppermute | solution.py:136
  74.6 29.6 %all-to-all-start.2 = ((bf16[16,64,1024]{2,1,0:T(8,128)(2,1)}), bf16[16,64,1024]{2,1,0:T(8,128)(2,1)}, u32[]{:S(2)}, u32[]{:S(2)}) async-start(bf16[16,64,1024]{2,1,0:T(8,128)(2,1)} %bitcast.14), calls=%async_computation.2 | async-start | bytes 4194304 | tf_op jit(solution)/shard_map/all_to_all | solution.py:149
  104.2 7.6 %slice-start = ((s8[8388608]{0:T(1024)(128)(4,1)}), s8[4194304]{0:T(1024)(128)(4,1)S(1)}, s32[]{:S(2)}) async-start(s8[8388608]{0:T(1024)(128)(4,1)} %bitcast.46), calls=%async_computation.4 | async-start | bytes 8388608
  104.2 7.6 %slice-start.1 = ((s8[8388608]{0:T(1024)(128)(4,1)}), s8[4194304]{0:T(1024)(128)(4,1)S(1)}, s32[]{:S(2)}) async-start(s8[8388608]{0:T(1024)(128)(4,1)} %bitcast.46), calls=%async_computation.5 | async-start | bytes 8388608
Sparse Core Ops, SparseCore 0:
  41.7 61.5 all-gather.1

commit v9 on v8

--- a/solution.py
+++ b/solution.py
@@ -12,6 +12,8 @@
 
 HEADS = 8
 HALVES = 2
+RADIX = 32
+CODE_ROWS = 16
 
 
 epsilon = 1e-06
@@ -133,8 +135,16 @@
     feature = item_rows.shape[1]
     per_pair = 2 * slot_count // sources
     swap = [(0, 1), (1, 0)]
-    other_rows = lax.ppermute(item_rows, "zh", swap)
-    other_ints = lax.ppermute(ints, "zh", swap)
+    table_span = item_rows.shape[0]
+    coded = jnp.stack(
+        [ints[0], ints[1], jnp.floor_divide(ints[2], RADIX), ints[2] % RADIX]
+    ).astype(jnp.bfloat16)
+    spare = jnp.zeros((CODE_ROWS - coded.shape[0], feature), jnp.bfloat16)
+    bundle = jnp.concatenate([item_rows, coded, spare], axis=0)
+    received = lax.ppermute(bundle, "zh", swap)
+    other_rows = received[:table_span]
+    codes = received[table_span : table_span + 4].astype(jnp.int32)
+    other_ints = jnp.stack([codes[0], codes[1], codes[2] * RADIX + codes[3]])
 
     own_row, own_slot = block_plan(ints, half, n_half, per_pair, sources)
     far_row, far_slot = block_plan(other_ints, half, n_half, per_pair, sources)
@@ -142,9 +152,9 @@
     far_data = select_rows(other_rows, far_row, far_slot)
     slots = jnp.concatenate([own_slot, far_slot], axis=1)
     capacity = 2 * per_pair
+    own_arrived = lax.all_to_all(own_data, "xy", split_axis=0, concat_axis=0, tiled=True)
+    slots, own_arrived = lax.optimization_barrier((slots, own_arrived))
     tags = lax.all_to_all(slots, "xy", split_axis=0, concat_axis=0, tiled=True)
-    tags = tags.reshape(-1)
-    own_arrived = lax.all_to_all(own_data, "xy", split_axis=0, concat_axis=0, tiled=True)
     tags, far_data = lax.optimization_barrier((tags, far_data))
     far_arrived = lax.all_to_all(far_data, "xy", split_axis=0, concat_axis=0, tiled=True)
     slot_ids = jnp.arange(slot_count, dtype=jnp.int32)

time: 152 us -> 152 us (level)
  starting transfers between devices: 26.3 us -> 21 us
  local copies, waits for them, and re-layouts: 0.43 us -> 2.55 us
    ppermute x2 -> x1, waiting for transfers between devices: 30.8 us -> 9.19 us  [shards(): received = lax.ppermute(bundle, 'zh', swap)]
    all_to_all x1, waiting for transfers between devices: 0.01 us -> 17.2 us  [shards(): lax.all_to_all(own_data, 'xy', split_axis=0, concat_axis=0, tiled=True)]
    all_to_all x1, waiting for transfers between devices: 18 us -> 22 us  [shards(): lax.all_to_all(far_data, 'xy', split_axis=0, concat_axis=0, tiled=True)]
    all_to_all x1, starting transfers between devices: 3.72 us -> 7.03 us  [shards(): lax.all_to_all(own_data, 'xy', split_axis=0, concat_axis=0, tiled=True)]
    all_to_all x1, starting transfers between devices: 7.04 us -> 3.83 us  [shards(): tags = lax.all_to_all(slots, 'xy', split_axis=0, concat_axis=0, tiled=True)]
    ppermute x2 -> x1, starting transfers between devices: 8.42 us -> 5.48 us  [shards(): received = lax.ppermute(bundle, 'zh', swap)]
    all_to_all x1, starting transfers between devices: 7.04 us -> 4.62 us  [shards(): lax.all_to_all(far_data, 'xy', split_axis=0, concat_axis=0, tiled=True)]
    concatenate x0 -> x1, local copies, waits for them, and re-layouts: none -> 2.12 us  [shards(): bundle = jnp.concatenate([item_rows, coded, spare], axis=0)]
  transfers between devices with their start and end apart: 6 -> 5, of which waited for: 3 -> 4; matrix products, arithmetic and copies ran while one was open for 23% -> 25% of each run, Pallas kernels for 0% -> 0%
where the time goes in v9:
time: 152 us; the launch traced here: 151 us
  waiting for transfers between devices  54.5 us (36%)
  matrix products  29.5 us (19%)
  starting transfers between devices  21 us (14%)
  Pallas kernels  20 us (13%)
  between operations  13.5 us (9%)
  other arithmetic  9.64 us (6%)
  local copies, waits for them, and re-layouts  2.55 us (2%)
    all_to_all x1, waiting for transfers between devices, shards(): lax.all_to_all(far_data, 'xy', split_axis=0, concat_axis=0, tiled=True)  22 us
    pallas_call x1, Pallas kernels, tail(): pl.pallas_call(kern, grid_spec=spec, out_shape=jax.ShapeDtypeStruct((slot...  20 us
    all_to_all x1, waiting for transfers between devices, shards(): lax.all_to_all(own_data, 'xy', split_axis=0, concat_axis=0, tiled=True)  17.2 us
    dot_general x1, matrix products, shards(): jnp.dot(normed_in, input_weight, preferred_element_type=jnp.float32)  12.5 us
    dot_general x2, matrix products, place_rows(): return jnp.dot(one_hot, rows, preferred_element_type=jnp.float32)  9.64 us
    ppermute x1, waiting for transfers between devices, shards(): received = lax.ppermute(bundle, 'zh', swap)  9.19 us
    all_to_all x1, starting transfers between devices, shards(): lax.all_to_all(own_data, 'xy', split_axis=0, concat_axis=0, tiled=True)  7.03 us
    dot_general x2, matrix products, select_rows(): jnp.dot(one_hot, table, preferred_element_type=jnp.float32)  5.55 us
  transfers between devices with their start and end apart: 5, of which 4 were waited for; matrix products, arithmetic and copies ran while one was open for 25% of the time, Pallas kernels for 0%

profile of v9, /device:TPU:64, one launch (start us, length us, event | category | flops | bytes accessed | tf_op | source)
XLA Modules:
  0.0 150.7 jit_solution(18328921120308573625)
XLA Ops:
  6.5 0.7 fusion.29
  7.2 0.7 fusion.35
  8.0 0.7 convert_bitcast_fusion
  8.7 2.1 %concatenate.7 = bf16[272,1024]{1,0:T(8,128)(2,1)S(1)} concatenate(bf16[256,1024]{1,0:T(8,128)(2,1)} %bitcast.43, bf16[1,1024]{1,0:T(2,128)(2,1)S(1)} %get-tuple-element.29, bf16[1,1024]{1,0:T(2,128)(2,1)S(1)} %get-tuple-element.28, bf16[1,1024]{1,0:T(2,128)(2,1)S(1)} %fusion.35, bf16[1,1024]{1,0:T(2,128)(2,1)S(1)} %get-tuple-element.19, bf16[12,1024]{1,0:T(8,128)(2,1)S(1)} %broadcast_in_dim.71), dimensions={0} | concatenate | bytes 1114112 | tf_op jit(solution)/shard_map/concatenate | solution.py:143
  10.8 5.5 %collective-permute-start = (bf16[272,1024]{1,0:T(8,128)(2,1)S(1)}, bf16[272,1024]{1,0:T(8,128)(2,1)S(1)}, u32[]{:S(2)}, u32[]{:S(2)}) collective-permute-start(bf16[272,1024]{1,0:T(8,128)(2,1)S(1)} %concatenate.7), channel_id=1, source_target_pairs={{0,128},{128,0},{1,129},{129,1},{2,130},{130,2},{3,131},{131,3},{4... | collective-permute-start | bytes 1671176 | tf_op jit(solution)/shard_map/ppermute | solution.py:144
  16.3 0.7 broadcast_add_fusion
  17.0 1.3 fusion.13
  18.3 0.7 fusion.28
  19.0 1.9 %select_reduce_fusion.1 = (s32[1024]{0:T(1024)S(1)}, s32[1024]{0:T(1024)S(1)}) fusion(s32[1024]{0:T(1024)} %bitcast.50, s32[1024]{0:T(1024)S(1)} %fusion.28, s32[1024]{0:T(1024)S(1)} %bitcast.47), kind=kLoop, calls=%fused_computation.5 | loop fusion | flops 5240832 | bytes 20480 | tf_op jit(solution)/shard_map/reduce_sum | solution.py:99
  20.9 3.3 %convolution_convert_fusion.1 = bf16[1024,1024]{1,0:T(8,128)(2,1)} fusion(s32[1024]{0:T(1024)S(1)} %get-tuple-element.17, pred[1024]{0:T(1024)(128)(4,1)S(1)} %broadcast_compare_fusion.1, bf16[1,1,256,1024]{3,2,1,0:T(8,128)(2,1)} %param.8), kind=kOutput, calls=%fused_computation.23 | convolution fusion | flops 538443776 | bytes 2626560 | tf_op jit(solution)/shard_map/dot_general | solution.py:109
  24.2 7.0 %all-to-all-start = ((bf16[16,64,1024]{2,1,0:T(8,128)(2,1)}), bf16[16,64,1024]{2,1,0:T(8,128)(2,1)S(1)}, u32[]{:S(2)}, u32[]{:S(2)}) async-start(bf16[16,64,1024]{2,1,0:T(8,128)(2,1)} %bitcast.12), calls=%async_computation | async-start | bytes 4194304 | tf_op jit(solution)/shard_map/all_to_all | solution.py:155
  32.1 9.2 %collective-permute-done = bf16[272,1024]{1,0:T(8,128)(2,1)S(1)} collective-permute-done((bf16[272,1024]{1,0:T(8,128)(2,1)S(1)}, bf16[272,1024]{1,0:T(8,128)(2,1)S(1)}, u32[]{:S(2)}, u32[]{:S(2)}) %collective-permute-start) | collective-permute-done | bytes 557088 | tf_op jit(solution)/shard_map/ppermute | solution.py:144
  41.9 1.2 select_reduce_fusion
  43.9 17.2 %all-to-all-done = bf16[16,64,1024]{2,1,0:T(8,128)(2,1)S(1)} async-done(((bf16[16,64,1024]{2,1,0:T(8,128)(2,1)}), bf16[16,64,1024]{2,1,0:T(8,128)(2,1)S(1)}, u32[]{:S(2)}, u32[]{:S(2)}) %all-to-all-start) | async-done | bytes 2097184 | tf_op jit(solution)/shard_map/all_to_all | solution.py:155
  61.1 3.8 %all-to-all-start.1 = ((s32[16,1,128]{2,1,0:T(1,128)}), s32[16,1,128]{2,1,0:T(1,128)S(1)}, u32[]{:S(2)}, u32[]{:S(2)}) async-start(s32[16,1,128]{2,1,0:T(1,128)} %bitcast.13), calls=%async_computation.1 | async-start | bytes 16384 | tf_op jit(solution)/shard_map/all_to_all | solution.py:157
  65.0 2.3 %convolution_convert_fusion = bf16[1024,1024]{1,0:T(8,128)(2,1)} fusion(bf16[272,1024]{1,0:T(8,128)(2,1)S(1)} %collective-permute-done, s32[1024]{0:T(1024)S(1)} %get-tuple-element.15, pred[1024]{0:T(1024)(128)(4,1)S(1)} %broadcast_compare_fusion), kind=kOutput, calls=%fused_computation.22 | convolution fusion | flops 538443776 | bytes 2626560 | tf_op jit(solution)/shard_map/dot_general | solution.py:109
  67.2 5.3 %all-to-all-done.1 = s32[16,1,128]{2,1,0:T(1,128)S(1)} async-done(((s32[16,1,128]{2,1,0:T(1,128)}), s32[16,1,128]{2,1,0:T(1,128)S(1)}, u32[]{:S(2)}, u32[]{:S(2)}) %all-to-all-start.1) | async-done | bytes 8224 | tf_op jit(solution)/shard_map/all_to_all | solution.py:157
  72.6 4.6 %all-to-all-start.2 = ((bf16[16,64,1024]{2,1,0:T(8,128)(2,1)}), bf16[16,64,1024]{2,1,0:T(8,128)(2,1)}, u32[]{:S(2)}, u32[]{:S(2)}) async-start(bf16[16,64,1024]{2,1,0:T(8,128)(2,1)} %bitcast.16), calls=%async_computation.2 | async-start | bytes 4194304 | tf_op jit(solution)/shard_map/all_to_all | solution.py:159
  77.5 4.3 %fusion.2 = f32[1024,1024]{1,0:T(8,128)} fusion(bf16[1024,1024]{1,0:T(8,128)(2,1)S(1)} %bitcast.44, s32[1024]{0:T(1024)S(1)} %eq.163), kind=kOutput, calls=%fused_computation.14 | convolution fusion | flops 2148532224 | bytes 6295552 | tf_op jit(solution)/shard_map/dot_general | solution.py:116
  81.7 22.0 %all-to-all-done.2 = bf16[16,64,1024]{2,1,0:T(8,128)(2,1)} async-done(((bf16[16,64,1024]{2,1,0:T(8,128)(2,1)}), bf16[16,64,1024]{2,1,0:T(8,128)(2,1)}, u32[]{:S(2)}, u32[]{:S(2)}) %all-to-all-start.2) | async-done | bytes 2097184 | tf_op jit(solution)/shard_map/all_to_all | solution.py:159
  103.7 5.4 %fusion.38 = (f32[1024]{0:T(1024)S(1)}, f32[1024,1024]{1,0:T(8,128)S(1)}) fusion(f32[1024,1024]{1,0:T(8,128)} %fusion.2, bf16[1024,1024]{1,0:T(8,128)(2,1)} %bitcast.18, s32[1024]{0:T(1024)S(1)} %eq.167), kind=kOutput, calls=%fused_computation.87 | convolution fusion | flops 2150628352 | bytes 10493952 | tf_op jit(solution)/shard_map/dot_general | solution.py:116
  109.1 2.2 %fusion.37 = (bf16[1024,1024]{1,0:T(8,128)(2,1)}, f32[1024]{0:T(1024)S(1)}) fusion(f32[1024,1024]{1,0:T(8,128)S(1)} %get-tuple-element.27, f32[1024]{0:T(1024)S(1)} %broadcast_multiply_fusion), kind=kLoop, calls=%fused_computation.86 | loop fusion | flops 4193280 | bytes 6299648 | tf_op jit(solution)/shard_map/convert_element_type | solution.py:165
  111.3 12.5 %multiply_convert_fusion.proj_ref = bf16[1024,4096]{1,0:T(8,128)(2,1)} fusion(bf16[1024,4096]{1,0:T(8,128)(2,1)S(1)} %bitcast.58, f32[1024,1024]{1,0:T(8,128)S(1)} %get-tuple-element.27, f32[1024]{0:T(1024)S(1)} %add_rsqrt_fusion, f32[1024]{0:T(1024)S(1)} %broadcast_multiply_fusion), kind=kOutput, calls=%fused_computation | convolution fusion | flops 8614051840 | bytes 20979712 | tf_op jit(solution)/shard_map/dot_general | solution.py:170
  123.8 20.0 %shard_map.82 = bf16[1024,1024]{1,0:T(8,128)(2,1)} custom-call(s32[8]{0:T(128)} %bitcast.56, bf16[1024,4096]{1,0:T(8,128)(2,1)} %multiply_convert_fusion.proj_ref, bf16[8,128,2048]{2,1,0:T(8,128)(2,1)} %bitcast.42, bf16[1024,1024]{1,0:T(8,128)(2,1)} %get-tuple-element.21.rows_ref, bf16[1024,1024]{1,0:T(8,128)(2,1)} %wout_ref.1), custom_call_target="tpu_custom_call" | custom-call | flops 2684354560 | bytes 18874368 | tf_op jit(solution)/shard_map/pallas_call | solution.py:79
  (27 shorter events, 2.5 us)
Async XLA Ops:
  10.8 30.5 %collective-permute-start = (bf16[272,1024]{1,0:T(8,128)(2,1)S(1)}, bf16[272,1024]{1,0:T(8,128)(2,1)S(1)}, u32[]{:S(2)}, u32[]{:S(2)}) collective-permute-start(bf16[272,1024]{1,0:T(8,128)(2,1)S(1)} %concatenate.7), channel_id=1, source_target_pairs={{0,128},{128,0},{1,129},{129,1},{2,130},{130,2},{3,131},{131,3},{4... | collective-permute-start | bytes 1671176 | tf_op jit(solution)/shard_map/ppermute | solution.py:144
  24.2 36.9 %all-to-all-start = ((bf16[16,64,1024]{2,1,0:T(8,128)(2,1)}), bf16[16,64,1024]{2,1,0:T(8,128)(2,1)S(1)}, u32[]{:S(2)}, u32[]{:S(2)}) async-start(bf16[16,64,1024]{2,1,0:T(8,128)(2,1)} %bitcast.12), calls=%async_computation | async-start | bytes 4194304 | tf_op jit(solution)/shard_map/all_to_all | solution.py:155
  31.3 92.6 %all-gather.2.cloned.1.call-start = ((), (), s32[]{:S(2)}) async-start(), calls=%async_computation.3 | async-start | bytes 4718592 | tf_op jit(solution)/shard_map/all_gather | solution.py:172
  61.1 11.4 %all-to-all-start.1 = ((s32[16,1,128]{2,1,0:T(1,128)}), s32[16,1,128]{2,1,0:T(1,128)S(1)}, u32[]{:S(2)}, u32[]{:S(2)}) async-start(s32[16,1,128]{2,1,0:T(1,128)} %bitcast.13), calls=%async_computation.1 | async-start | bytes 16384 | tf_op jit(solution)/shard_map/all_to_all | solution.py:157
  72.6 31.2 %all-to-all-start.2 = ((bf16[16,64,1024]{2,1,0:T(8,128)(2,1)}), bf16[16,64,1024]{2,1,0:T(8,128)(2,1)}, u32[]{:S(2)}, u32[]{:S(2)}) async-start(bf16[16,64,1024]{2,1,0:T(8,128)(2,1)} %bitcast.16), calls=%async_computation.2 | async-start | bytes 4194304 | tf_op jit(solution)/shard_map/all_to_all | solution.py:159
  103.7 7.6 %slice-start = ((s8[8388608]{0:T(1024)(128)(4,1)}), s8[4194304]{0:T(1024)(128)(4,1)S(1)}, s32[]{:S(2)}) async-start(s8[8388608]{0:T(1024)(128)(4,1)} %bitcast.57), calls=%async_computation.4 | async-start | bytes 8388608
  103.7 7.6 %slice-start.1 = ((s8[8388608]{0:T(1024)(128)(4,1)}), s8[4194304]{0:T(1024)(128)(4,1)S(1)}, s32[]{:S(2)}) async-start(s8[8388608]{0:T(1024)(128)(4,1)} %bitcast.57), calls=%async_computation.5 | async-start | bytes 8388608
Sparse Core Ops, SparseCore 0:
  33.9 50.7 all-gather.1

commit v10 on v9

--- a/solution.py
+++ b/solution.py
@@ -110,6 +110,20 @@
     return picked.reshape(rows.shape + (table.shape[1],))
 
 
+TAG_LANES = 128
+
+
+def with_tags(data, *slot_lists):
+    lane = lax.broadcasted_iota(jnp.int32, data.shape[:-1] + (TAG_LANES,), 2)
+    tags = jnp.zeros(lane.shape, jnp.int32)
+    for n, slots in enumerate(slot_lists):
+        high = jnp.floor_divide(slots, RADIX)
+        low = slots - high * RADIX
+        tags = jnp.where(lane == 2 * n, high[..., None], tags)
+        tags = jnp.where(lane == 2 * n + 1, low[..., None], tags)
+    return jnp.concatenate([data, tags.astype(data.dtype)], axis=-1)
+
+
 def place_rows(arrived, tags, slot_ids):
     rows = arrived.reshape(-1, arrived.shape[-1])
     one_hot = (slot_ids[:, None] == tags.reshape(-1)[None, :]).astype(rows.dtype)
@@ -150,17 +164,18 @@
     far_row, far_slot = block_plan(other_ints, half, n_half, per_pair, sources)
     own_data = select_rows(item_rows, own_row, own_slot)
     far_data = select_rows(other_rows, far_row, far_slot)
-    slots = jnp.concatenate([own_slot, far_slot], axis=1)
-    capacity = 2 * per_pair
     own_arrived = lax.all_to_all(own_data, "xy", split_axis=0, concat_axis=0, tiled=True)
-    slots, own_arrived = lax.optimization_barrier((slots, own_arrived))
-    tags = lax.all_to_all(slots, "xy", split_axis=0, concat_axis=0, tiled=True)
-    tags, far_data = lax.optimization_barrier((tags, far_data))
-    far_arrived = lax.all_to_all(far_data, "xy", split_axis=0, concat_axis=0, tiled=True)
+    payload, own_arrived = lax.optimization_barrier(
+        (with_tags(far_data, far_slot, own_slot), own_arrived)
+    )
+    far_arrived = lax.all_to_all(payload, "xy", split_axis=0, concat_axis=0, tiled=True)
+    far_rows = far_arrived[..., :feature]
+    codes = far_arrived[..., feature : feature + 4].astype(jnp.int32)
+    far_tags = codes[..., 0] * RADIX + codes[..., 1]
+    own_tags = codes[..., 2] * RADIX + codes[..., 3]
     slot_ids = jnp.arange(slot_count, dtype=jnp.int32)
-    tags = tags.reshape(n_half, 2, per_pair)
-    as_float = place_rows(own_arrived, tags[:, 0], slot_ids) + place_rows(
-        far_arrived, tags[:, 1], slot_ids
+    as_float = place_rows(own_arrived, own_tags, slot_ids) + place_rows(
+        far_rows, far_tags, slot_ids
     )
     arranged = as_float.astype(jnp.bfloat16)
 

time: 152 us -> 150 us (0.987)
  the two profiles are of different devices: /device:TPU:64 before, /device:TPU:2 now
where the time goes in v10:
time: 150 us
  waiting for transfers between devices  53.3 us (36%)
  matrix products  23.4 us (16%)
  starting transfers between devices  21.8 us (15%)
  Pallas kernels  20 us (13%)
  between operations  13.6 us (9%)
  other arithmetic  12.5 us (8%)
  local copies, waits for them, and re-layouts  5.35 us (4%)
    all_to_all x1, waiting for transfers between devices, shards(): lax.all_to_all(payload, 'xy', split_axis=0, concat_axis=0, tiled=True)  27.3 us
    all_to_all x1, waiting for transfers between devices, shards(): lax.all_to_all(own_data, 'xy', split_axis=0, concat_axis=0, tiled=True)  21.1 us
    pallas_call x1, Pallas kernels, tail(): pl.pallas_call(kern, grid_spec=spec, out_shape=jax.ShapeDtypeStruct((slot...  20 us
    dot_general x1, matrix products, shards(): jnp.dot(normed_in, input_weight, preferred_element_type=jnp.float32)  12.2 us
    all_to_all x1, starting transfers between devices, shards(): lax.all_to_all(own_data, 'xy', split_axis=0, concat_axis=0, tiled=True)  7.48 us
    ppermute x1, starting transfers between devices, shards(): received = lax.ppermute(bundle, 'zh', swap)  7.28 us
    all_to_all x1, starting transfers between devices, shards(): lax.all_to_all(payload, 'xy', split_axis=0, concat_axis=0, tiled=True)  6.84 us
    dot_general x2, matrix products, place_rows(): return jnp.dot(one_hot, rows, preferred_element_type=jnp.float32)  4.79 us
  transfers between devices with their start and end apart: 4, of which 3 were waited for; matrix products, arithmetic and copies ran while one was open for 23% of the time, Pallas kernels for 0%

profile of v10, /device:TPU:2, one launch (start us, length us, event | category | flops | bytes accessed | tf_op | source)
XLA Modules:
  0.0 150.0 jit_solution(693691311874400836)
XLA Ops:
  7.2 0.7 fusion.41
  8.0 0.7 convert_bitcast_fusion
  8.7 2.1 %concatenate.7 = bf16[272,1024]{1,0:T(8,128)(2,1)S(1)} concatenate(bf16[256,1024]{1,0:T(8,128)(2,1)} %bitcast.42, bf16[1,1024]{1,0:T(2,128)(2,1)S(1)} %get-tuple-element.29, bf16[1,1024]{1,0:T(2,128)(2,1)S(1)} %get-tuple-element.28, bf16[1,1024]{1,0:T(2,128)(2,1)S(1)} %fusion.41, bf16[1,1024]{1,0:T(2,128)(2,1)S(1)} %get-tuple-element.15, bf16[12,1024]{1,0:T(8,128)(2,1)S(1)} %broadcast_in_dim.95), dimensions={0} | concatenate | bytes 1114112 | tf_op jit(solution)/shard_map/concatenate | solution.py:157
  10.8 7.3 %collective-permute-start = (bf16[272,1024]{1,0:T(8,128)(2,1)S(1)}, bf16[272,1024]{1,0:T(8,128)(2,1)S(1)}, u32[]{:S(2)}, u32[]{:S(2)}) collective-permute-start(bf16[272,1024]{1,0:T(8,128)(2,1)S(1)} %concatenate.7), channel_id=1, source_target_pairs={{0,128},{128,0},{1,129},{129,1},{2,130},{130,2},{3,131},{131,3},{4... | collective-permute-start | bytes 1671176 | tf_op jit(solution)/shard_map/ppermute | solution.py:158
  18.8 1.3 fusion.12
  20.8 1.9 %select_reduce_fusion = (s32[1024]{0:T(1024)S(1)}, s32[1024]{0:T(1024)S(1)}) fusion(s32[1024]{0:T(1024)} %bitcast.49, s32[1024]{0:T(1024)S(1)} %fusion.34, s32[1024]{0:T(1024)S(1)} %bitcast.46), kind=kLoop, calls=%fused_computation.4 | loop fusion | flops 5240832 | bytes 20480 | tf_op jit(solution)/shard_map/reduce_sum | solution.py:99
  22.7 3.3 %convolution_convert_fusion = bf16[1024,1024]{1,0:T(8,128)(2,1)} fusion(s32[1024]{0:T(1024)S(1)} %get-tuple-element.11, pred[1024]{0:T(1024)(128)(4,1)S(1)} %broadcast_compare_fusion, bf16[1,1,256,1024]{3,2,1,0:T(8,128)(2,1)} %param.8), kind=kOutput, calls=%fused_computation.23 | convolution fusion | flops 538443776 | bytes 2626560 | tf_op jit(solution)/shard_map/dot_general | solution.py:109
  26.0 7.5 %all-to-all-start = ((bf16[16,64,1024]{2,1,0:T(8,128)(2,1)}), bf16[16,64,1024]{2,1,0:T(8,128)(2,1)S(1)}, u32[]{:S(2)}, u32[]{:S(2)}) async-start(bf16[16,64,1024]{2,1,0:T(8,128)(2,1)} %bitcast.14), calls=%async_computation | async-start | bytes 4194304 | tf_op jit(solution)/shard_map/all_to_all | solution.py:167
  34.2 1.2 select_reduce_fusion.3
  35.6 0.7 select_convert_fusion
  36.3 1.3 convolution_convert_fusion.1
  37.6 1.7 %pad_maximum_fusion = bf16[16,64,1152]{2,1,0:T(8,128)(2,1)} fusion(bf16[16,64,128]{2,1,0:T(8,128)(2,1)S(1)} %select_convert_fusion, bf16[16,64,1024]{2,1,0:T(8,128)(2,1)S(1)} %bitcast.40), kind=kLoop, calls=%fused_computation.16 | loop fusion | flops 4718592 | bytes 4718592 | tf_op jit(solution)/shard_map/concatenate | solution.py:124
  39.3 21.1 %all-to-all-done = bf16[16,64,1024]{2,1,0:T(8,128)(2,1)S(1)} async-done(((bf16[16,64,1024]{2,1,0:T(8,128)(2,1)}), bf16[16,64,1024]{2,1,0:T(8,128)(2,1)S(1)}, u32[]{:S(2)}, u32[]{:S(2)}) %all-to-all-start) | async-done | bytes 2097184 | tf_op jit(solution)/shard_map/all_to_all | solution.py:167
  60.4 1.3 copy-done
  61.7 6.8 %all-to-all-start.1 = ((bf16[16,64,1152]{2,1,0:T(8,128)(2,1)}), bf16[16,64,1152]{2,1,0:T(8,128)(2,1)S(1)}, u32[]{:S(2)}, u32[]{:S(2)}) async-start(bf16[16,64,1152]{2,1,0:T(8,128)(2,1)} %pad_maximum_fusion), calls=%async_computation.1 | async-start | bytes 4718592 | tf_op jit(solution)/shard_map/all_to_all | solution.py:171
  69.3 27.3 %all-to-all-done.1 = bf16[16,64,1152]{2,1,0:T(8,128)(2,1)S(1)} async-done(((bf16[16,64,1152]{2,1,0:T(8,128)(2,1)}), bf16[16,64,1152]{2,1,0:T(8,128)(2,1)S(1)}, u32[]{:S(2)}, u32[]{:S(2)}) %all-to-all-start.1) | async-done | bytes 2359328 | tf_op jit(solution)/shard_map/all_to_all | solution.py:171
  96.6 1.1 fusion.18
  98.1 1.3 copy-done.1
  99.4 2.3 %fusion.2 = f32[1024,1024]{1,0:T(8,128)S(1)} fusion(bf16[1024,1024]{1,0:T(8,128)(2,1)S(1)} %bitcast.43, s32[1024]{0:T(1024)S(1)} %add.164), kind=kOutput, calls=%fused_computation.14 | convolution fusion | flops 2148532224 | bytes 6295552 | tf_op jit(solution)/shard_map/dot_general | solution.py:130
  101.8 2.4 %fusion.44 = (f32[1024]{0:T(1024)S(1)}, f32[1024,1024]{1,0:T(8,128)S(1)}) fusion(f32[1024,1024]{1,0:T(8,128)S(1)} %fusion.2, bf16[1024,1024]{1,0:T(8,128)(2,1)S(1)} %bitcast.44, s32[1024]{0:T(1024)S(1)} %add.166), kind=kOutput, calls=%fused_computation.113 | convolution fusion | flops 2150628352 | bytes 10493952 | tf_op jit(solution)/shard_map/dot_general | solution.py:130
  104.3 2.2 %fusion.43 = (bf16[1024,1024]{1,0:T(8,128)(2,1)}, f32[1024]{0:T(1024)S(1)}) fusion(f32[1024,1024]{1,0:T(8,128)S(1)} %get-tuple-element.27, f32[1024]{0:T(1024)S(1)} %broadcast_multiply_fusion), kind=kLoop, calls=%fused_computation.112 | loop fusion | flops 4193280 | bytes 6299648 | tf_op jit(solution)/shard_map/convert_element_type | solution.py:180
  106.5 12.2 %multiply_convert_fusion.proj_ref = bf16[1024,4096]{1,0:T(8,128)(2,1)} fusion(bf16[1024,4096]{1,0:T(8,128)(2,1)S(1)} %bitcast.57, f32[1024,1024]{1,0:T(8,128)S(1)} %get-tuple-element.27, f32[1024]{0:T(1024)S(1)} %add_rsqrt_fusion, f32[1024]{0:T(1024)S(1)} %broadcast_multiply_fusion), kind=kOutput, calls=%fused_computation | convolution fusion | flops 8614051840 | bytes 20979712 | tf_op jit(solution)/shard_map/dot_general | solution.py:185
  118.7 4.4 %all-gather.2.cloned.1.call-done = bf16[1,8,128,2048]{3,2,0,1:T(8,128)(2,1)} async-done(((bf16[1,1,128,2048]{3,2,0,1:T(8,128)(2,1)}), bf16[1,8,128,2048]{3,2,0,1:T(8,128)(2,1)}) %all-gather.2.cloned.1.call-update) | async-done | bytes 4194320 | tf_op jit(solution)/shard_map/all_gather | solution.py:187
  123.1 20.0 %shard_map.82 = bf16[1024,1024]{1,0:T(8,128)(2,1)} custom-call(s32[8]{0:T(128)} %bitcast.55, bf16[1024,4096]{1,0:T(8,128)(2,1)} %multiply_convert_fusion.proj_ref, bf16[8,128,2048]{2,1,0:T(8,128)(2,1)} %bitcast.41, bf16[1024,1024]{1,0:T(8,128)(2,1)} %get-tuple-element.17.rows_ref, bf16[1024,1024]{1,0:T(8,128)(2,1)} %wout_ref.1), custom_call_target="tpu_custom_call" | custom-call | flops 2684354560 | bytes 18874368 | tf_op jit(solution)/shard_map/pallas_call | solution.py:79
  (35 shorter events, 4.1 us)
Async XLA Ops:
  10.8 22.8 %collective-permute-start = (bf16[272,1024]{1,0:T(8,128)(2,1)S(1)}, bf16[272,1024]{1,0:T(8,128)(2,1)S(1)}, u32[]{:S(2)}, u32[]{:S(2)}) collective-permute-start(bf16[272,1024]{1,0:T(8,128)(2,1)S(1)} %concatenate.7), channel_id=1, source_target_pairs={{0,128},{128,0},{1,129},{129,1},{2,130},{130,2},{3,131},{131,3},{4... | collective-permute-start | bytes 1671176 | tf_op jit(solution)/shard_map/ppermute | solution.py:158
  26.0 34.4 %all-to-all-start = ((bf16[16,64,1024]{2,1,0:T(8,128)(2,1)}), bf16[16,64,1024]{2,1,0:T(8,128)(2,1)S(1)}, u32[]{:S(2)}, u32[]{:S(2)}) async-start(bf16[16,64,1024]{2,1,0:T(8,128)(2,1)} %bitcast.14), calls=%async_computation | async-start | bytes 4194304 | tf_op jit(solution)/shard_map/all_to_all | solution.py:167
  60.4 1.3 copy-start
  61.7 34.9 %all-to-all-start.1 = ((bf16[16,64,1152]{2,1,0:T(8,128)(2,1)}), bf16[16,64,1152]{2,1,0:T(8,128)(2,1)S(1)}, u32[]{:S(2)}, u32[]{:S(2)}) async-start(bf16[16,64,1152]{2,1,0:T(8,128)(2,1)} %pad_maximum_fusion), calls=%async_computation.1 | async-start | bytes 4718592 | tf_op jit(solution)/shard_map/all_to_all | solution.py:171
  68.5 54.6 %all-gather.2.cloned.1.call-start = ((), (), s32[]{:S(2)}) async-start(), calls=%async_computation.2 | async-start | bytes 4718592 | tf_op jit(solution)/shard_map/all_gather | solution.py:187
  97.8 1.6 %copy-start.1 = (bf16[16,64,1024]{2,1,0:T(8,128)(2,1)S(1)}, bf16[16,64,1024]{2,1,0:T(8,128)(2,1)}, u32[]{:S(2)}) copy-start(bf16[16,64,1024]{2,1,0:T(8,128)(2,1)} %copy-done) | copy-start | bytes 6291460
  101.8 4.7 %slice-start = ((s8[8388608]{0:T(1024)(128)(4,1)}), s8[4194304]{0:T(1024)(128)(4,1)S(1)}, s32[]{:S(2)}) async-start(s8[8388608]{0:T(1024)(128)(4,1)} %bitcast.56), calls=%async_computation.3 | async-start | bytes 8388608
  101.8 4.7 %slice-start.1 = ((s8[8388608]{0:T(1024)(128)(4,1)}), s8[4194304]{0:T(1024)(128)(4,1)S(1)}, s32[]{:S(2)}) async-start(s8[8388608]{0:T(1024)(128)(4,1)} %bitcast.56), calls=%async_computation.4 | async-start | bytes 8388608
Sparse Core Ops, SparseCore 0:
  71.1 51.9 all-gather.1
